TPU v7x, 128 devices: a whole 4x4x4 slice. The times are simulated.
128 devices in a mesh: ctx: 64 (over x, y_lo, z, core), tp: 2 (over y_hi).
Axes of the slice: x: 4, y: 4 (y_hi: 2, y_lo: 2; y = y_hi * 2 + y_lo), z: 4, core: 2. Of those that a mesh axis runs over, the one named last changes fastest.
Arguments:
- rotated_queries: bfloat16 [8192, 2048], P('ctx', 'tp'), may hold values from -150 to 150
- rotated_keys: bfloat16 [8192, 1024], P('ctx', 'tp'), may hold values from -5 to 5
- value_matrix: bfloat16 [8192, 1024], P('ctx', 'tp'), may hold values from -6 to 6
- out_grad: bfloat16 [8192, 5376], P('ctx', 'tp'), may hold values from -16 to 16
- out_weight: bfloat16 [2048, 5376], P('tp', 'ctx'), may hold values from -0.125 to 0.125
Outputs:
- query_grad: bfloat16 [8192, 2048], P('ctx', 'tp')
- key_gradient: bfloat16 [8192, 1024], P('ctx', 'tp')
- value_gradient: bfloat16 [8192, 1024], P('ctx', 'tp')
- weight_grad: float32 [2048, 5376], P('tp', 'ctx')
All inputs are finite; a program needn't handle non-finite values.
Results may differ from a plain program's by a relative error of at most 0.013.
The roundings to bfloat16 on the way count: a program that leaves them out, or rounds other values in their place, can miss the bound.
Values may be sent and summed in bfloat16 or wider, within the bound.
No kernel may reach another device: no remote copies, remote signals or barrier semaphores. Data moves between devices by JAX's collectives and lax.ppermute only.
A program may use at most 128 MiB of HBM per device.

v0:
```python
import jax
import jax.numpy as jnp
from jax import lax
from jax.sharding import PartitionSpec as P


HEAD_SIZE = 128
WINDOW_SPAN = 1024
QUERY_HEAD_COUNT = 16
KEY_VALUE_HEADS = 8


score_scale = 168.0 ** (-0.5)


def from_behind(block, axis, distance):
    devices = range(lax.axis_size(axis))
    route = [(i - distance, i) for i in devices if i - distance in devices]
    return lax.ppermute(block, axis, route)


def band_mask(query_pos, key_pos):
    earlier = key_pos[None, :] <= query_pos[:, None]
    within = query_pos[:, None] - key_pos[None, :] < WINDOW_SPAN
    return earlier & within & (key_pos[None, :] >= 0)


def scores_for(query_head, key_head, allowed):
    scaled = (
        jnp.einsum("tgd,kd->gtk", query_head, key_head, preferred_element_type=jnp.float32)
        * score_scale
    )
    return jnp.where(allowed[None], scaled, -jnp.inf)


def forward_head(query_head, key_head, value_head, allowed):
    scores = scores_for(query_head, key_head, allowed)
    row_max = jnp.max(scores, axis=-1, keepdims=True)
    log_total = row_max + jnp.log(jnp.sum(jnp.exp(scores - row_max), axis=-1, keepdims=True))
    probs = jnp.exp(scores - log_total).astype(jnp.bfloat16)
    output = jnp.einsum("gtk,kd->tgd", probs, value_head, preferred_element_type=jnp.float32)
    return (output.astype(jnp.bfloat16), log_total[..., 0])


def grad_band(query_head, grad_head, log_total, delta_head, key_head, value_head, allowed):
    scores = scores_for(query_head, key_head, allowed)
    probs = jnp.exp(scores - log_total[..., None])
    probs_low = probs.astype(jnp.bfloat16)
    prob_grad = jnp.einsum("tgd,kd->gtk", grad_head, value_head, preferred_element_type=jnp.float32)
    score_grad = (probs * (prob_grad - delta_head.T[..., None])).astype(jnp.bfloat16)
    query_part = (
        jnp.einsum("gtk,kd->tgd", score_grad, key_head, preferred_element_type=jnp.float32)
        * score_scale
    )
    key_part = (
        jnp.einsum("gtk,tgd->kd", score_grad, query_head, preferred_element_type=jnp.float32)
        * score_scale
    )
    value_part = jnp.einsum("gtk,tgd->kd", probs_low, grad_head, preferred_element_type=jnp.float32)
    return (query_part, key_part, value_part)


def device_body(rotated_queries, rotated_keys, value_matrix, out_grad, out_weight):
    tokens_dev = rotated_queries.shape[0]
    n_ctx = lax.axis_size(("cg", "cp"))
    kv_local = rotated_keys.shape[1] // HEAD_SIZE
    group_width = QUERY_HEAD_COUNT // KEY_VALUE_HEADS
    reach_count = WINDOW_SPAN // tokens_dev
    start_pos = lax.axis_index(("cg", "cp")) * tokens_dev
    query_pos = start_pos + jnp.arange(tokens_dev, dtype=jnp.int32)
    kv_width = rotated_keys.shape[1]
    own_pair = jnp.concatenate([rotated_keys, value_matrix], 1)
    earlier = [from_behind(own_pair, ("cg", "cp"), offset) for offset in range(reach_count, 0, -1)]
    pair_ext = jnp.concatenate(earlier + [own_pair], 0)
    key_ext = pair_ext[:, :kv_width]
    value_ext = pair_ext[:, kv_width:]
    key_pos = (
        start_pos
        - reach_count * tokens_dev
        + jnp.arange((reach_count + 1) * tokens_dev, dtype=jnp.int32)
    )
    full_mask = band_mask(query_pos, key_pos)
    query_heads = rotated_queries.reshape(tokens_dev, kv_local, group_width, HEAD_SIZE).transpose(
        1, 0, 2, 3
    )
    key_heads = key_ext.reshape(-1, kv_local, HEAD_SIZE).transpose(1, 0, 2)
    value_heads = value_ext.reshape(-1, kv_local, HEAD_SIZE).transpose(1, 0, 2)
    attn_heads, log_totals = lax.map(
        lambda items: forward_head(items[0], items[1], items[2], full_mask),
        (query_heads, key_heads, value_heads),
    )
    attn_rows = attn_heads.transpose(1, 0, 2, 3)
    attention_probs = attn_rows.reshape(tokens_dev, -1)
    partner_grad = lax.ppermute(out_grad, "tp", [(0, 1), (1, 0)])
    cotangent = jnp.where(
        lax.axis_index("tp") == 0,
        jnp.concatenate([out_grad, partner_grad], 1),
        jnp.concatenate([partner_grad, out_grad], 1),
    )
    group_size = lax.axis_size("cp")
    group_count = lax.axis_size("cg")
    block = cotangent.shape[1] // n_ctx
    weight_rows = out_weight.T
    by_position = cotangent.reshape(tokens_dev, group_count, group_size, block).transpose(2, 0, 1, 3)
    lanes = 128
    weight_flat = weight_rows.reshape(-1, lanes)
    packed = jnp.concatenate(
        [
            jnp.broadcast_to(weight_flat, (group_size,) + weight_flat.shape),
            by_position.reshape(group_size, -1, lanes),
        ],
        1,
    )
    unpacked = lax.all_to_all(packed, "cp", 0, 0, tiled=True)
    weight_count = weight_flat.shape[0]
    group_weights = unpacked[:, :weight_count].reshape(group_size * block, -1)
    group_cotangent = unpacked[:, weight_count:].reshape(
        group_size * tokens_dev, group_count, block
    )
    by_group = cotangent.reshape(tokens_dev, group_count, group_size * block).transpose(1, 0, 2)
    group_columns = lax.all_to_all(by_group, "cg", 0, 0, tiled=True)
    partial_grads = jnp.einsum(
        "btk,kh->bth", group_columns, group_weights, preferred_element_type=jnp.float32
    )
    grad_sum = jnp.sum(
        lax.all_to_all(partial_grads.astype(jnp.bfloat16), "cg", 0, 0, tiled=True).astype(
            jnp.float32
        ),
        0,
    )
    attention_gradient = grad_sum.astype(jnp.bfloat16)
    group_probs = lax.all_gather(attention_probs, "cp", axis=0, tiled=True)
    grad_rows = attention_gradient.reshape(tokens_dev, kv_local, group_width, HEAD_SIZE)
    row_deltas = jnp.sum(grad_rows.astype(jnp.float32) * attn_rows.astype(jnp.float32), axis=-1)
    head_gradients = grad_rows.transpose(1, 0, 2, 3)
    delta_heads = row_deltas.transpose(1, 0, 2)
    query_parts, key_parts, value_parts = lax.map(
        lambda items: grad_band(
            items[0], items[1], items[2], items[3], items[4], items[5], full_mask
        ),
        (query_heads, head_gradients, log_totals, delta_heads, key_heads, value_heads),
    )
    key_ext_grad = key_parts.transpose(1, 0, 2).reshape(-1, kv_local * HEAD_SIZE)
    value_ext_grad = value_parts.transpose(1, 0, 2).reshape(-1, kv_local * HEAD_SIZE)
    pair_grad = jnp.concatenate([key_ext_grad, value_ext_grad], 1)
    pair_total = pair_grad[reach_count * tokens_dev :]
    sent = [
        pair_grad[(reach_count - offset) * tokens_dev : (reach_count - offset + 1) * tokens_dev]
        for offset in range(1, reach_count + 1)
    ]
    sent = [block.astype(jnp.bfloat16) for block in sent]
    for offset in range(1, reach_count + 1):
        arrived = from_behind(sent[offset - 1], ("cg", "cp"), -offset)
        pair_total = pair_total + arrived.astype(jnp.float32)
    group_probs, group_cotangent, sent = lax.optimization_barrier(
        (group_probs, group_cotangent, sent)
    )
    weight_term = jnp.einsum(
        "th,tak->ahk", group_probs, group_cotangent, preferred_element_type=jnp.float32
    ) * (tokens_dev * n_ctx) ** (-0.5)
    weight_grad = jnp.sum(lax.all_to_all(weight_term, "cg", 0, 0, tiled=True), 0)
    key_total = pair_total[:, :kv_width]
    value_total = pair_total[:, kv_width:]
    query_grad = query_parts.transpose(1, 0, 2, 3).reshape(tokens_dev, -1).astype(jnp.bfloat16)
    return (
        query_grad,
        key_total.astype(jnp.bfloat16),
        value_total.astype(jnp.bfloat16),
        weight_grad,
    )


GROUP_SIZE = 8


def solution(mesh):
    n_ctx = mesh.shape["ctx"]
    group_size = GROUP_SIZE if n_ctx % GROUP_SIZE == 0 else 1
    devices = mesh.devices.reshape(n_ctx // group_size, group_size, mesh.shape["tp"])
    grouped = jax.sharding.Mesh(devices, ("cg", "cp", "tp"))
    ctx = ("cg", "cp")
    placed = (P(ctx, "tp"), P(ctx, "tp"), P(ctx, "tp"), P(ctx, "tp"), P("tp", ctx))
    return jax.shard_map(
        device_body,
        mesh=grouped,
        in_specs=placed,
        out_specs=(P(ctx, "tp"), P(ctx, "tp"), P(ctx, "tp"), P("tp", ctx)),
        check_vma=False,
    )
```

profile of v0, /device:TPU:8, one launch (start us, length us, event | category | flops | bytes accessed | tf_op | source)
XLA Modules:
  0.0 306.0 jit_solution(15687669916339335663)
XLA Ops:
  11.3 14.9 %collective-permute-done.8 = bf16[128,2688]{1,0:T(8,128)(2,1)S(1)} collective-permute-done((bf16[128,2688]{1,0:T(8,128)(2,1)}, bf16[128,2688]{1,0:T(8,128)(2,1)S(1)}, u32[]{:S(2)}, u32[]{:S(2)}) %collective-permute-start.8) | collective-permute-done | bytes 688160 | tf_op jit(solution)/shard_map/ppermute | solution.py:94
  28.7 3.1 %copy.54 = bf16[8,128,8,84]{3,2,1,0:T(8,128)(2,1)S(1)} copy(bf16[8,128,8,84]{1,3,0,2:T(8,128)(2,1)} %fusion.63) | data formatting | bytes 2752512 | tf_op jit(solution)/shard_map/transpose | solution.py:104
  31.9 8.0 %reshape.100 = bf16[8,672,128]{2,1,0:T(8,128)(2,1)} reshape(bf16[8,128,8,84]{3,2,1,0:T(8,128)(2,1)S(1)} %copy.54) | data formatting | bytes 2752512 | tf_op jit(solution)/shard_map/reshape | solution.py:110
  43.0 5.3 %all-to-all-start.1 = ((bf16[8,1344,128]{2,1,0:T(8,128)(2,1)}), bf16[8,1344,128]{2,1,0:T(8,128)(2,1)S(1)}, u32[]{:S(2)}, u32[]{:S(2)}) async-start(bf16[8,1344,128]{2,1,0:T(8,128)(2,1)} %pad_maximum_fusion), calls=%async_computation.1 | async-start | bytes 5505024 | tf_op jit(solution)/shard_map/all_to_all | solution.py:114
  53.3 3.3 %collective-permute-start = (bf16[128,1024]{0,1:T(8,128)(2,1)}, bf16[128,1024]{0,1:T(8,128)(2,1)}, u32[]{:S(2)}, u32[]{:S(2)}) collective-permute-start(bf16[128,1024]{0,1:T(8,128)(2,1)} %pad_maximum_fusion.1), channel_id=1, source_target_pairs={{0,16},{2,18},{4,20},{6,22},{8,24},{10,26},{12,28},{14,30},{16,32}... | collective-permute-start | bytes 786440 | tf_op jit(solution)/shard_map/ppermute | solution.py:19
  56.6 4.6 %collective-permute-start.1 = (bf16[128,1024]{0,1:T(8,128)(2,1)}, bf16[128,1024]{0,1:T(8,128)(2,1)}, u32[]{:S(2)}, u32[]{:S(2)}) collective-permute-start(bf16[128,1024]{0,1:T(8,128)(2,1)} %pad_maximum_fusion.1), channel_id=1, source_target_pairs={{0,14},{2,16},{4,18},{6,20},{8,22},{10,24},{12,26},{14,28},{16,30}... | collective-permute-start | bytes 786440 | tf_op jit(solution)/shard_map/ppermute | solution.py:19
  61.2 3.8 %collective-permute-start.2 = (bf16[128,1024]{0,1:T(8,128)(2,1)}, bf16[128,1024]{0,1:T(8,128)(2,1)}, u32[]{:S(2)}, u32[]{:S(2)}) collective-permute-start(bf16[128,1024]{0,1:T(8,128)(2,1)} %pad_maximum_fusion.1), channel_id=1, source_target_pairs={{0,12},{2,14},{4,16},{6,18},{8,20},{10,22},{12,24},{14,26},{16,28}... | collective-permute-start | bytes 786440 | tf_op jit(solution)/shard_map/ppermute | solution.py:19
  65.0 3.3 %collective-permute-start.3 = (bf16[128,1024]{0,1:T(8,128)(2,1)}, bf16[128,1024]{0,1:T(8,128)(2,1)}, u32[]{:S(2)}, u32[]{:S(2)}) collective-permute-start(bf16[128,1024]{0,1:T(8,128)(2,1)} %pad_maximum_fusion.1), channel_id=1, source_target_pairs={{0,10},{2,12},{4,14},{6,16},{8,18},{10,20},{12,22},{14,24},{16,26}... | collective-permute-start | bytes 786440 | tf_op jit(solution)/shard_map/ppermute | solution.py:19
  68.3 4.6 %collective-permute-start.4 = (bf16[128,1024]{0,1:T(8,128)(2,1)}, bf16[128,1024]{0,1:T(8,128)(2,1)}, u32[]{:S(2)}, u32[]{:S(2)}) collective-permute-start(bf16[128,1024]{0,1:T(8,128)(2,1)} %pad_maximum_fusion.1), channel_id=1, source_target_pairs={{0,8},{2,10},{4,12},{6,14},{8,16},{10,18},{12,20},{14,22},{16,24},... | collective-permute-start | bytes 786440 | tf_op jit(solution)/shard_map/ppermute | solution.py:19
  80.4 3.2 %collective-permute-start.6 = (bf16[128,1024]{0,1:T(8,128)(2,1)}, bf16[128,1024]{0,1:T(8,128)(2,1)}, u32[]{:S(2)}, u32[]{:S(2)}) collective-permute-start(bf16[128,1024]{0,1:T(8,128)(2,1)} %pad_maximum_fusion.1), channel_id=1, source_target_pairs={{0,4},{2,6},{4,8},{6,10},{8,12},{10,14},{12,16},{14,18},{16,20},{1... | collective-permute-start | bytes 786440 | tf_op jit(solution)/shard_map/ppermute | solution.py:19
  85.2 3.2 %collective-permute-start.7 = (bf16[128,1024]{0,1:T(8,128)(2,1)}, bf16[128,1024]{0,1:T(8,128)(2,1)}, u32[]{:S(2)}, u32[]{:S(2)}) collective-permute-start(bf16[128,1024]{0,1:T(8,128)(2,1)} %pad_maximum_fusion.1), channel_id=1, source_target_pairs={{0,2},{2,4},{4,6},{6,8},{8,10},{10,12},{12,14},{14,16},{16,18},{18... | collective-permute-start | bytes 786440 | tf_op jit(solution)/shard_map/ppermute | solution.py:19
  93.6 2.5 collective-permute-done.5
  98.2 17.3 %all-to-all-start = ((bf16[8,128,672]{1,2,0:T(8,128)(2,1)}), bf16[8,128,672]{1,2,0:T(8,128)(2,1)}, u32[]{:S(2)}, u32[]{:S(2)}) async-start(bf16[8,128,672]{1,2,0:T(8,128)(2,1)} %fusion.64), calls=%async_computation | async-start | bytes 2752512 | tf_op jit(solution)/shard_map/all_to_all | solution.py:121
  122.4 3.4 %fusion.74 = (bf16[8,672,128]{2,1,0:T(8,128)(2,1)}, bf16[8,672,128]{2,1,0:T(8,128)(2,1)}) fusion(bf16[8,1344,128]{2,1,0:T(8,128)(2,1)} %copy-done.1), kind=kLoop, calls=%fused_computation.105 | loop fusion | bytes 5505024 | tf_op jit(solution)/shard_map/slice | solution.py:117
  125.8 3.4 %reshape.114 = bf16[672,1024,1]{1,0,2:T(8,128)(2,1)} reshape(bf16[8,672,128]{2,1,0:T(8,128)(2,1)} %get-tuple-element.266) | data formatting | bytes 2752512 | tf_op jit(solution)/shard_map/reshape | solution.py:116
  131.4 4.9 %convolution_convert_fusion.1 = bf16[8,128,1024]{2,1,0:T(8,128)(2,1)} fusion(bf16[8,128,672]{1,2,0:T(8,128)(2,1)} %all-to-all-done, bf16[672,1024,1]{1,0,2:T(8,128)(2,1)} %reshape.114), kind=kOutput, calls=%fused_computation.76 | convolution fusion | flops 1410334720 | bytes 4849664 | tf_op jit(solution)/shard_map/btk,kh->bth/dot_general | solution.py:122
  136.4 5.2 %all-to-all-start.2 = ((bf16[8,128,1024]{2,1,0:T(8,128)(2,1)}), bf16[8,128,1024]{2,1,0:T(8,128)(2,1)}, u32[]{:S(2)}, u32[]{:S(2)}) async-start(bf16[8,128,1024]{2,1,0:T(8,128)(2,1)} %convolution_convert_fusion.1), calls=%async_computation.2 | async-start | bytes 4194304 | tf_op jit(solution)/shard_map/all_to_all | solution.py:126
  141.6 7.3 %while.28 = (s32[]{:T(128)}, bf16[4,128,2,128]{1,3,2,0:T(8,128)(2,1)S(1)}, f32[4,2,128]{2,1,0:T(2,128)S(1)}, bf16[4,1152,128]{1,2,0:T(8,128)(2,1)S(1)}, bf16[4,1...) while((s32[]{:T(128)}, ...), condition=%wide.region_4.5_spmd.clone, body=%wide.region_1.0_spmd.clone.sunk | while | flops 153829120 | bytes 4571369 | solution.py:88
  149.7 9.2 %reshape.106 = bf16[1024,8,84]{2,1,0:T(8,128)(2,1)} reshape(bf16[8,672,128]{2,1,0:T(8,128)(2,1)} %get-tuple-element.265) | data formatting | bytes 2752512 | tf_op jit(solution)/shard_map/reshape | solution.py:117
  158.9 6.0 %all-to-all-done.2 = bf16[8,128,1024]{2,1,0:T(8,128)(2,1)} async-done(((bf16[8,128,1024]{2,1,0:T(8,128)(2,1)}), bf16[8,128,1024]{2,1,0:T(8,128)(2,1)}, u32[]{:S(2)}, u32[]{:S(2)}) %all-to-all-start.2) | async-done | bytes 2097184 | tf_op jit(solution)/shard_map/all_to_all | solution.py:126
  167.2 20.0 %while.29 = (s32[]{:T(128)}, bf16[4,128,2,128]{1,3,2,0:T(8,128)(2,1)}, f32[4,1152,128]{2,1,0:T(8,128)}, f32[4,1152,128]{2,1,0:T(8,128)}, bf16[4,1152,128]{2,1,0:...) while((s32[]{:T(128)}, ...), condition=%wide.region_7.8_spmd.clone, body=%wide.region_6.7_spmd.clone.sunk | while | flops 380469248 | bytes 10175813 | solution.py:137
  194.3 5.6 %multiply_bitcast_fusion = f32[8,1024,84]{1,2,0:T(8,128)} fusion(bf16[1024,1024]{0,1:T(8,128)(2,1)} %all-gather.2.cloned.1.call-done, bf16[1024,8,84]{2,1,0:T(8,128)(2,1)S(1)} %copy-done.7), kind=kOutput, calls=%fused_computation.69 | convolution fusion | flops 1409974272 | bytes 6225920 | tf_op jit(solution)/shard_map/th,tak->ahk/dot_general | solution.py:158
  199.9 7.2 %all-to-all-start.3 = ((f32[8,1024,84]{1,2,0:T(8,128)}), f32[8,1024,84]{1,2,0:T(8,128)S(1)}, u32[]{:S(2)}, u32[]{:S(2)}) async-start(f32[8,1024,84]{1,2,0:T(8,128)} %multiply_bitcast_fusion), calls=%async_computation.3 | async-start | bytes 5767168 | tf_op jit(solution)/shard_map/all_to_all | solution.py:161
  207.0 9.3 %collective-permute-start.10 = (bf16[128,1024]{1,0:T(8,128)(2,1)}, bf16[128,1024]{1,0:T(8,128)(2,1)S(1)}, u32[]{:S(2)}, u32[]{:S(2)}) collective-permute-start(bf16[128,1024]{1,0:T(8,128)(2,1)} %get-tuple-element.274), channel_id=1, source_target_pairs={{4,0},{6,2},{8,4},{10,6},{12,8},{14,10},{16,12},{18,14},{20,16},{2... | collective-permute-start | bytes 786440 | tf_op jit(solution)/shard_map/ppermute | solution.py:19
  216.3 7.1 %collective-permute-start.11 = (bf16[128,1024]{1,0:T(8,128)(2,1)}, bf16[128,1024]{1,0:T(8,128)(2,1)S(1)}, u32[]{:S(2)}, u32[]{:S(2)}) collective-permute-start(bf16[128,1024]{1,0:T(8,128)(2,1)} %get-tuple-element.273), channel_id=1, source_target_pairs={{6,0},{8,2},{10,4},{12,6},{14,8},{16,10},{18,12},{20,14},{22,16},{... | collective-permute-start | bytes 786440 | tf_op jit(solution)/shard_map/ppermute | solution.py:19
  229.5 21.4 %collective-permute-done.10 = bf16[128,1024]{1,0:T(8,128)(2,1)S(1)} collective-permute-done((bf16[128,1024]{1,0:T(8,128)(2,1)}, bf16[128,1024]{1,0:T(8,128)(2,1)S(1)}, u32[]{:S(2)}, u32[]{:S(2)}) %collective-permute-start.10) | collective-permute-done | bytes 262176 | tf_op jit(solution)/shard_map/ppermute | solution.py:19
  252.8 5.4 %collective-permute-done.11 = bf16[128,1024]{1,0:T(8,128)(2,1)S(1)} collective-permute-done((bf16[128,1024]{1,0:T(8,128)(2,1)}, bf16[128,1024]{1,0:T(8,128)(2,1)S(1)}, u32[]{:S(2)}, u32[]{:S(2)}) %collective-permute-start.11) | collective-permute-done | bytes 262176 | tf_op jit(solution)/shard_map/ppermute | solution.py:19
  260.2 8.2 %collective-permute-done.12 = bf16[128,1024]{1,0:T(8,128)(2,1)S(1)} collective-permute-done((bf16[128,1024]{1,0:T(8,128)(2,1)}, bf16[128,1024]{1,0:T(8,128)(2,1)S(1)}, u32[]{:S(2)}, u32[]{:S(2)}) %collective-permute-start.12) | collective-permute-done | bytes 262176 | tf_op jit(solution)/shard_map/ppermute | solution.py:19
  272.2 2.6 collective-permute-done.13
  274.8 5.6 %collective-permute-done.14 = bf16[128,1024]{1,0:T(8,128)(2,1)} collective-permute-done((bf16[128,1024]{1,0:T(8,128)(2,1)}, bf16[128,1024]{1,0:T(8,128)(2,1)}, u32[]{:S(2)}, u32[]{:S(2)}) %collective-permute-start.14) | collective-permute-done | bytes 262176 | tf_op jit(solution)/shard_map/ppermute | solution.py:19
  280.5 5.6 %collective-permute-done.15 = bf16[128,1024]{1,0:T(8,128)(2,1)} collective-permute-done((bf16[128,1024]{1,0:T(8,128)(2,1)}, bf16[128,1024]{1,0:T(8,128)(2,1)}, u32[]{:S(2)}, u32[]{:S(2)}) %collective-permute-start.15) | collective-permute-done | bytes 262176 | tf_op jit(solution)/shard_map/ppermute | solution.py:19
  286.1 9.4 %collective-permute-done.16 = bf16[128,1024]{1,0:T(8,128)(2,1)} collective-permute-done((bf16[128,1024]{1,0:T(8,128)(2,1)S(1)}, bf16[128,1024]{1,0:T(8,128)(2,1)}, u32[]{:S(2)}, u32[]{:S(2)}) %collective-permute-start.16) | collective-permute-done | bytes 262176 | tf_op jit(solution)/shard_map/ppermute | solution.py:19
  (170 shorter events, 94.6 us)
Async XLA Ops:
  7.2 19.0 %collective-permute-start.8 = (bf16[128,2688]{1,0:T(8,128)(2,1)}, bf16[128,2688]{1,0:T(8,128)(2,1)S(1)}, u32[]{:S(2)}, u32[]{:S(2)}) collective-permute-start(bf16[128,2688]{1,0:T(8,128)(2,1)} %param.12), channel_id=1, source_target_pairs={{0,1},{1,0},{2,3},{3,2},{4,5},{5,4},{6,7},{7,6},{8,9},{9,8},{10,11... | collective-permute-start | bytes 2064392 | tf_op jit(solution)/shard_map/ppermute | solution.py:94
  43.0 55.2 %all-to-all-start.1 = ((bf16[8,1344,128]{2,1,0:T(8,128)(2,1)}), bf16[8,1344,128]{2,1,0:T(8,128)(2,1)S(1)}, u32[]{:S(2)}, u32[]{:S(2)}) async-start(bf16[8,1344,128]{2,1,0:T(8,128)(2,1)} %pad_maximum_fusion), calls=%async_computation.1 | async-start | bytes 5505024 | tf_op jit(solution)/shard_map/all_to_all | solution.py:114
  53.3 23.2 %collective-permute-start = (bf16[128,1024]{0,1:T(8,128)(2,1)}, bf16[128,1024]{0,1:T(8,128)(2,1)}, u32[]{:S(2)}, u32[]{:S(2)}) collective-permute-start(bf16[128,1024]{0,1:T(8,128)(2,1)} %pad_maximum_fusion.1), channel_id=1, source_target_pairs={{0,16},{2,18},{4,20},{6,22},{8,24},{10,26},{12,28},{14,30},{16,32}... | collective-permute-start | bytes 786440 | tf_op jit(solution)/shard_map/ppermute | solution.py:19
  56.6 23.7 %collective-permute-start.1 = (bf16[128,1024]{0,1:T(8,128)(2,1)}, bf16[128,1024]{0,1:T(8,128)(2,1)}, u32[]{:S(2)}, u32[]{:S(2)}) collective-permute-start(bf16[128,1024]{0,1:T(8,128)(2,1)} %pad_maximum_fusion.1), channel_id=1, source_target_pairs={{0,14},{2,16},{4,18},{6,20},{8,22},{10,24},{12,26},{14,28},{16,30}... | collective-permute-start | bytes 786440 | tf_op jit(solution)/shard_map/ppermute | solution.py:19
  61.2 24.0 %collective-permute-start.2 = (bf16[128,1024]{0,1:T(8,128)(2,1)}, bf16[128,1024]{0,1:T(8,128)(2,1)}, u32[]{:S(2)}, u32[]{:S(2)}) collective-permute-start(bf16[128,1024]{0,1:T(8,128)(2,1)} %pad_maximum_fusion.1), channel_id=1, source_target_pairs={{0,12},{2,14},{4,16},{6,18},{8,20},{10,22},{12,24},{14,26},{16,28}... | collective-permute-start | bytes 786440 | tf_op jit(solution)/shard_map/ppermute | solution.py:19
  65.0 25.2 %collective-permute-start.3 = (bf16[128,1024]{0,1:T(8,128)(2,1)}, bf16[128,1024]{0,1:T(8,128)(2,1)}, u32[]{:S(2)}, u32[]{:S(2)}) collective-permute-start(bf16[128,1024]{0,1:T(8,128)(2,1)} %pad_maximum_fusion.1), channel_id=1, source_target_pairs={{0,10},{2,12},{4,14},{6,16},{8,18},{10,20},{12,22},{14,24},{16,26}... | collective-permute-start | bytes 786440 | tf_op jit(solution)/shard_map/ppermute | solution.py:19
  68.3 23.6 %collective-permute-start.4 = (bf16[128,1024]{0,1:T(8,128)(2,1)}, bf16[128,1024]{0,1:T(8,128)(2,1)}, u32[]{:S(2)}, u32[]{:S(2)}) collective-permute-start(bf16[128,1024]{0,1:T(8,128)(2,1)} %pad_maximum_fusion.1), channel_id=1, source_target_pairs={{0,8},{2,10},{4,12},{6,14},{8,16},{10,18},{12,20},{14,22},{16,24},... | collective-permute-start | bytes 786440 | tf_op jit(solution)/shard_map/ppermute | solution.py:19
  76.6 20.3 %copy-start.3 = (bf16[128,2688]{0,1:T(8,128)(2,1)S(1)}, bf16[128,2688]{0,1:T(8,128)(2,1)}, u32[]{:S(2)}) copy-start(bf16[128,2688]{0,1:T(8,128)(2,1)} %copy-done.2) | copy-start | bytes 2064388
  76.6 19.5 %collective-permute-start.5 = (bf16[128,1024]{0,1:T(8,128)(2,1)}, bf16[128,1024]{0,1:T(8,128)(2,1)S(1)}, u32[]{:S(2)}, u32[]{:S(2)}) collective-permute-start(bf16[128,1024]{0,1:T(8,128)(2,1)} %pad_maximum_fusion.1), channel_id=1, source_target_pairs={{0,6},{2,8},{4,10},{6,12},{8,14},{10,16},{12,18},{14,20},{16,22},{... | collective-permute-start | bytes 786440 | tf_op jit(solution)/shard_map/ppermute | solution.py:19
  80.4 35.2 %collective-permute-start.6 = (bf16[128,1024]{0,1:T(8,128)(2,1)}, bf16[128,1024]{0,1:T(8,128)(2,1)}, u32[]{:S(2)}, u32[]{:S(2)}) collective-permute-start(bf16[128,1024]{0,1:T(8,128)(2,1)} %pad_maximum_fusion.1), channel_id=1, source_target_pairs={{0,4},{2,6},{4,8},{6,10},{8,12},{10,14},{12,16},{14,18},{16,20},{1... | collective-permute-start | bytes 786440 | tf_op jit(solution)/shard_map/ppermute | solution.py:19
  85.2 32.0 %collective-permute-start.7 = (bf16[128,1024]{0,1:T(8,128)(2,1)}, bf16[128,1024]{0,1:T(8,128)(2,1)}, u32[]{:S(2)}, u32[]{:S(2)}) collective-permute-start(bf16[128,1024]{0,1:T(8,128)(2,1)} %pad_maximum_fusion.1), channel_id=1, source_target_pairs={{0,2},{2,4},{4,6},{6,8},{8,10},{10,12},{12,14},{14,16},{16,18},{18... | collective-permute-start | bytes 786440 | tf_op jit(solution)/shard_map/ppermute | solution.py:19
  98.2 20.7 %copy-start.8 = (bf16[128,512]{0,1:T(8,128)(2,1)S(1)}, bf16[128,512]{0,1:T(8,128)(2,1)}, u32[]{:S(2)}) copy-start(bf16[128,512]{0,1:T(8,128)(2,1)} %copy.45) | copy-start | bytes 393220
  98.2 20.7 %copy-start.9 = (bf16[128,512]{0,1:T(8,128)(2,1)S(1)}, bf16[128,512]{0,1:T(8,128)(2,1)}, u32[]{:S(2)}) copy-start(bf16[128,512]{0,1:T(8,128)(2,1)} %copy.46) | copy-start | bytes 393220
  98.2 20.7 %copy-start.1 = (bf16[8,1344,128]{2,1,0:T(8,128)(2,1)}, bf16[8,1344,128]{2,1,0:T(8,128)(2,1)S(1)}, u32[]{:S(2)}) copy-start(bf16[8,1344,128]{2,1,0:T(8,128)(2,1)S(1)} %all-to-all-done.1) | copy-start | bytes 8257540
  98.2 33.2 %all-to-all-start = ((bf16[8,128,672]{1,2,0:T(8,128)(2,1)}), bf16[8,128,672]{1,2,0:T(8,128)(2,1)}, u32[]{:S(2)}, u32[]{:S(2)}) async-start(bf16[8,128,672]{1,2,0:T(8,128)(2,1)} %fusion.64), calls=%async_computation | async-start | bytes 2752512 | tf_op jit(solution)/shard_map/all_to_all | solution.py:121
  136.4 5.2 %copy-start.5 = (bf16[4,128,2,128]{3,1,2,0:T(8,128)(2,1)S(1)}, bf16[4,128,2,128]{3,1,2,0:T(8,128)(2,1)}, u32[]{:S(2)}) copy-start(bf16[4,128,2,128]{3,1,2,0:T(8,128)(2,1)} %copy.57) | copy-start | bytes 786436
  136.4 5.2 %copy-start.10 = (bf16[4,128,2,128]{1,3,2,0:T(8,128)(2,1)S(1)}, bf16[4,128,2,128]{1,3,2,0:T(8,128)(2,1)}, u32[]{:S(2)}) copy-start(bf16[4,128,2,128]{1,3,2,0:T(8,128)(2,1)} %custom-call.2) | copy-start | bytes 786436
  136.4 5.2 %copy-start.19 = (f32[4,2,128]{2,1,0:T(2,128)S(1)}, f32[4,2,128]{2,1,0:T(2,128)}, u32[]{:S(2)}) copy-start(f32[4,2,128]{2,1,0:T(2,128)} %custom-call.3) | copy-start | bytes 12292
  136.4 28.5 %all-to-all-start.2 = ((bf16[8,128,1024]{2,1,0:T(8,128)(2,1)}), bf16[8,128,1024]{2,1,0:T(8,128)(2,1)}, u32[]{:S(2)}, u32[]{:S(2)}) async-start(bf16[8,128,1024]{2,1,0:T(8,128)(2,1)} %convolution_convert_fusion.1), calls=%async_computation.2 | async-start | bytes 4194304 | tf_op jit(solution)/shard_map/all_to_all | solution.py:126
  141.6 51.7 %all-gather.2.cloned.1.call-start = ((), (), s32[]{:S(2)}) async-start(), calls=%async_computation.4 | async-start | bytes 2359296 | tf_op jit(solution)/shard_map/all_gather | solution.py:132
  158.9 8.2 %copy-start.12 = (bf16[4,128,2,128]{1,3,2,0:T(8,128)(2,1)S(1)}, bf16[4,128,2,128]{1,3,2,0:T(8,128)(2,1)}, u32[]{:S(2)}) copy-start(bf16[4,128,2,128]{1,3,2,0:T(8,128)(2,1)} %copy-done.11) | copy-start | bytes 786436
  199.9 98.4 %all-to-all-start.3 = ((f32[8,1024,84]{1,2,0:T(8,128)}), f32[8,1024,84]{1,2,0:T(8,128)S(1)}, u32[]{:S(2)}, u32[]{:S(2)}) async-start(f32[8,1024,84]{1,2,0:T(8,128)} %multiply_bitcast_fusion), calls=%async_computation.3 | async-start | bytes 5767168 | tf_op jit(solution)/shard_map/all_to_all | solution.py:161
  207.0 43.9 %collective-permute-start.10 = (bf16[128,1024]{1,0:T(8,128)(2,1)}, bf16[128,1024]{1,0:T(8,128)(2,1)S(1)}, u32[]{:S(2)}, u32[]{:S(2)}) collective-permute-start(bf16[128,1024]{1,0:T(8,128)(2,1)} %get-tuple-element.274), channel_id=1, source_target_pairs={{4,0},{6,2},{8,4},{10,6},{12,8},{14,10},{16,12},{18,14},{20,16},{2... | collective-permute-start | bytes 786440 | tf_op jit(solution)/shard_map/ppermute | solution.py:19
  216.3 42.0 %collective-permute-start.11 = (bf16[128,1024]{1,0:T(8,128)(2,1)}, bf16[128,1024]{1,0:T(8,128)(2,1)S(1)}, u32[]{:S(2)}, u32[]{:S(2)}) collective-permute-start(bf16[128,1024]{1,0:T(8,128)(2,1)} %get-tuple-element.273), channel_id=1, source_target_pairs={{6,0},{8,2},{10,4},{12,6},{14,8},{16,10},{18,12},{20,14},{22,16},{... | collective-permute-start | bytes 786440 | tf_op jit(solution)/shard_map/ppermute | solution.py:19
  223.3 45.1 %collective-permute-start.12 = (bf16[128,1024]{1,0:T(8,128)(2,1)}, bf16[128,1024]{1,0:T(8,128)(2,1)S(1)}, u32[]{:S(2)}, u32[]{:S(2)}) collective-permute-start(bf16[128,1024]{1,0:T(8,128)(2,1)} %get-tuple-element.272), channel_id=1, source_target_pairs={{8,0},{10,2},{12,4},{14,6},{16,8},{18,10},{20,12},{22,14},{24,16},... | collective-permute-start | bytes 786440 | tf_op jit(solution)/shard_map/ppermute | solution.py:19
  225.7 49.2 %collective-permute-start.13 = (bf16[128,1024]{1,0:T(8,128)(2,1)}, bf16[128,1024]{1,0:T(8,128)(2,1)}, u32[]{:S(2)}, u32[]{:S(2)}) collective-permute-start(bf16[128,1024]{1,0:T(8,128)(2,1)} %get-tuple-element.271), channel_id=1, source_target_pairs={{10,0},{12,2},{14,4},{16,6},{18,8},{20,10},{22,12},{24,14},{26,16}... | collective-permute-start | bytes 786440 | tf_op jit(solution)/shard_map/ppermute | solution.py:19
  227.6 52.9 %collective-permute-start.14 = (bf16[128,1024]{1,0:T(8,128)(2,1)}, bf16[128,1024]{1,0:T(8,128)(2,1)}, u32[]{:S(2)}, u32[]{:S(2)}) collective-permute-start(bf16[128,1024]{1,0:T(8,128)(2,1)} %get-tuple-element.270), channel_id=1, source_target_pairs={{12,0},{14,2},{16,4},{18,6},{20,8},{22,10},{24,12},{26,14},{28,16}... | collective-permute-start | bytes 786440 | tf_op jit(solution)/shard_map/ppermute | solution.py:19
  250.9 19.4 %copy-start.15 = (bf16[128,1024]{1,0:T(8,128)(2,1)}, bf16[128,1024]{1,0:T(8,128)(2,1)S(1)}, u32[]{:S(2)}) copy-start(bf16[128,1024]{1,0:T(8,128)(2,1)S(1)} %collective-permute-done.10) | copy-start | bytes 786436
  250.9 35.2 %collective-permute-start.15 = (bf16[128,1024]{1,0:T(8,128)(2,1)}, bf16[128,1024]{1,0:T(8,128)(2,1)}, u32[]{:S(2)}, u32[]{:S(2)}) collective-permute-start(bf16[128,1024]{1,0:T(8,128)(2,1)} %get-tuple-element.269), channel_id=1, source_target_pairs={{14,0},{16,2},{18,4},{20,6},{22,8},{24,10},{26,12},{28,14},{30,16}... | collective-permute-start | bytes 786440 | tf_op jit(solution)/shard_map/ppermute | solution.py:19
  258.3 12.1 %copy-start.16 = (bf16[128,1024]{1,0:T(8,128)(2,1)}, bf16[128,1024]{1,0:T(8,128)(2,1)S(1)}, u32[]{:S(2)}) copy-start(bf16[128,1024]{1,0:T(8,128)(2,1)S(1)} %collective-permute-done.11) | copy-start | bytes 786436
  258.3 37.2 %collective-permute-start.16 = (bf16[128,1024]{1,0:T(8,128)(2,1)S(1)}, bf16[128,1024]{1,0:T(8,128)(2,1)}, u32[]{:S(2)}, u32[]{:S(2)}) collective-permute-start(bf16[128,1024]{1,0:T(8,128)(2,1)S(1)} %get-tuple-element.268), channel_id=1, source_target_pairs={{16,0},{18,2},{20,4},{22,6},{24,8},{26,10},{28,12},{30,14},{32,16}... | collective-permute-start | bytes 786440 | tf_op jit(solution)/shard_map/ppermute | solution.py:19
  268.4 27.0 %collective-permute-start.9 = (bf16[128,1024]{1,0:T(8,128)(2,1)S(1)}, bf16[128,1024]{1,0:T(8,128)(2,1)}, u32[]{:S(2)}, u32[]{:S(2)}) collective-permute-start(bf16[128,1024]{1,0:T(8,128)(2,1)S(1)} %get-tuple-element.267), channel_id=1, source_target_pairs={{2,0},{4,2},{6,4},{8,6},{10,8},{12,10},{14,12},{16,14},{18,16},{20... | collective-permute-start | bytes 786440 | tf_op jit(solution)/shard_map/ppermute | solution.py:19
  (16 other events, 29.1 us)
Sparse Core Ops, SparseCore 0:
  149.8 33.2 all-gather.1
where the time goes:
time: 310 us; the launch traced here: 306 us
  starting transfers between devices  93.4 us (30%)
  waiting for transfers between devices  84 us (27%)
  local copies, waits for them, and re-layouts  66.6 us (21%)
  matrix products  26.9 us (9%)
  other arithmetic  20.2 us (7%)
  between operations  14.4 us (5%)
    ppermute x16, waiting for transfers between devices, from_behind(): return lax.ppermute(block, axis, route)  60.9 us
    ppermute x16, starting transfers between devices, from_behind(): return lax.ppermute(block, axis, route)  56.1 us
    unnamed x51, local copies, waits for them, and re-layouts  29.7 us
    all_to_all x1, starting transfers between devices, device_body(): group_columns = lax.all_to_all(by_group, 'cg', 0, 0, tiled=True)  17.3 us
    ppermute x1, waiting for transfers between devices, device_body(): partner_grad = lax.ppermute(out_grad, 'tp', [(0, 1), (1, 0)])  14.9 us
    reshape x1, local copies, waits for them, and re-layouts, device_body(): unpacked[:, weight_count:]  9.21 us
    reshape x1, local copies, waits for them, and re-layouts, device_body(): by_position.reshape(group_size, -1, lanes)  8.01 us
    all_to_all x1, starting transfers between devices, device_body(): lax.all_to_all(weight_term, 'cg', 0, 0, tiled=True)  7.15 us
  transfers between devices with their start and end apart: 22, of which 11 were waited for; matrix products, arithmetic and copies ran while one was open for 26% of the time, Pallas kernels for 0%

commit v1 on v0

--- a/solution.py
+++ b/solution.py
@@ -101,29 +101,20 @@
     group_count = lax.axis_size("cg")
     block = cotangent.shape[1] // n_ctx
     weight_rows = out_weight.T
-    by_position = cotangent.reshape(tokens_dev, group_count, group_size, block).transpose(2, 0, 1, 3)
-    lanes = 128
-    weight_flat = weight_rows.reshape(-1, lanes)
-    packed = jnp.concatenate(
-        [
-            jnp.broadcast_to(weight_flat, (group_size,) + weight_flat.shape),
-            by_position.reshape(group_size, -1, lanes),
-        ],
-        1,
+    group_weights = lax.all_to_all(
+        jnp.broadcast_to(weight_rows, (group_count,) + weight_rows.shape), "cg", 0, 0, tiled=True
+    ).reshape(group_count * block, -1)
+    by_group = (
+        cotangent.reshape(tokens_dev, group_count, group_size, block)
+        .transpose(2, 0, 1, 3)
+        .reshape(group_size, tokens_dev, group_count * block)
     )
-    unpacked = lax.all_to_all(packed, "cp", 0, 0, tiled=True)
-    weight_count = weight_flat.shape[0]
-    group_weights = unpacked[:, :weight_count].reshape(group_size * block, -1)
-    group_cotangent = unpacked[:, weight_count:].reshape(
-        group_size * tokens_dev, group_count, block
-    )
-    by_group = cotangent.reshape(tokens_dev, group_count, group_size * block).transpose(1, 0, 2)
-    group_columns = lax.all_to_all(by_group, "cg", 0, 0, tiled=True)
+    group_columns = lax.all_to_all(by_group, "cp", 0, 0, tiled=True)
     partial_grads = jnp.einsum(
         "btk,kh->bth", group_columns, group_weights, preferred_element_type=jnp.float32
     )
     grad_sum = jnp.sum(
-        lax.all_to_all(partial_grads.astype(jnp.bfloat16), "cg", 0, 0, tiled=True).astype(
+        lax.all_to_all(partial_grads.astype(jnp.bfloat16), "cp", 0, 0, tiled=True).astype(
             jnp.float32
         ),
         0,
@@ -152,13 +143,15 @@
     for offset in range(1, reach_count + 1):
         arrived = from_behind(sent[offset - 1], ("cg", "cp"), -offset)
         pair_total = pair_total + arrived.astype(jnp.float32)
-    group_probs, group_cotangent, sent = lax.optimization_barrier(
-        (group_probs, group_cotangent, sent)
-    )
+    group_probs, group_columns, sent = lax.optimization_barrier((group_probs, group_columns, sent))
     weight_term = jnp.einsum(
-        "th,tak->ahk", group_probs, group_cotangent, preferred_element_type=jnp.float32
+        "th,tqk->qhk",
+        group_probs,
+        group_columns.reshape(group_size * tokens_dev, group_count, block),
+        preferred_element_type=jnp.float32,
     ) * (tokens_dev * n_ctx) ** (-0.5)
-    weight_grad = jnp.sum(lax.all_to_all(weight_term, "cg", 0, 0, tiled=True), 0)
+    weight_parts = lax.all_to_all(weight_term.astype(jnp.bfloat16), "cg", 0, 0, tiled=True)
+    weight_grad = jnp.sum(weight_parts.astype(jnp.float32), 0)
     key_total = pair_total[:, :kv_width]
     value_total = pair_total[:, kv_width:]
     query_grad = query_parts.transpose(1, 0, 2, 3).reshape(tokens_dev, -1).astype(jnp.bfloat16)

time: 310 us -> 287 us (0.926)
  local copies, waits for them, and re-layouts: 66.6 us -> 42.2 us
  waiting for transfers between devices: 84 us -> 94.9 us
  other arithmetic: 20.2 us -> 14.7 us
    reshape x4 -> x3, local copies, waits for them, and re-layouts: 20.7 us -> 4.33 us  [the longest x1 2.35 us: device_body(): group_weights = lax.all_to_all(jnp.broadcast_to(weight_rows, (group_count...]
    ppermute x1, waiting for transfers between devices: 14.9 us -> 0.01 us  [device_body(): partner_grad = lax.ppermute(out_grad, 'tp', [(0, 1), (1, 0)])]
    ppermute x16, waiting for transfers between devices: 60.9 us -> 75.2 us  [from_behind(): return lax.ppermute(block, axis, route)]
    all_to_all x4, waiting for transfers between devices: 8.24 us -> 19.7 us  [the longest x1 18.8 us: device_body(): lax.all_to_all(partial_grads.astype(jnp.bfloat16), 'cp', 0, 0, tiled=True)]
    ppermute x16, starting transfers between devices: 56.1 us -> 46.6 us  [from_behind(): return lax.ppermute(block, axis, route)]
    unnamed x51 -> x53, local copies, waits for them, and re-layouts: 29.7 us -> 21.1 us
    all_to_all x4, starting transfers between devices: 35 us -> 43 us  [the longest x1 26.4 us: device_body(): lax.all_to_all(weight_term.astype(jnp.bfloat16), 'cg', 0, 0, tiled=True)]
    slice x1 -> x0, local copies, waits for them, and re-layouts: 3.44 us -> none  [device_body(): unpacked[:, weight_count:]]
  transfers between devices with their start and end apart: 22 -> 22, of which waited for: 11 -> 16; matrix products, arithmetic and copies ran while one was open for 26% -> 22% of each run, Pallas kernels for 0% -> 0%
where the time goes in v1:
time: 287 us; the launch traced here: 285 us
  waiting for transfers between devices  94.9 us (33%)
  starting transfers between devices  92.1 us (32%)
  local copies, waits for them, and re-layouts  42.2 us (15%)
  matrix products  25.8 us (9%)
  other arithmetic  14.7 us (5%)
  between operations  14.5 us (5%)
    ppermute x16, waiting for transfers between devices, from_behind(): return lax.ppermute(block, axis, route)  75.2 us
    ppermute x16, starting transfers between devices, from_behind(): return lax.ppermute(block, axis, route)  46.6 us
    all_to_all x1, starting transfers between devices, device_body(): lax.all_to_all(weight_term.astype(jnp.bfloat16), 'cg', 0, 0, tiled=True)  26.4 us
    unnamed x53, local copies, waits for them, and re-layouts  21.1 us
    all_to_all x1, waiting for transfers between devices, device_body(): lax.all_to_all(partial_grads.astype(jnp.bfloat16), 'cp', 0, 0, tiled=True)  18.8 us
    and x8, other arithmetic, band_mask(): return earlier & within & (key_pos[None, :] >= 0)  6.89 us
    all_to_all x1, starting transfers between devices, device_body(): group_columns = lax.all_to_all(by_group, 'cp', 0, 0, tiled=True)  6.18 us
    all_to_all x1, starting transfers between devices, device_body(): lax.all_to_all(jnp.broadcast_to(weight_rows, (group_count,) + weight_rows...  5.89 us
  transfers between devices with their start and end apart: 22, of which 16 were waited for; matrix products, arithmetic and copies ran while one was open for 22% of the time, Pallas kernels for 0%

profile of v1, /device:TPU:8, one launch (start us, length us, event | category | flops | bytes accessed | tf_op | source)
XLA Modules:
  0.0 284.6 jit_solution(17431990171514628319)
XLA Ops:
  7.2 2.2 broadcast_in_dim.63
  9.4 5.9 %all-to-all-start.1 = ((bf16[8,84,1024]{2,1,0:T(8,128)(2,1)}), bf16[8,84,1024]{2,1,0:T(8,128)(2,1)S(1)}, u32[]{:S(2)}, u32[]{:S(2)}) async-start(bf16[8,84,1024]{2,1,0:T(8,128)(2,1)} %broadcast_in_dim.63), calls=%async_computation.1 | async-start | bytes 2883584 | tf_op jit(solution)/shard_map/all_to_all | solution.py:104
  16.3 3.4 %collective-permute-start = (bf16[128,1024]{0,1:T(8,128)(2,1)}, bf16[128,1024]{0,1:T(8,128)(2,1)}, u32[]{:S(2)}, u32[]{:S(2)}) collective-permute-start(bf16[128,1024]{0,1:T(8,128)(2,1)} %pad_maximum_fusion), channel_id=1, source_target_pairs={{0,16},{2,18},{4,20},{6,22},{8,24},{10,26},{12,28},{14,30},{16,32}... | collective-permute-start | bytes 786440 | tf_op jit(solution)/shard_map/ppermute | solution.py:19
  19.7 4.5 %collective-permute-start.1 = (bf16[128,1024]{0,1:T(8,128)(2,1)}, bf16[128,1024]{0,1:T(8,128)(2,1)}, u32[]{:S(2)}, u32[]{:S(2)}) collective-permute-start(bf16[128,1024]{0,1:T(8,128)(2,1)} %pad_maximum_fusion), channel_id=1, source_target_pairs={{0,14},{2,16},{4,18},{6,20},{8,22},{10,24},{12,26},{14,28},{16,30}... | collective-permute-start | bytes 786440 | tf_op jit(solution)/shard_map/ppermute | solution.py:19
  24.2 3.3 %collective-permute-start.2 = (bf16[128,1024]{0,1:T(8,128)(2,1)}, bf16[128,1024]{0,1:T(8,128)(2,1)}, u32[]{:S(2)}, u32[]{:S(2)}) collective-permute-start(bf16[128,1024]{0,1:T(8,128)(2,1)} %pad_maximum_fusion), channel_id=1, source_target_pairs={{0,12},{2,14},{4,16},{6,18},{8,20},{10,22},{12,24},{14,26},{16,28}... | collective-permute-start | bytes 786440 | tf_op jit(solution)/shard_map/ppermute | solution.py:19
  27.5 3.6 %collective-permute-start.3 = (bf16[128,1024]{0,1:T(8,128)(2,1)}, bf16[128,1024]{0,1:T(8,128)(2,1)}, u32[]{:S(2)}, u32[]{:S(2)}) collective-permute-start(bf16[128,1024]{0,1:T(8,128)(2,1)} %pad_maximum_fusion), channel_id=1, source_target_pairs={{0,10},{2,12},{4,14},{6,16},{8,18},{10,20},{12,22},{14,24},{16,26}... | collective-permute-start | bytes 786440 | tf_op jit(solution)/shard_map/ppermute | solution.py:19
  31.2 2.4 collective-permute-start.8
  38.2 5.8 %collective-permute-start.4 = (bf16[128,1024]{0,1:T(8,128)(2,1)}, bf16[128,1024]{0,1:T(8,128)(2,1)S(1)}, u32[]{:S(2)}, u32[]{:S(2)}) collective-permute-start(bf16[128,1024]{0,1:T(8,128)(2,1)} %pad_maximum_fusion), channel_id=1, source_target_pairs={{0,8},{2,10},{4,12},{6,14},{8,16},{10,18},{12,20},{14,22},{16,24},... | collective-permute-start | bytes 786440 | tf_op jit(solution)/shard_map/ppermute | solution.py:19
  45.7 3.0 %collective-permute-start.5 = (bf16[128,1024]{0,1:T(8,128)(2,1)}, bf16[128,1024]{0,1:T(8,128)(2,1)}, u32[]{:S(2)}, u32[]{:S(2)}) collective-permute-start(bf16[128,1024]{0,1:T(8,128)(2,1)} %pad_maximum_fusion), channel_id=1, source_target_pairs={{0,6},{2,8},{4,10},{6,12},{8,14},{10,16},{12,18},{14,20},{16,22},{... | collective-permute-start | bytes 786440 | tf_op jit(solution)/shard_map/ppermute | solution.py:19
  50.9 3.7 %collective-permute-start.6 = (bf16[128,1024]{0,1:T(8,128)(2,1)}, bf16[128,1024]{0,1:T(8,128)(2,1)}, u32[]{:S(2)}, u32[]{:S(2)}) collective-permute-start(bf16[128,1024]{0,1:T(8,128)(2,1)} %pad_maximum_fusion), channel_id=1, source_target_pairs={{0,4},{2,6},{4,8},{6,10},{8,12},{10,14},{12,16},{14,18},{16,20},{1... | collective-permute-start | bytes 786440 | tf_op jit(solution)/shard_map/ppermute | solution.py:19
  56.3 2.4 collective-permute-start.7
  58.7 2.2 copy.51
  63.9 6.2 %all-to-all-start = ((bf16[8,128,672]{1,2,0:T(8,128)(2,1)}), bf16[8,128,672]{1,2,0:T(8,128)(2,1)}, u32[]{:S(2)}, u32[]{:S(2)}) async-start(bf16[8,128,672]{1,2,0:T(8,128)(2,1)} %copy.53), calls=%async_computation | async-start | bytes 2752512 | tf_op jit(solution)/shard_map/all_to_all | solution.py:112
  71.8 7.0 %collective-permute-done.4 = bf16[128,1024]{0,1:T(8,128)(2,1)S(1)} collective-permute-done((bf16[128,1024]{0,1:T(8,128)(2,1)}, bf16[128,1024]{0,1:T(8,128)(2,1)S(1)}, u32[]{:S(2)}, u32[]{:S(2)}) %collective-permute-start.4) | collective-permute-done | bytes 262176 | tf_op jit(solution)/shard_map/ppermute | solution.py:19
  83.1 11.8 %collective-permute-done.6 = bf16[128,1024]{0,1:T(8,128)(2,1)} collective-permute-done((bf16[128,1024]{0,1:T(8,128)(2,1)}, bf16[128,1024]{0,1:T(8,128)(2,1)}, u32[]{:S(2)}, u32[]{:S(2)}) %collective-permute-start.6) | collective-permute-done | bytes 262176 | tf_op jit(solution)/shard_map/ppermute | solution.py:19
  103.2 2.3 reshape.105
  106.4 5.0 %convolution_convert_fusion.1 = bf16[8,128,1024]{2,1,0:T(8,128)(2,1)} fusion(bf16[8,128,672]{1,2,0:T(8,128)(2,1)} %all-to-all-done, bf16[672,1024,1]{1,0,2:T(8,128)(2,1)} %reshape.105), kind=kOutput, calls=%fused_computation.75 | convolution fusion | flops 1410334720 | bytes 4849664 | tf_op jit(solution)/shard_map/btk,kh->bth/dot_general | solution.py:113
  111.4 4.5 %all-to-all-start.2 = ((bf16[8,128,1024]{2,1,0:T(8,128)(2,1)}), bf16[8,128,1024]{2,1,0:T(8,128)(2,1)}, u32[]{:S(2)}, u32[]{:S(2)}) async-start(bf16[8,128,1024]{2,1,0:T(8,128)(2,1)} %convolution_convert_fusion.1), calls=%async_computation.2 | async-start | bytes 4194304 | tf_op jit(solution)/shard_map/all_to_all | solution.py:117
  116.1 7.3 %while.28 = (s32[]{:T(128)}, bf16[4,128,2,128]{1,3,2,0:T(8,128)(2,1)S(1)}, f32[4,2,128]{2,1,0:T(2,128)S(1)}, bf16[4,1152,128]{1,2,0:T(8,128)(2,1)S(1)}, bf16[4,1...) while((s32[]{:T(128)}, ...), condition=%wide.region_4.5_spmd.clone, body=%wide.region_1.0_spmd.clone.sunk | while | flops 153829120 | bytes 4571369 | solution.py:88
  124.2 18.8 %all-to-all-done.2 = bf16[8,128,1024]{2,1,0:T(8,128)(2,1)} async-done(((bf16[8,128,1024]{2,1,0:T(8,128)(2,1)}), bf16[8,128,1024]{2,1,0:T(8,128)(2,1)}, u32[]{:S(2)}, u32[]{:S(2)}) %all-to-all-start.2) | async-done | bytes 2097184 | tf_op jit(solution)/shard_map/all_to_all | solution.py:117
  145.3 19.9 %while.29 = (s32[]{:T(128)}, bf16[4,128,2,128]{1,3,2,0:T(8,128)(2,1)}, f32[4,1152,128]{2,1,0:T(8,128)}, f32[4,1152,128]{2,1,0:T(8,128)}, bf16[4,1152,128]{2,1,0:...) while((s32[]{:T(128)}, ...), condition=%wide.region_7.8_spmd.clone, body=%wide.region_6.7_spmd.clone.sunk | while | flops 380469248 | bytes 10175813 | solution.py:128
  165.2 2.2 bitcast_dynamic-update-slice_fusion.1
  173.9 4.4 %fusion.60 = bf16[8,1024,84]{1,2,0:T(8,128)(2,1)} fusion(bf16[1024,8,84]{0,2,1:T(8,128)(2,1)S(1)} %reshape.97, bf16[1024,1024]{0,1:T(8,128)(2,1)} %all-gather.2.cloned.1.call-done), kind=kOutput, calls=%fused_computation.76 | convolution fusion | flops 1410662400 | bytes 4849664 | tf_op jit(solution)/shard_map/th,tqk->qhk/dot_general | solution.py:147
  178.3 26.4 %all-to-all-start.3 = ((bf16[8,1024,84]{1,2,0:T(8,128)(2,1)}), bf16[8,1024,84]{1,2,0:T(8,128)(2,1)S(1)}, u32[]{:S(2)}, u32[]{:S(2)}) async-start(bf16[8,1024,84]{1,2,0:T(8,128)(2,1)} %fusion.60), calls=%async_computation.3 | async-start | bytes 2883584 | tf_op jit(solution)/shard_map/all_to_all | solution.py:153
  208.6 3.5 %collective-permute-start.12 = (bf16[128,1024]{1,0:T(8,128)(2,1)S(1)}, bf16[128,1024]{1,0:T(8,128)(2,1)S(1)}, u32[]{:S(2)}, u32[]{:S(2)}) collective-permute-start(bf16[128,1024]{1,0:T(8,128)(2,1)S(1)} %copy-done.10), channel_id=1, source_target_pairs={{8,0},{10,2},{12,4},{14,6},{16,8},{18,10},{20,12},{22,14},{24,16},... | collective-permute-start | bytes 786440 | tf_op jit(solution)/shard_map/ppermute | solution.py:19
  216.0 17.3 %collective-permute-done.10 = bf16[128,1024]{1,0:T(8,128)(2,1)S(1)} collective-permute-done((bf16[128,1024]{1,0:T(8,128)(2,1)}, bf16[128,1024]{1,0:T(8,128)(2,1)S(1)}, u32[]{:S(2)}, u32[]{:S(2)}) %collective-permute-start.10) | collective-permute-done | bytes 262176 | tf_op jit(solution)/shard_map/ppermute | solution.py:19
  235.2 5.3 %collective-permute-done.11 = bf16[128,1024]{1,0:T(8,128)(2,1)S(1)} collective-permute-done((bf16[128,1024]{1,0:T(8,128)(2,1)S(1)}, bf16[128,1024]{1,0:T(8,128)(2,1)S(1)}, u32[]{:S(2)}, u32[]{:S(2)}) %collective-permute-start.11) | collective-permute-done | bytes 262176 | tf_op jit(solution)/shard_map/ppermute | solution.py:19
  242.4 8.3 %collective-permute-done.12 = bf16[128,1024]{1,0:T(8,128)(2,1)S(1)} collective-permute-done((bf16[128,1024]{1,0:T(8,128)(2,1)S(1)}, bf16[128,1024]{1,0:T(8,128)(2,1)S(1)}, u32[]{:S(2)}, u32[]{:S(2)}) %collective-permute-start.12) | collective-permute-done | bytes 262176 | tf_op jit(solution)/shard_map/ppermute | solution.py:19
  254.4 2.6 collective-permute-done.13
  257.0 5.6 %collective-permute-done.14 = bf16[128,1024]{1,0:T(8,128)(2,1)} collective-permute-done((bf16[128,1024]{1,0:T(8,128)(2,1)S(1)}, bf16[128,1024]{1,0:T(8,128)(2,1)}, u32[]{:S(2)}, u32[]{:S(2)}) %collective-permute-start.14) | collective-permute-done | bytes 262176 | tf_op jit(solution)/shard_map/ppermute | solution.py:19
  262.7 5.6 %collective-permute-done.15 = bf16[128,1024]{1,0:T(8,128)(2,1)} collective-permute-done((bf16[128,1024]{1,0:T(8,128)(2,1)S(1)}, bf16[128,1024]{1,0:T(8,128)(2,1)}, u32[]{:S(2)}, u32[]{:S(2)}) %collective-permute-start.15) | collective-permute-done | bytes 262176 | tf_op jit(solution)/shard_map/ppermute | solution.py:19
  268.3 4.9 %collective-permute-done.16 = bf16[128,1024]{1,0:T(8,128)(2,1)S(1)} collective-permute-done((bf16[128,1024]{1,0:T(8,128)(2,1)S(1)}, bf16[128,1024]{1,0:T(8,128)(2,1)S(1)}, u32[]{:S(2)}, u32[]{:S(2)}) %collective-permute-start.16) | collective-permute-done | bytes 262176 | tf_op jit(solution)/shard_map/ppermute | solution.py:19
  (169 shorter events, 85.5 us)
Async XLA Ops:
  9.4 54.5 %all-to-all-start.1 = ((bf16[8,84,1024]{2,1,0:T(8,128)(2,1)}), bf16[8,84,1024]{2,1,0:T(8,128)(2,1)S(1)}, u32[]{:S(2)}, u32[]{:S(2)}) async-start(bf16[8,84,1024]{2,1,0:T(8,128)(2,1)} %broadcast_in_dim.63), calls=%async_computation.1 | async-start | bytes 2883584 | tf_op jit(solution)/shard_map/all_to_all | solution.py:104
  15.3 19.8 %copy-start.12 = (bf16[128,1024]{1,0:T(8,128)(2,1)S(1)}, bf16[128,1024]{1,0:T(8,128)(2,1)}, u32[]{:S(2)}) copy-start(bf16[128,1024]{1,0:T(8,128)(2,1)} %param.9) | copy-start | bytes 786436
  16.3 21.9 %collective-permute-start = (bf16[128,1024]{0,1:T(8,128)(2,1)}, bf16[128,1024]{0,1:T(8,128)(2,1)}, u32[]{:S(2)}, u32[]{:S(2)}) collective-permute-start(bf16[128,1024]{0,1:T(8,128)(2,1)} %pad_maximum_fusion), channel_id=1, source_target_pairs={{0,16},{2,18},{4,20},{6,22},{8,24},{10,26},{12,28},{14,30},{16,32}... | collective-permute-start | bytes 786440 | tf_op jit(solution)/shard_map/ppermute | solution.py:19
  19.7 26.0 %collective-permute-start.1 = (bf16[128,1024]{0,1:T(8,128)(2,1)}, bf16[128,1024]{0,1:T(8,128)(2,1)}, u32[]{:S(2)}, u32[]{:S(2)}) collective-permute-start(bf16[128,1024]{0,1:T(8,128)(2,1)} %pad_maximum_fusion), channel_id=1, source_target_pairs={{0,14},{2,16},{4,18},{6,20},{8,22},{10,24},{12,26},{14,28},{16,30}... | collective-permute-start | bytes 786440 | tf_op jit(solution)/shard_map/ppermute | solution.py:19
  24.2 26.7 %collective-permute-start.2 = (bf16[128,1024]{0,1:T(8,128)(2,1)}, bf16[128,1024]{0,1:T(8,128)(2,1)}, u32[]{:S(2)}, u32[]{:S(2)}) collective-permute-start(bf16[128,1024]{0,1:T(8,128)(2,1)} %pad_maximum_fusion), channel_id=1, source_target_pairs={{0,12},{2,14},{4,16},{6,18},{8,20},{10,22},{12,24},{14,26},{16,28}... | collective-permute-start | bytes 786440 | tf_op jit(solution)/shard_map/ppermute | solution.py:19
  27.5 42.5 %collective-permute-start.3 = (bf16[128,1024]{0,1:T(8,128)(2,1)}, bf16[128,1024]{0,1:T(8,128)(2,1)}, u32[]{:S(2)}, u32[]{:S(2)}) collective-permute-start(bf16[128,1024]{0,1:T(8,128)(2,1)} %pad_maximum_fusion), channel_id=1, source_target_pairs={{0,10},{2,12},{4,14},{6,16},{8,18},{10,20},{12,22},{14,24},{16,26}... | collective-permute-start | bytes 786440 | tf_op jit(solution)/shard_map/ppermute | solution.py:19
  31.2 25.1 %collective-permute-start.8 = (bf16[128,2688]{1,0:T(8,128)(2,1)}, bf16[128,2688]{1,0:T(8,128)(2,1)}, u32[]{:S(2)}, u32[]{:S(2)}) collective-permute-start(bf16[128,2688]{1,0:T(8,128)(2,1)} %param.12), channel_id=1, source_target_pairs={{0,1},{1,0},{2,3},{3,2},{4,5},{5,4},{6,7},{7,6},{8,9},{9,8},{10,11... | collective-permute-start | bytes 2064392 | tf_op jit(solution)/shard_map/ppermute | solution.py:94
  38.2 40.6 %collective-permute-start.4 = (bf16[128,1024]{0,1:T(8,128)(2,1)}, bf16[128,1024]{0,1:T(8,128)(2,1)S(1)}, u32[]{:S(2)}, u32[]{:S(2)}) collective-permute-start(bf16[128,1024]{0,1:T(8,128)(2,1)} %pad_maximum_fusion), channel_id=1, source_target_pairs={{0,8},{2,10},{4,12},{6,14},{8,16},{10,18},{12,20},{14,22},{16,24},... | collective-permute-start | bytes 786440 | tf_op jit(solution)/shard_map/ppermute | solution.py:19
  45.7 35.7 %collective-permute-start.5 = (bf16[128,1024]{0,1:T(8,128)(2,1)}, bf16[128,1024]{0,1:T(8,128)(2,1)}, u32[]{:S(2)}, u32[]{:S(2)}) collective-permute-start(bf16[128,1024]{0,1:T(8,128)(2,1)} %pad_maximum_fusion), channel_id=1, source_target_pairs={{0,6},{2,8},{4,10},{6,12},{8,14},{10,16},{12,18},{14,20},{16,22},{... | collective-permute-start | bytes 786440 | tf_op jit(solution)/shard_map/ppermute | solution.py:19
  50.9 44.0 %collective-permute-start.6 = (bf16[128,1024]{0,1:T(8,128)(2,1)}, bf16[128,1024]{0,1:T(8,128)(2,1)}, u32[]{:S(2)}, u32[]{:S(2)}) collective-permute-start(bf16[128,1024]{0,1:T(8,128)(2,1)} %pad_maximum_fusion), channel_id=1, source_target_pairs={{0,4},{2,6},{4,8},{6,10},{8,12},{10,14},{12,16},{14,18},{16,20},{1... | collective-permute-start | bytes 786440 | tf_op jit(solution)/shard_map/ppermute | solution.py:19
  56.3 41.9 %collective-permute-start.7 = (bf16[128,1024]{0,1:T(8,128)(2,1)}, bf16[128,1024]{0,1:T(8,128)(2,1)}, u32[]{:S(2)}, u32[]{:S(2)}) collective-permute-start(bf16[128,1024]{0,1:T(8,128)(2,1)} %pad_maximum_fusion), channel_id=1, source_target_pairs={{0,2},{2,4},{4,6},{6,8},{8,10},{10,12},{12,14},{14,16},{16,18},{18... | collective-permute-start | bytes 786440 | tf_op jit(solution)/shard_map/ppermute | solution.py:19
  63.9 7.9 %copy-start.1 = (bf16[8,84,1024]{2,1,0:T(8,128)(2,1)}, bf16[8,84,1024]{2,1,0:T(8,128)(2,1)S(1)}, u32[]{:S(2)}) copy-start(bf16[8,84,1024]{2,1,0:T(8,128)(2,1)S(1)} %all-to-all-done.1) | copy-start | bytes 4128772
  63.9 42.5 %all-to-all-start = ((bf16[8,128,672]{1,2,0:T(8,128)(2,1)}), bf16[8,128,672]{1,2,0:T(8,128)(2,1)}, u32[]{:S(2)}, u32[]{:S(2)}) async-start(bf16[8,128,672]{1,2,0:T(8,128)(2,1)} %copy.53), calls=%async_computation | async-start | bytes 2752512 | tf_op jit(solution)/shard_map/all_to_all | solution.py:112
  111.4 31.7 %all-to-all-start.2 = ((bf16[8,128,1024]{2,1,0:T(8,128)(2,1)}), bf16[8,128,1024]{2,1,0:T(8,128)(2,1)}, u32[]{:S(2)}, u32[]{:S(2)}) async-start(bf16[8,128,1024]{2,1,0:T(8,128)(2,1)} %convolution_convert_fusion.1), calls=%async_computation.2 | async-start | bytes 4194304 | tf_op jit(solution)/shard_map/all_to_all | solution.py:117
  115.8 55.4 %all-gather.2.cloned.1.call-start = ((), (), s32[]{:S(2)}) async-start(), calls=%async_computation.4 | async-start | bytes 2359296 | tf_op jit(solution)/shard_map/all_gather | solution.py:123
  124.2 21.0 %copy-start.6 = (bf16[4,128,2,128]{1,3,2,0:T(8,128)(2,1)S(1)}, bf16[4,128,2,128]{1,3,2,0:T(8,128)(2,1)}, u32[]{:S(2)}) copy-start(bf16[4,128,2,128]{1,3,2,0:T(8,128)(2,1)} %copy-done.5) | copy-start | bytes 786436
  178.3 28.3 %copy-start.11 = (bf16[128,1024]{1,0:T(8,128)(2,1)S(1)}, bf16[128,1024]{1,0:T(8,128)(2,1)}, u32[]{:S(2)}) copy-start(bf16[128,1024]{1,0:T(8,128)(2,1)} %get-tuple-element.271) | copy-start | bytes 786436
  178.3 30.3 %copy-start.10 = (bf16[128,1024]{1,0:T(8,128)(2,1)S(1)}, bf16[128,1024]{1,0:T(8,128)(2,1)}, u32[]{:S(2)}) copy-start(bf16[128,1024]{1,0:T(8,128)(2,1)} %get-tuple-element.270) | copy-start | bytes 786436
  178.3 33.8 %copy-start.9 = (bf16[128,1024]{1,0:T(8,128)(2,1)S(1)}, bf16[128,1024]{1,0:T(8,128)(2,1)}, u32[]{:S(2)}) copy-start(bf16[128,1024]{1,0:T(8,128)(2,1)} %get-tuple-element.269) | copy-start | bytes 786436
  178.3 35.7 %copy-start.8 = (bf16[128,1024]{1,0:T(8,128)(2,1)S(1)}, bf16[128,1024]{1,0:T(8,128)(2,1)}, u32[]{:S(2)}) copy-start(bf16[128,1024]{1,0:T(8,128)(2,1)} %get-tuple-element.268) | copy-start | bytes 786436
  178.3 55.0 %copy-start.7 = (bf16[128,1024]{1,0:T(8,128)(2,1)S(1)}, bf16[128,1024]{1,0:T(8,128)(2,1)}, u32[]{:S(2)}) copy-start(bf16[128,1024]{1,0:T(8,128)(2,1)} %get-tuple-element.267) | copy-start | bytes 786436
  178.3 98.4 %all-to-all-start.3 = ((bf16[8,1024,84]{1,2,0:T(8,128)(2,1)}), bf16[8,1024,84]{1,2,0:T(8,128)(2,1)S(1)}, u32[]{:S(2)}, u32[]{:S(2)}) async-start(bf16[8,1024,84]{1,2,0:T(8,128)(2,1)} %fusion.60), calls=%async_computation.3 | async-start | bytes 2883584 | tf_op jit(solution)/shard_map/all_to_all | solution.py:153
  204.8 28.5 %collective-permute-start.10 = (bf16[128,1024]{1,0:T(8,128)(2,1)}, bf16[128,1024]{1,0:T(8,128)(2,1)S(1)}, u32[]{:S(2)}, u32[]{:S(2)}) collective-permute-start(bf16[128,1024]{1,0:T(8,128)(2,1)} %get-tuple-element.272), channel_id=1, source_target_pairs={{4,0},{6,2},{8,4},{10,6},{12,8},{14,10},{16,12},{18,14},{20,16},{2... | collective-permute-start | bytes 786440 | tf_op jit(solution)/shard_map/ppermute | solution.py:19
  206.7 33.8 %collective-permute-start.11 = (bf16[128,1024]{1,0:T(8,128)(2,1)S(1)}, bf16[128,1024]{1,0:T(8,128)(2,1)S(1)}, u32[]{:S(2)}, u32[]{:S(2)}) collective-permute-start(bf16[128,1024]{1,0:T(8,128)(2,1)S(1)} %copy-done.11), channel_id=1, source_target_pairs={{6,0},{8,2},{10,4},{12,6},{14,8},{16,10},{18,12},{20,14},{22,16},{... | collective-permute-start | bytes 786440 | tf_op jit(solution)/shard_map/ppermute | solution.py:19
  208.6 42.0 %collective-permute-start.12 = (bf16[128,1024]{1,0:T(8,128)(2,1)S(1)}, bf16[128,1024]{1,0:T(8,128)(2,1)S(1)}, u32[]{:S(2)}, u32[]{:S(2)}) collective-permute-start(bf16[128,1024]{1,0:T(8,128)(2,1)S(1)} %copy-done.10), channel_id=1, source_target_pairs={{8,0},{10,2},{12,4},{14,6},{16,8},{18,10},{20,12},{22,14},{24,16},... | collective-permute-start | bytes 786440 | tf_op jit(solution)/shard_map/ppermute | solution.py:19
  212.1 44.9 %collective-permute-start.13 = (bf16[128,1024]{1,0:T(8,128)(2,1)S(1)}, bf16[128,1024]{1,0:T(8,128)(2,1)}, u32[]{:S(2)}, u32[]{:S(2)}) collective-permute-start(bf16[128,1024]{1,0:T(8,128)(2,1)S(1)} %copy-done.9), channel_id=1, source_target_pairs={{10,0},{12,2},{14,4},{16,6},{18,8},{20,10},{22,12},{24,14},{26,16}... | collective-permute-start | bytes 786440 | tf_op jit(solution)/shard_map/ppermute | solution.py:19
  214.0 48.6 %collective-permute-start.14 = (bf16[128,1024]{1,0:T(8,128)(2,1)S(1)}, bf16[128,1024]{1,0:T(8,128)(2,1)}, u32[]{:S(2)}, u32[]{:S(2)}) collective-permute-start(bf16[128,1024]{1,0:T(8,128)(2,1)S(1)} %copy-done.8), channel_id=1, source_target_pairs={{12,0},{14,2},{16,4},{18,6},{20,8},{22,10},{24,12},{26,14},{28,16}... | collective-permute-start | bytes 786440 | tf_op jit(solution)/shard_map/ppermute | solution.py:19
  233.3 19.3 %copy-start.15 = (bf16[128,1024]{1,0:T(8,128)(2,1)}, bf16[128,1024]{1,0:T(8,128)(2,1)S(1)}, u32[]{:S(2)}) copy-start(bf16[128,1024]{1,0:T(8,128)(2,1)S(1)} %collective-permute-done.10) | copy-start | bytes 786436
  233.3 35.0 %collective-permute-start.15 = (bf16[128,1024]{1,0:T(8,128)(2,1)S(1)}, bf16[128,1024]{1,0:T(8,128)(2,1)}, u32[]{:S(2)}, u32[]{:S(2)}) collective-permute-start(bf16[128,1024]{1,0:T(8,128)(2,1)S(1)} %copy-done.7), channel_id=1, source_target_pairs={{14,0},{16,2},{18,4},{20,6},{22,8},{24,10},{26,12},{28,14},{30,16}... | collective-permute-start | bytes 786440 | tf_op jit(solution)/shard_map/ppermute | solution.py:19
  240.5 12.1 %copy-start.16 = (bf16[128,1024]{1,0:T(8,128)(2,1)}, bf16[128,1024]{1,0:T(8,128)(2,1)S(1)}, u32[]{:S(2)}) copy-start(bf16[128,1024]{1,0:T(8,128)(2,1)S(1)} %collective-permute-done.11) | copy-start | bytes 786436
  240.5 32.7 %collective-permute-start.16 = (bf16[128,1024]{1,0:T(8,128)(2,1)S(1)}, bf16[128,1024]{1,0:T(8,128)(2,1)S(1)}, u32[]{:S(2)}, u32[]{:S(2)}) collective-permute-start(bf16[128,1024]{1,0:T(8,128)(2,1)S(1)} %get-tuple-element.266), channel_id=1, source_target_pairs={{16,0},{18,2},{20,4},{22,6},{24,8},{26,10},{28,12},{30,14},{32,16}... | collective-permute-start | bytes 786440 | tf_op jit(solution)/shard_map/ppermute | solution.py:19
  250.7 23.5 %collective-permute-start.9 = (bf16[128,1024]{1,0:T(8,128)(2,1)S(1)}, bf16[128,1024]{1,0:T(8,128)(2,1)S(1)}, u32[]{:S(2)}, u32[]{:S(2)}) collective-permute-start(bf16[128,1024]{1,0:T(8,128)(2,1)S(1)} %get-tuple-element.265), channel_id=1, source_target_pairs={{2,0},{4,2},{6,4},{8,6},{10,8},{12,10},{14,12},{16,14},{18,16},{20... | collective-permute-start | bytes 786440 | tf_op jit(solution)/shard_map/ppermute | solution.py:19
  (17 other events, 45.4 us)
Sparse Core Ops, SparseCore 0:
  124.3 42.6 all-gather.1

commit v2 on v1

--- a/solution.py
+++ b/solution.py
@@ -102,24 +102,25 @@
     block = cotangent.shape[1] // n_ctx
     weight_rows = out_weight.T
     group_weights = lax.all_to_all(
-        jnp.broadcast_to(weight_rows, (group_count,) + weight_rows.shape), "cg", 0, 0, tiled=True
-    ).reshape(group_count * block, -1)
-    by_group = (
-        cotangent.reshape(tokens_dev, group_count, group_size, block)
-        .transpose(2, 0, 1, 3)
-        .reshape(group_size, tokens_dev, group_count * block)
-    )
-    group_columns = lax.all_to_all(by_group, "cp", 0, 0, tiled=True)
+        jnp.broadcast_to(weight_rows, (group_size,) + weight_rows.shape), "cp", 0, 0, tiled=True
+    ).reshape(group_size * block, -1)
+    by_group = cotangent.reshape(tokens_dev, group_count, group_size * block).transpose(1, 0, 2)
+    group_columns = lax.all_to_all(by_group, "cg", 0, 0, tiled=True)
     partial_grads = jnp.einsum(
         "btk,kh->bth", group_columns, group_weights, preferred_element_type=jnp.float32
     )
     grad_sum = jnp.sum(
-        lax.all_to_all(partial_grads.astype(jnp.bfloat16), "cp", 0, 0, tiled=True).astype(
+        lax.all_to_all(partial_grads.astype(jnp.bfloat16), "cg", 0, 0, tiled=True).astype(
             jnp.float32
         ),
         0,
     )
+    by_position = cotangent.reshape(tokens_dev, group_count, group_size, block).transpose(2, 0, 1, 3)
+    by_position, grad_sum = lax.optimization_barrier((by_position, grad_sum))
     attention_gradient = grad_sum.astype(jnp.bfloat16)
+    wg_columns = lax.all_to_all(by_position, "cp", 0, 0, tiled=True).reshape(
+        group_size * tokens_dev, group_count, block
+    )
     group_probs = lax.all_gather(attention_probs, "cp", axis=0, tiled=True)
     grad_rows = attention_gradient.reshape(tokens_dev, kv_local, group_width, HEAD_SIZE)
     row_deltas = jnp.sum(grad_rows.astype(jnp.float32) * attn_rows.astype(jnp.float32), axis=-1)
@@ -143,12 +144,9 @@
     for offset in range(1, reach_count + 1):
         arrived = from_behind(sent[offset - 1], ("cg", "cp"), -offset)
         pair_total = pair_total + arrived.astype(jnp.float32)
-    group_probs, group_columns, sent = lax.optimization_barrier((group_probs, group_columns, sent))
+    group_probs, wg_columns, sent = lax.optimization_barrier((group_probs, wg_columns, sent))
     weight_term = jnp.einsum(
-        "th,tqk->qhk",
-        group_probs,
-        group_columns.reshape(group_size * tokens_dev, group_count, block),
-        preferred_element_type=jnp.float32,
+        "th,tak->ahk", group_probs, wg_columns, preferred_element_type=jnp.float32
     ) * (tokens_dev * n_ctx) ** (-0.5)
     weight_parts = lax.all_to_all(weight_term.astype(jnp.bfloat16), "cg", 0, 0, tiled=True)
     weight_grad = jnp.sum(weight_parts.astype(jnp.float32), 0)

time: 287 us -> 291 us (1.014)
  waiting for transfers between devices: 94.9 us -> 79.3 us
  starting transfers between devices: 92.1 us -> 104 us
  other arithmetic: 14.7 us -> 19.8 us
    all_to_all x3 -> x4, starting transfers between devices: 16.6 us -> 49.5 us  [the longest x1 22.3 us: device_body(): lax.all_to_all(by_position, 'cp', 0, 0, tiled=True)]
    all_to_all x1, starting transfers between devices: 26.4 us -> 6.04 us  [device_body(): lax.all_to_all(weight_term.astype(jnp.bfloat16), 'cg', 0, 0, tiled=True)]
    ppermute x16, waiting for transfers between devices: 75.2 us -> 59.3 us  [from_behind(): return lax.ppermute(block, axis, route)]
    transpose x1 -> x2, other arithmetic: 0.25 us -> 4.59 us  [the longest x1 3.3 us: device_body(): cotangent.reshape(tokens_dev, group_count, group_size, block)]
    unnamed x53 -> x43, local copies, waits for them, and re-layouts: 21.1 us -> 20.6 us
    all_to_all x3 -> x4, waiting for transfers between devices: 19.7 us -> 19.9 us  [the longest x1 13.4 us: device_body(): lax.all_to_all(by_position, 'cp', 0, 0, tiled=True)]
  transfers between devices with their start and end apart: 22 -> 23, of which waited for: 16 -> 14; matrix products, arithmetic and copies ran while one was open for 22% -> 25% of each run, Pallas kernels for 0% -> 0%
where the time goes in v2:
time: 291 us; the launch traced here: 288 us
  starting transfers between devices  104 us (36%)
  waiting for transfers between devices  79.3 us (27%)
  local copies, waits for them, and re-layouts  42.2 us (15%)
  matrix products  28.6 us (10%)
  other arithmetic  19.8 us (7%)
  between operations  14.4 us (5%)
    ppermute x16, waiting for transfers between devices, from_behind(): return lax.ppermute(block, axis, route)  59.3 us
    ppermute x16, starting transfers between devices, from_behind(): return lax.ppermute(block, axis, route)  45.5 us
    all_to_all x1, starting transfers between devices, device_body(): lax.all_to_all(by_position, 'cp', 0, 0, tiled=True)  22.3 us
    unnamed x43, local copies, waits for them, and re-layouts  20.6 us
    all_to_all x1, waiting for transfers between devices, device_body(): lax.all_to_all(by_position, 'cp', 0, 0, tiled=True)  13.4 us
    all_to_all x1, starting transfers between devices, device_body(): lax.all_to_all(partial_grads.astype(jnp.bfloat16), 'cg', 0, 0, tiled=True)  13.3 us
    all_to_all x1, starting transfers between devices, device_body(): group_columns = lax.all_to_all(by_group, 'cg', 0, 0, tiled=True)  8.42 us
    and x8, other arithmetic, band_mask(): return earlier & within & (key_pos[None, :] >= 0)  6.78 us
  transfers between devices with their start and end apart: 23, of which 14 were waited for; matrix products, arithmetic and copies ran while one was open for 25% of the time, Pallas kernels for 0%

profile of v2, /device:TPU:8, one launch (start us, length us, event | category | flops | bytes accessed | tf_op | source)
XLA Modules:
  0.0 288.3 jit_solution(9915937436138776180)
XLA Ops:
  9.5 5.4 %all-to-all-start.1 = ((bf16[8,84,1024]{2,1,0:T(8,128)(2,1)}), bf16[8,84,1024]{2,1,0:T(8,128)(2,1)S(1)}, u32[]{:S(2)}, u32[]{:S(2)}) async-start(bf16[8,84,1024]{2,1,0:T(8,128)(2,1)} %broadcast_in_dim.63), calls=%async_computation.1 | async-start | bytes 2883584 | tf_op jit(solution)/shard_map/all_to_all | solution.py:104
  15.9 3.3 %collective-permute-start = (bf16[128,1024]{0,1:T(8,128)(2,1)}, bf16[128,1024]{0,1:T(8,128)(2,1)}, u32[]{:S(2)}, u32[]{:S(2)}) collective-permute-start(bf16[128,1024]{0,1:T(8,128)(2,1)} %pad_maximum_fusion), channel_id=1, source_target_pairs={{0,16},{2,18},{4,20},{6,22},{8,24},{10,26},{12,28},{14,30},{16,32}... | collective-permute-start | bytes 786440 | tf_op jit(solution)/shard_map/ppermute | solution.py:19
  19.2 4.6 %collective-permute-start.1 = (bf16[128,1024]{0,1:T(8,128)(2,1)}, bf16[128,1024]{0,1:T(8,128)(2,1)}, u32[]{:S(2)}, u32[]{:S(2)}) collective-permute-start(bf16[128,1024]{0,1:T(8,128)(2,1)} %pad_maximum_fusion), channel_id=1, source_target_pairs={{0,14},{2,16},{4,18},{6,20},{8,22},{10,24},{12,26},{14,28},{16,30}... | collective-permute-start | bytes 786440 | tf_op jit(solution)/shard_map/ppermute | solution.py:19
  23.8 3.8 %collective-permute-start.2 = (bf16[128,1024]{0,1:T(8,128)(2,1)}, bf16[128,1024]{0,1:T(8,128)(2,1)S(1)}, u32[]{:S(2)}, u32[]{:S(2)}) collective-permute-start(bf16[128,1024]{0,1:T(8,128)(2,1)} %pad_maximum_fusion), channel_id=1, source_target_pairs={{0,12},{2,14},{4,16},{6,18},{8,20},{10,22},{12,24},{14,26},{16,28}... | collective-permute-start | bytes 786440 | tf_op jit(solution)/shard_map/ppermute | solution.py:19
  27.6 3.3 %collective-permute-start.3 = (bf16[128,1024]{0,1:T(8,128)(2,1)}, bf16[128,1024]{0,1:T(8,128)(2,1)}, u32[]{:S(2)}, u32[]{:S(2)}) collective-permute-start(bf16[128,1024]{0,1:T(8,128)(2,1)} %pad_maximum_fusion), channel_id=1, source_target_pairs={{0,10},{2,12},{4,14},{6,16},{8,18},{10,20},{12,22},{14,24},{16,26}... | collective-permute-start | bytes 786440 | tf_op jit(solution)/shard_map/ppermute | solution.py:19
  30.8 2.7 collective-permute-start.8
  36.5 4.6 %collective-permute-start.4 = (bf16[128,1024]{0,1:T(8,128)(2,1)}, bf16[128,1024]{0,1:T(8,128)(2,1)}, u32[]{:S(2)}, u32[]{:S(2)}) collective-permute-start(bf16[128,1024]{0,1:T(8,128)(2,1)} %pad_maximum_fusion), channel_id=1, source_target_pairs={{0,8},{2,10},{4,12},{6,14},{8,16},{10,18},{12,20},{14,22},{16,24},... | collective-permute-start | bytes 786440 | tf_op jit(solution)/shard_map/ppermute | solution.py:19
  46.4 3.2 %collective-permute-start.6 = (bf16[128,1024]{0,1:T(8,128)(2,1)}, bf16[128,1024]{0,1:T(8,128)(2,1)}, u32[]{:S(2)}, u32[]{:S(2)}) collective-permute-start(bf16[128,1024]{0,1:T(8,128)(2,1)} %pad_maximum_fusion), channel_id=1, source_target_pairs={{0,4},{2,6},{4,8},{6,10},{8,12},{10,14},{12,16},{14,18},{16,20},{1... | collective-permute-start | bytes 786440 | tf_op jit(solution)/shard_map/ppermute | solution.py:19
  50.4 3.5 %collective-permute-start.7 = (bf16[128,1024]{0,1:T(8,128)(2,1)}, bf16[128,1024]{0,1:T(8,128)(2,1)}, u32[]{:S(2)}, u32[]{:S(2)}) collective-permute-start(bf16[128,1024]{0,1:T(8,128)(2,1)} %pad_maximum_fusion), channel_id=1, source_target_pairs={{0,2},{2,4},{4,6},{6,8},{8,10},{10,12},{12,14},{14,16},{16,18},{18... | collective-permute-start | bytes 786440 | tf_op jit(solution)/shard_map/ppermute | solution.py:19
  56.6 8.4 %all-to-all-start = ((bf16[8,128,672]{1,2,0:T(8,128)(2,1)}), bf16[8,128,672]{1,2,0:T(8,128)(2,1)}, u32[]{:S(2)}, u32[]{:S(2)}) async-start(bf16[8,128,672]{1,2,0:T(8,128)(2,1)} %fusion.65), calls=%async_computation | async-start | bytes 2752512 | tf_op jit(solution)/shard_map/all_to_all | solution.py:108
  73.1 6.0 %collective-permute-done.6 = bf16[128,1024]{0,1:T(8,128)(2,1)} collective-permute-done((bf16[128,1024]{0,1:T(8,128)(2,1)}, bf16[128,1024]{0,1:T(8,128)(2,1)}, u32[]{:S(2)}, u32[]{:S(2)}) %collective-permute-start.6) | collective-permute-done | bytes 262176 | tf_op jit(solution)/shard_map/ppermute | solution.py:19
  83.6 2.9 fusion.76
  90.5 5.0 %convolution_convert_fusion.1 = bf16[8,128,1024]{2,1,0:T(8,128)(2,1)} fusion(bf16[8,128,672]{1,2,0:T(8,128)(2,1)} %all-to-all-done, bf16[672,1024,1]{1,0,2:T(8,128)(2,1)} %reshape.106), kind=kOutput, calls=%fused_computation.76 | convolution fusion | flops 1410334720 | bytes 4849664 | tf_op jit(solution)/shard_map/btk,kh->bth/dot_general | solution.py:109
  95.5 13.3 %all-to-all-start.2 = ((bf16[8,128,1024]{2,1,0:T(8,128)(2,1)}), bf16[8,128,1024]{2,1,0:T(8,128)(2,1)}, u32[]{:S(2)}, u32[]{:S(2)}) async-start(bf16[8,128,1024]{2,1,0:T(8,128)(2,1)} %convolution_convert_fusion.1), calls=%async_computation.2 | async-start | bytes 4194304 | tf_op jit(solution)/shard_map/all_to_all | solution.py:113
  108.8 9.7 %while.28 = (s32[]{:T(128)}, bf16[4,128,2,128]{1,3,2,0:T(8,128)(2,1)}, f32[4,2,128]{2,1,0:T(2,128)S(1)}, bf16[4,1152,128]{1,2,0:T(8,128)(2,1)S(1)}, bf16[4,1152,...) while((s32[]{:T(128)}, ...), condition=%wide.region_4.5_spmd.clone, body=%wide.region_1.0_spmd.clone.sunk | while | flops 153829120 | bytes 4571369 | solution.py:88
  119.5 3.3 %fusion.63 = bf16[8,128,8,84]{1,3,0,2:T(8,128)(2,1)} fusion(bf16[128,4,8,84]{0,3,2,1:T(8,128)(2,1)} %concatenate.34, bf16[128,4,8,84]{0,3,2,1:T(8,128)(2,1)} %concatenate.33, pred[]{:T(512)S(6)} %eq.3), kind=kLoop, calls=%fused_computation.79 | loop fusion | flops 2064384 | bytes 2752513 | tf_op jit(solution)/shard_map/transpose | solution.py:118
  122.8 6.5 %all-to-all-done.2 = bf16[8,128,1024]{2,1,0:T(8,128)(2,1)} async-done(((bf16[8,128,1024]{2,1,0:T(8,128)(2,1)}), bf16[8,128,1024]{2,1,0:T(8,128)(2,1)}, u32[]{:S(2)}, u32[]{:S(2)}) %all-to-all-start.2) | async-done | bytes 2097184 | tf_op jit(solution)/shard_map/all_to_all | solution.py:113
  132.5 19.9 %while.29 = (s32[]{:T(128)}, bf16[4,128,2,128]{1,3,2,0:T(8,128)(2,1)}, f32[4,1152,128]{2,1,0:T(8,128)}, f32[4,1152,128]{2,1,0:T(8,128)}, bf16[4,1152,128]{2,1,0:...) while((s32[]{:T(128)}, ...), condition=%wide.region_7.8_spmd.clone, body=%wide.region_6.7_spmd.clone.sunk | while | flops 380469248 | bytes 10175813 | solution.py:129
  152.4 3.4 %copy.62 = bf16[8,128,8,84]{1,2,3,0:T(8,128)(2,1)} copy(bf16[8,128,8,84]{1,3,0,2:T(8,128)(2,1)} %fusion.63) | data formatting | bytes 2752512 | tf_op jit(solution)/shard_map/optimization_barrier | solution.py:119
  155.8 22.3 %all-to-all-start.3 = ((bf16[8,128,8,84]{1,2,3,0:T(8,128)(2,1)}), bf16[8,128,8,84]{1,2,3,0:T(8,128)(2,1)S(1)}, u32[]{:S(2)}, u32[]{:S(2)}) async-start(bf16[8,128,8,84]{1,2,3,0:T(8,128)(2,1)} %copy.62), calls=%async_computation.3 | async-start | bytes 2752512 | tf_op jit(solution)/shard_map/all_to_all | solution.py:121
  184.1 13.4 %all-to-all-done.3 = bf16[8,128,8,84]{1,2,3,0:T(8,128)(2,1)S(1)} async-done(((bf16[8,128,8,84]{1,2,3,0:T(8,128)(2,1)}), bf16[8,128,8,84]{1,2,3,0:T(8,128)(2,1)S(1)}, u32[]{:S(2)}, u32[]{:S(2)}) %all-to-all-start.3) | async-done | bytes 1376288 | tf_op jit(solution)/shard_map/all_to_all | solution.py:121
  197.7 4.8 %fusion.60 = bf16[8,1024,84]{1,2,0:T(8,128)(2,1)} fusion(bf16[1024,1024]{0,1:T(8,128)(2,1)} %all-gather.2.cloned.1.call-done, bf16[1024,8,84]{0,1,2:T(8,128)(2,1)S(1)} %copy_bitcast_fusion), kind=kOutput, calls=%fused_computation.77 | convolution fusion | flops 1410662400 | bytes 4849664 | tf_op jit(solution)/shard_map/th,tak->ahk/dot_general | solution.py:148
  202.6 6.0 %all-to-all-start.4 = ((bf16[8,1024,84]{1,2,0:T(8,128)(2,1)}), bf16[8,1024,84]{1,2,0:T(8,128)(2,1)S(1)}, u32[]{:S(2)}, u32[]{:S(2)}) async-start(bf16[8,1024,84]{1,2,0:T(8,128)(2,1)} %fusion.60), calls=%async_computation.4 | async-start | bytes 2883584 | tf_op jit(solution)/shard_map/all_to_all | solution.py:151
  208.6 2.6 collective-permute-start.10
  213.5 3.1 %collective-permute-start.12 = (bf16[128,1024]{1,0:T(8,128)(2,1)S(1)}, bf16[128,1024]{1,0:T(8,128)(2,1)S(1)}, u32[]{:S(2)}, u32[]{:S(2)}) collective-permute-start(bf16[128,1024]{1,0:T(8,128)(2,1)S(1)} %copy-done.5), channel_id=1, source_target_pairs={{8,0},{10,2},{12,4},{14,6},{16,8},{18,10},{20,12},{22,14},{24,16},... | collective-permute-start | bytes 786440 | tf_op jit(solution)/shard_map/ppermute | solution.py:19
  220.4 16.5 %collective-permute-done.10 = bf16[128,1024]{1,0:T(8,128)(2,1)S(1)} collective-permute-done((bf16[128,1024]{1,0:T(8,128)(2,1)S(1)}, bf16[128,1024]{1,0:T(8,128)(2,1)S(1)}, u32[]{:S(2)}, u32[]{:S(2)}) %collective-permute-start.10) | collective-permute-done | bytes 262176 | tf_op jit(solution)/shard_map/ppermute | solution.py:19
  238.8 4.3 %collective-permute-done.11 = bf16[128,1024]{1,0:T(8,128)(2,1)S(1)} collective-permute-done((bf16[128,1024]{1,0:T(8,128)(2,1)S(1)}, bf16[128,1024]{1,0:T(8,128)(2,1)S(1)}, u32[]{:S(2)}, u32[]{:S(2)}) %collective-permute-start.11) | collective-permute-done | bytes 262176 | tf_op jit(solution)/shard_map/ppermute | solution.py:19
  245.1 8.3 %collective-permute-done.12 = bf16[128,1024]{1,0:T(8,128)(2,1)S(1)} collective-permute-done((bf16[128,1024]{1,0:T(8,128)(2,1)S(1)}, bf16[128,1024]{1,0:T(8,128)(2,1)S(1)}, u32[]{:S(2)}, u32[]{:S(2)}) %collective-permute-start.12) | collective-permute-done | bytes 262176 | tf_op jit(solution)/shard_map/ppermute | solution.py:19
  257.1 2.7 collective-permute-done.13
  259.8 5.6 %collective-permute-done.14 = bf16[128,1024]{1,0:T(8,128)(2,1)} collective-permute-done((bf16[128,1024]{1,0:T(8,128)(2,1)S(1)}, bf16[128,1024]{1,0:T(8,128)(2,1)}, u32[]{:S(2)}, u32[]{:S(2)}) %collective-permute-start.14) | collective-permute-done | bytes 262176 | tf_op jit(solution)/shard_map/ppermute | solution.py:19
  265.4 5.6 %collective-permute-done.15 = bf16[128,1024]{1,0:T(8,128)(2,1)S(1)} collective-permute-done((bf16[128,1024]{1,0:T(8,128)(2,1)S(1)}, bf16[128,1024]{1,0:T(8,128)(2,1)S(1)}, u32[]{:S(2)}, u32[]{:S(2)}) %collective-permute-start.15) | collective-permute-done | bytes 262176 | tf_op jit(solution)/shard_map/ppermute | solution.py:19
  271.0 6.6 %collective-permute-done.16 = bf16[128,1024]{1,0:T(8,128)(2,1)S(1)} collective-permute-done((bf16[128,1024]{1,0:T(8,128)(2,1)S(1)}, bf16[128,1024]{1,0:T(8,128)(2,1)S(1)}, u32[]{:S(2)}, u32[]{:S(2)}) %collective-permute-start.16) | collective-permute-done | bytes 262176 | tf_op jit(solution)/shard_map/ppermute | solution.py:19
  (160 shorter events, 88.7 us)
Async XLA Ops:
  9.5 47.1 %all-to-all-start.1 = ((bf16[8,84,1024]{2,1,0:T(8,128)(2,1)}), bf16[8,84,1024]{2,1,0:T(8,128)(2,1)S(1)}, u32[]{:S(2)}, u32[]{:S(2)}) async-start(bf16[8,84,1024]{2,1,0:T(8,128)(2,1)} %broadcast_in_dim.63), calls=%async_computation.1 | async-start | bytes 2883584 | tf_op jit(solution)/shard_map/all_to_all | solution.py:104
  14.9 20.1 %copy-start.8 = (bf16[128,1024]{1,0:T(8,128)(2,1)S(1)}, bf16[128,1024]{1,0:T(8,128)(2,1)}, u32[]{:S(2)}) copy-start(bf16[128,1024]{1,0:T(8,128)(2,1)} %param.9) | copy-start | bytes 786436
  15.9 20.6 %collective-permute-start = (bf16[128,1024]{0,1:T(8,128)(2,1)}, bf16[128,1024]{0,1:T(8,128)(2,1)}, u32[]{:S(2)}, u32[]{:S(2)}) collective-permute-start(bf16[128,1024]{0,1:T(8,128)(2,1)} %pad_maximum_fusion), channel_id=1, source_target_pairs={{0,16},{2,18},{4,20},{6,22},{8,24},{10,26},{12,28},{14,30},{16,32}... | collective-permute-start | bytes 786440 | tf_op jit(solution)/shard_map/ppermute | solution.py:19
  19.2 23.6 %collective-permute-start.1 = (bf16[128,1024]{0,1:T(8,128)(2,1)}, bf16[128,1024]{0,1:T(8,128)(2,1)}, u32[]{:S(2)}, u32[]{:S(2)}) collective-permute-start(bf16[128,1024]{0,1:T(8,128)(2,1)} %pad_maximum_fusion), channel_id=1, source_target_pairs={{0,14},{2,16},{4,18},{6,20},{8,22},{10,24},{12,26},{14,28},{16,30}... | collective-permute-start | bytes 786440 | tf_op jit(solution)/shard_map/ppermute | solution.py:19
  23.8 22.6 %collective-permute-start.2 = (bf16[128,1024]{0,1:T(8,128)(2,1)}, bf16[128,1024]{0,1:T(8,128)(2,1)S(1)}, u32[]{:S(2)}, u32[]{:S(2)}) collective-permute-start(bf16[128,1024]{0,1:T(8,128)(2,1)} %pad_maximum_fusion), channel_id=1, source_target_pairs={{0,12},{2,14},{4,16},{6,18},{8,20},{10,22},{12,24},{14,26},{16,28}... | collective-permute-start | bytes 786440 | tf_op jit(solution)/shard_map/ppermute | solution.py:19
  27.6 37.4 %collective-permute-start.3 = (bf16[128,1024]{0,1:T(8,128)(2,1)}, bf16[128,1024]{0,1:T(8,128)(2,1)}, u32[]{:S(2)}, u32[]{:S(2)}) collective-permute-start(bf16[128,1024]{0,1:T(8,128)(2,1)} %pad_maximum_fusion), channel_id=1, source_target_pairs={{0,10},{2,12},{4,14},{6,16},{8,18},{10,20},{12,22},{14,24},{16,26}... | collective-permute-start | bytes 786440 | tf_op jit(solution)/shard_map/ppermute | solution.py:19
  30.8 19.5 %collective-permute-start.8 = (bf16[128,2688]{1,0:T(8,128)(2,1)}, bf16[128,2688]{1,0:T(8,128)(2,1)}, u32[]{:S(2)}, u32[]{:S(2)}) collective-permute-start(bf16[128,2688]{1,0:T(8,128)(2,1)} %param.12), channel_id=1, source_target_pairs={{0,1},{1,0},{2,3},{3,2},{4,5},{5,4},{6,7},{7,6},{8,9},{9,8},{10,11... | collective-permute-start | bytes 2064392 | tf_op jit(solution)/shard_map/ppermute | solution.py:94
  36.5 31.7 %collective-permute-start.4 = (bf16[128,1024]{0,1:T(8,128)(2,1)}, bf16[128,1024]{0,1:T(8,128)(2,1)}, u32[]{:S(2)}, u32[]{:S(2)}) collective-permute-start(bf16[128,1024]{0,1:T(8,128)(2,1)} %pad_maximum_fusion), channel_id=1, source_target_pairs={{0,8},{2,10},{4,12},{6,14},{8,16},{10,18},{12,20},{14,22},{16,24},... | collective-permute-start | bytes 786440 | tf_op jit(solution)/shard_map/ppermute | solution.py:19
  42.8 28.7 %collective-permute-start.5 = (bf16[128,1024]{0,1:T(8,128)(2,1)}, bf16[128,1024]{0,1:T(8,128)(2,1)}, u32[]{:S(2)}, u32[]{:S(2)}) collective-permute-start(bf16[128,1024]{0,1:T(8,128)(2,1)} %pad_maximum_fusion), channel_id=1, source_target_pairs={{0,6},{2,8},{4,10},{6,12},{8,14},{10,16},{12,18},{14,20},{16,22},{... | collective-permute-start | bytes 786440 | tf_op jit(solution)/shard_map/ppermute | solution.py:19
  46.4 32.7 %collective-permute-start.6 = (bf16[128,1024]{0,1:T(8,128)(2,1)}, bf16[128,1024]{0,1:T(8,128)(2,1)}, u32[]{:S(2)}, u32[]{:S(2)}) collective-permute-start(bf16[128,1024]{0,1:T(8,128)(2,1)} %pad_maximum_fusion), channel_id=1, source_target_pairs={{0,4},{2,6},{4,8},{6,10},{8,12},{10,14},{12,16},{14,18},{16,20},{1... | collective-permute-start | bytes 786440 | tf_op jit(solution)/shard_map/ppermute | solution.py:19
  50.4 30.7 %collective-permute-start.7 = (bf16[128,1024]{0,1:T(8,128)(2,1)}, bf16[128,1024]{0,1:T(8,128)(2,1)}, u32[]{:S(2)}, u32[]{:S(2)}) collective-permute-start(bf16[128,1024]{0,1:T(8,128)(2,1)} %pad_maximum_fusion), channel_id=1, source_target_pairs={{0,2},{2,4},{4,6},{6,8},{8,10},{10,12},{12,14},{14,16},{16,18},{18... | collective-permute-start | bytes 786440 | tf_op jit(solution)/shard_map/ppermute | solution.py:19
  56.6 10.1 %copy-start.1 = (bf16[8,84,1024]{2,1,0:T(8,128)(2,1)}, bf16[8,84,1024]{2,1,0:T(8,128)(2,1)S(1)}, u32[]{:S(2)}) copy-start(bf16[8,84,1024]{2,1,0:T(8,128)(2,1)S(1)} %all-to-all-done.1) | copy-start | bytes 4128772
  56.6 33.9 %all-to-all-start = ((bf16[8,128,672]{1,2,0:T(8,128)(2,1)}), bf16[8,128,672]{1,2,0:T(8,128)(2,1)}, u32[]{:S(2)}, u32[]{:S(2)}) async-start(bf16[8,128,672]{1,2,0:T(8,128)(2,1)} %fusion.65), calls=%async_computation | async-start | bytes 2752512 | tf_op jit(solution)/shard_map/all_to_all | solution.py:108
  95.5 33.8 %all-to-all-start.2 = ((bf16[8,128,1024]{2,1,0:T(8,128)(2,1)}), bf16[8,128,1024]{2,1,0:T(8,128)(2,1)}, u32[]{:S(2)}, u32[]{:S(2)}) async-start(bf16[8,128,1024]{2,1,0:T(8,128)(2,1)} %convolution_convert_fusion.1), calls=%async_computation.2 | async-start | bytes 4194304 | tf_op jit(solution)/shard_map/all_to_all | solution.py:113
  108.8 88.9 %all-gather.2.cloned.1.call-start = ((), (), s32[]{:S(2)}) async-start(), calls=%async_computation.5 | async-start | bytes 2359296 | tf_op jit(solution)/shard_map/all_gather | solution.py:124
  155.8 41.7 %all-to-all-start.3 = ((bf16[8,128,8,84]{1,2,3,0:T(8,128)(2,1)}), bf16[8,128,8,84]{1,2,3,0:T(8,128)(2,1)S(1)}, u32[]{:S(2)}, u32[]{:S(2)}) async-start(bf16[8,128,8,84]{1,2,3,0:T(8,128)(2,1)} %copy.62), calls=%async_computation.3 | async-start | bytes 2752512 | tf_op jit(solution)/shard_map/all_to_all | solution.py:121
  202.5 6.1 %copy-start.7 = (bf16[128,1024]{1,0:T(8,128)(2,1)S(1)}, bf16[128,1024]{1,0:T(8,128)(2,1)}, u32[]{:S(2)}) copy-start(bf16[128,1024]{1,0:T(8,128)(2,1)} %get-tuple-element.276) | copy-start | bytes 786436
  202.5 8.7 %copy-start.6 = (bf16[128,1024]{1,0:T(8,128)(2,1)S(1)}, bf16[128,1024]{1,0:T(8,128)(2,1)}, u32[]{:S(2)}) copy-start(bf16[128,1024]{1,0:T(8,128)(2,1)} %get-tuple-element.275) | copy-start | bytes 786436
  202.5 10.9 %copy-start.5 = (bf16[128,1024]{1,0:T(8,128)(2,1)S(1)}, bf16[128,1024]{1,0:T(8,128)(2,1)}, u32[]{:S(2)}) copy-start(bf16[128,1024]{1,0:T(8,128)(2,1)} %get-tuple-element.274) | copy-start | bytes 786436
  202.5 14.0 %copy-start.4 = (bf16[128,1024]{1,0:T(8,128)(2,1)S(1)}, bf16[128,1024]{1,0:T(8,128)(2,1)}, u32[]{:S(2)}) copy-start(bf16[128,1024]{1,0:T(8,128)(2,1)} %get-tuple-element.273) | copy-start | bytes 786436
  202.5 16.0 %copy-start.3 = (bf16[128,1024]{1,0:T(8,128)(2,1)S(1)}, bf16[128,1024]{1,0:T(8,128)(2,1)}, u32[]{:S(2)}) copy-start(bf16[128,1024]{1,0:T(8,128)(2,1)} %get-tuple-element.272) | copy-start | bytes 786436
  202.6 78.0 %all-to-all-start.4 = ((bf16[8,1024,84]{1,2,0:T(8,128)(2,1)}), bf16[8,1024,84]{1,2,0:T(8,128)(2,1)S(1)}, u32[]{:S(2)}, u32[]{:S(2)}) async-start(bf16[8,1024,84]{1,2,0:T(8,128)(2,1)} %fusion.60), calls=%async_computation.4 | async-start | bytes 2883584 | tf_op jit(solution)/shard_map/all_to_all | solution.py:151
  208.6 28.3 %collective-permute-start.10 = (bf16[128,1024]{1,0:T(8,128)(2,1)S(1)}, bf16[128,1024]{1,0:T(8,128)(2,1)S(1)}, u32[]{:S(2)}, u32[]{:S(2)}) collective-permute-start(bf16[128,1024]{1,0:T(8,128)(2,1)S(1)} %copy-done.7), channel_id=1, source_target_pairs={{4,0},{6,2},{8,4},{10,6},{12,8},{14,10},{16,12},{18,14},{20,16},{2... | collective-permute-start | bytes 786440 | tf_op jit(solution)/shard_map/ppermute | solution.py:19
  211.2 31.9 %collective-permute-start.11 = (bf16[128,1024]{1,0:T(8,128)(2,1)S(1)}, bf16[128,1024]{1,0:T(8,128)(2,1)S(1)}, u32[]{:S(2)}, u32[]{:S(2)}) collective-permute-start(bf16[128,1024]{1,0:T(8,128)(2,1)S(1)} %copy-done.6), channel_id=1, source_target_pairs={{6,0},{8,2},{10,4},{12,6},{14,8},{16,10},{18,12},{20,14},{22,16},{... | collective-permute-start | bytes 786440 | tf_op jit(solution)/shard_map/ppermute | solution.py:19
  213.5 39.9 %collective-permute-start.12 = (bf16[128,1024]{1,0:T(8,128)(2,1)S(1)}, bf16[128,1024]{1,0:T(8,128)(2,1)S(1)}, u32[]{:S(2)}, u32[]{:S(2)}) collective-permute-start(bf16[128,1024]{1,0:T(8,128)(2,1)S(1)} %copy-done.5), channel_id=1, source_target_pairs={{8,0},{10,2},{12,4},{14,6},{16,8},{18,10},{20,12},{22,14},{24,16},... | collective-permute-start | bytes 786440 | tf_op jit(solution)/shard_map/ppermute | solution.py:19
  216.6 43.2 %collective-permute-start.13 = (bf16[128,1024]{1,0:T(8,128)(2,1)S(1)}, bf16[128,1024]{1,0:T(8,128)(2,1)}, u32[]{:S(2)}, u32[]{:S(2)}) collective-permute-start(bf16[128,1024]{1,0:T(8,128)(2,1)S(1)} %copy-done.4), channel_id=1, source_target_pairs={{10,0},{12,2},{14,4},{16,6},{18,8},{20,10},{22,12},{24,14},{26,16}... | collective-permute-start | bytes 786440 | tf_op jit(solution)/shard_map/ppermute | solution.py:19
  218.5 46.9 %collective-permute-start.14 = (bf16[128,1024]{1,0:T(8,128)(2,1)S(1)}, bf16[128,1024]{1,0:T(8,128)(2,1)}, u32[]{:S(2)}, u32[]{:S(2)}) collective-permute-start(bf16[128,1024]{1,0:T(8,128)(2,1)S(1)} %copy-done.3), channel_id=1, source_target_pairs={{12,0},{14,2},{16,4},{18,6},{20,8},{22,10},{24,12},{26,14},{28,16}... | collective-permute-start | bytes 786440 | tf_op jit(solution)/shard_map/ppermute | solution.py:19
  236.9 18.4 %copy-start.11 = (bf16[128,1024]{1,0:T(8,128)(2,1)}, bf16[128,1024]{1,0:T(8,128)(2,1)S(1)}, u32[]{:S(2)}) copy-start(bf16[128,1024]{1,0:T(8,128)(2,1)S(1)} %collective-permute-done.10) | copy-start | bytes 786436
  236.9 34.1 %collective-permute-start.15 = (bf16[128,1024]{1,0:T(8,128)(2,1)S(1)}, bf16[128,1024]{1,0:T(8,128)(2,1)S(1)}, u32[]{:S(2)}, u32[]{:S(2)}) collective-permute-start(bf16[128,1024]{1,0:T(8,128)(2,1)S(1)} %get-tuple-element.271), channel_id=1, source_target_pairs={{14,0},{16,2},{18,4},{20,6},{22,8},{24,10},{26,12},{28,14},{30,16}... | collective-permute-start | bytes 786440 | tf_op jit(solution)/shard_map/ppermute | solution.py:19
  243.1 12.2 %copy-start.12 = (bf16[128,1024]{1,0:T(8,128)(2,1)}, bf16[128,1024]{1,0:T(8,128)(2,1)S(1)}, u32[]{:S(2)}) copy-start(bf16[128,1024]{1,0:T(8,128)(2,1)S(1)} %collective-permute-done.11) | copy-start | bytes 786436
  243.1 34.5 %collective-permute-start.16 = (bf16[128,1024]{1,0:T(8,128)(2,1)S(1)}, bf16[128,1024]{1,0:T(8,128)(2,1)S(1)}, u32[]{:S(2)}, u32[]{:S(2)}) collective-permute-start(bf16[128,1024]{1,0:T(8,128)(2,1)S(1)} %get-tuple-element.270), channel_id=1, source_target_pairs={{16,0},{18,2},{20,4},{22,6},{24,8},{26,10},{28,12},{30,14},{32,16}... | collective-permute-start | bytes 786440 | tf_op jit(solution)/shard_map/ppermute | solution.py:19
  253.4 24.6 %collective-permute-start.9 = (bf16[128,1024]{1,0:T(8,128)(2,1)S(1)}, bf16[128,1024]{1,0:T(8,128)(2,1)S(1)}, u32[]{:S(2)}, u32[]{:S(2)}) collective-permute-start(bf16[128,1024]{1,0:T(8,128)(2,1)S(1)} %get-tuple-element.269), channel_id=1, source_target_pairs={{2,0},{4,2},{6,4},{8,6},{10,8},{12,10},{14,12},{16,14},{18,16},{20... | collective-permute-start | bytes 786440 | tf_op jit(solution)/shard_map/ppermute | solution.py:19
  (13 other events, 29.6 us)
Sparse Core Ops, SparseCore 0:
  118.7 37.1 all-gather.1

commit v3 on v2

--- a/solution.py
+++ b/solution.py
@@ -115,13 +115,8 @@
         ),
         0,
     )
-    by_position = cotangent.reshape(tokens_dev, group_count, group_size, block).transpose(2, 0, 1, 3)
-    by_position, grad_sum = lax.optimization_barrier((by_position, grad_sum))
     attention_gradient = grad_sum.astype(jnp.bfloat16)
-    wg_columns = lax.all_to_all(by_position, "cp", 0, 0, tiled=True).reshape(
-        group_size * tokens_dev, group_count, block
-    )
-    group_probs = lax.all_gather(attention_probs, "cp", axis=0, tiled=True)
+    group_probs = lax.all_gather(attention_probs, "cg", axis=0, tiled=True)
     grad_rows = attention_gradient.reshape(tokens_dev, kv_local, group_width, HEAD_SIZE)
     row_deltas = jnp.sum(grad_rows.astype(jnp.float32) * attn_rows.astype(jnp.float32), axis=-1)
     head_gradients = grad_rows.transpose(1, 0, 2, 3)
@@ -135,20 +130,31 @@
     key_ext_grad = key_parts.transpose(1, 0, 2).reshape(-1, kv_local * HEAD_SIZE)
     value_ext_grad = value_parts.transpose(1, 0, 2).reshape(-1, kv_local * HEAD_SIZE)
     pair_grad = jnp.concatenate([key_ext_grad, value_ext_grad], 1)
-    pair_total = pair_grad[reach_count * tokens_dev :]
-    sent = [
-        pair_grad[(reach_count - offset) * tokens_dev : (reach_count - offset + 1) * tokens_dev]
-        for offset in range(1, reach_count + 1)
+    ctx = ("cg", "cp")
+    parts = [
+        pair_grad[(reach_count - d) * tokens_dev : (reach_count - d + 1) * tokens_dev]
+        for d in range(reach_count + 1)
     ]
-    sent = [block.astype(jnp.bfloat16) for block in sent]
-    for offset in range(1, reach_count + 1):
-        arrived = from_behind(sent[offset - 1], ("cg", "cp"), -offset)
-        pair_total = pair_total + arrived.astype(jnp.float32)
-    group_probs, wg_columns, sent = lax.optimization_barrier((group_probs, wg_columns, sent))
+    width = reach_count
+    arrived = from_behind(parts[width].astype(jnp.bfloat16), ctx, -1)
+    parts = parts[:width]
+    parts[width - 1] = parts[width - 1] + arrived.astype(jnp.float32)
+    sent = arrived
+    assert width & (width - 1) == 0
+    while width > 1:
+        half = width // 2
+        moved = from_behind(jnp.stack(parts[half:]).astype(jnp.bfloat16), ctx, -half)
+        parts = [parts[k] + moved[k].astype(jnp.float32) for k in range(half)]
+        width = half
+    pair_total = parts[0]
+    group_probs, group_columns, sent = lax.optimization_barrier((group_probs, group_columns, sent))
     weight_term = jnp.einsum(
-        "th,tak->ahk", group_probs, wg_columns, preferred_element_type=jnp.float32
+        "th,tqk->qhk",
+        group_probs,
+        group_columns.reshape(group_count * tokens_dev, group_size, block),
+        preferred_element_type=jnp.float32,
     ) * (tokens_dev * n_ctx) ** (-0.5)
-    weight_parts = lax.all_to_all(weight_term.astype(jnp.bfloat16), "cg", 0, 0, tiled=True)
+    weight_parts = lax.all_to_all(weight_term.astype(jnp.bfloat16), "cp", 0, 0, tiled=True)
     weight_grad = jnp.sum(weight_parts.astype(jnp.float32), 0)
     key_total = pair_total[:, :kv_width]
     value_total = pair_total[:, kv_width:]

time: 291 us -> 275 us (0.945)
  the two profiles are of different devices: /device:TPU:8 before, /device:TPU:19 now
where the time goes in v3:
time: 275 us; the launch traced here: 274 us
  starting transfers between devices  111 us (40%)
  waiting for transfers between devices  68.2 us (25%)
  local copies, waits for them, and re-layouts  35.7 us (13%)
  matrix products  25.7 us (9%)
  other arithmetic  18.4 us (7%)
  between operations  14.4 us (5%)
    ppermute x12, starting transfers between devices, from_behind(): return lax.ppermute(block, axis, route)  79.5 us
    ppermute x12, waiting for transfers between devices, from_behind(): return lax.ppermute(block, axis, route)  33.1 us
    unnamed x39, local copies, waits for them, and re-layouts  20.3 us
    all_gather x1, waiting for transfers between devices, device_body(): group_probs = lax.all_gather(attention_probs, 'cg', axis=0, tiled=True)  18 us
    all_to_all x1, waiting for transfers between devices, device_body(): lax.all_to_all(partial_grads.astype(jnp.bfloat16), 'cg', 0, 0, tiled=True)  13.5 us
    all_to_all x1, starting transfers between devices, device_body(): lax.all_to_all(weight_term.astype(jnp.bfloat16), 'cp', 0, 0, tiled=True)  10 us
    all_to_all x1, starting transfers between devices, device_body(): group_columns = lax.all_to_all(by_group, 'cg', 0, 0, tiled=True)  9.85 us
    and x8, other arithmetic, band_mask(): return earlier & within & (key_pos[None, :] >= 0)  6.89 us
  transfers between devices with their start and end apart: 18, of which 6 were waited for; matrix products, arithmetic and copies ran while one was open for 24% of the time, Pallas kernels for 0%

profile of v3, /device:TPU:19, one launch (start us, length us, event | category | flops | bytes accessed | tf_op | source)
XLA Modules:
  0.0 274.0 jit_solution(12350615957469632834)
XLA Ops:
  7.2 2.3 broadcast_in_dim.63
  9.4 6.1 %all-to-all-start.1 = ((bf16[8,84,1024]{2,1,0:T(8,128)(2,1)}), bf16[8,84,1024]{2,1,0:T(8,128)(2,1)S(1)}, u32[]{:S(2)}, u32[]{:S(2)}) async-start(bf16[8,84,1024]{2,1,0:T(8,128)(2,1)} %broadcast_in_dim.63), calls=%async_computation.1 | async-start | bytes 2883584 | tf_op jit(solution)/shard_map/all_to_all | solution.py:104
  15.8 2.9 %collective-permute-start = (bf16[128,1024]{0,1:T(8,128)(2,1)S(1)}, bf16[128,1024]{0,1:T(8,128)(2,1)}, u32[]{:S(2)}, u32[]{:S(2)}) collective-permute-start(bf16[128,1024]{0,1:T(8,128)(2,1)S(1)} %pad_maximum_fusion.2), channel_id=1, source_target_pairs={{0,16},{2,18},{4,20},{6,22},{8,24},{10,26},{12,28},{14,30},{16,32}... | collective-permute-start | bytes 786440 | tf_op jit(solution)/shard_map/ppermute | solution.py:19
  18.8 3.5 %collective-permute-start.1 = (bf16[128,1024]{0,1:T(8,128)(2,1)S(1)}, bf16[128,1024]{0,1:T(8,128)(2,1)}, u32[]{:S(2)}, u32[]{:S(2)}) collective-permute-start(bf16[128,1024]{0,1:T(8,128)(2,1)S(1)} %pad_maximum_fusion.2), channel_id=1, source_target_pairs={{0,14},{2,16},{4,18},{6,20},{8,22},{10,24},{12,26},{14,28},{16,30}... | collective-permute-start | bytes 786440 | tf_op jit(solution)/shard_map/ppermute | solution.py:19
  22.2 4.9 %collective-permute-start.2 = (bf16[128,1024]{0,1:T(8,128)(2,1)S(1)}, bf16[128,1024]{0,1:T(8,128)(2,1)}, u32[]{:S(2)}, u32[]{:S(2)}) collective-permute-start(bf16[128,1024]{0,1:T(8,128)(2,1)S(1)} %pad_maximum_fusion.2), channel_id=1, source_target_pairs={{0,12},{2,14},{4,16},{6,18},{8,20},{10,22},{12,24},{14,26},{16,28}... | collective-permute-start | bytes 786440 | tf_op jit(solution)/shard_map/ppermute | solution.py:19
  27.1 3.2 %collective-permute-start.3 = (bf16[128,1024]{0,1:T(8,128)(2,1)S(1)}, bf16[128,1024]{0,1:T(8,128)(2,1)}, u32[]{:S(2)}, u32[]{:S(2)}) collective-permute-start(bf16[128,1024]{0,1:T(8,128)(2,1)S(1)} %pad_maximum_fusion.2), channel_id=1, source_target_pairs={{0,10},{2,12},{4,14},{6,16},{8,18},{10,20},{12,22},{14,24},{16,26}... | collective-permute-start | bytes 786440 | tf_op jit(solution)/shard_map/ppermute | solution.py:19
  33.4 4.3 %collective-permute-start.4 = (bf16[128,1024]{0,1:T(8,128)(2,1)S(1)}, bf16[128,1024]{0,1:T(8,128)(2,1)}, u32[]{:S(2)}, u32[]{:S(2)}) collective-permute-start(bf16[128,1024]{0,1:T(8,128)(2,1)S(1)} %pad_maximum_fusion.2), channel_id=1, source_target_pairs={{0,8},{2,10},{4,12},{6,14},{8,16},{10,18},{12,20},{14,22},{16,24},... | collective-permute-start | bytes 786440 | tf_op jit(solution)/shard_map/ppermute | solution.py:19
  39.4 4.4 %collective-permute-start.5 = (bf16[128,1024]{0,1:T(8,128)(2,1)S(1)}, bf16[128,1024]{0,1:T(8,128)(2,1)}, u32[]{:S(2)}, u32[]{:S(2)}) collective-permute-start(bf16[128,1024]{0,1:T(8,128)(2,1)S(1)} %pad_maximum_fusion.2), channel_id=1, source_target_pairs={{0,6},{2,8},{4,10},{6,12},{8,14},{10,16},{12,18},{14,20},{16,22},{... | collective-permute-start | bytes 786440 | tf_op jit(solution)/shard_map/ppermute | solution.py:19
  45.6 2.5 collective-permute-start.6
  48.0 1.8 constant_dynamic-update-slice_fusion.7
  49.8 6.7 %collective-permute-start.7 = (bf16[128,1024]{0,1:T(8,128)(2,1)S(1)}, bf16[128,1024]{0,1:T(8,128)(2,1)}, u32[]{:S(2)}, u32[]{:S(2)}) collective-permute-start(bf16[128,1024]{0,1:T(8,128)(2,1)S(1)} %pad_maximum_fusion.2), channel_id=1, source_target_pairs={{0,2},{2,4},{4,6},{6,8},{8,10},{10,12},{12,14},{14,16},{16,18},{18... | collective-permute-start | bytes 786440 | tf_op jit(solution)/shard_map/ppermute | solution.py:19
  59.2 9.8 %all-to-all-start = ((bf16[8,128,672]{1,2,0:T(8,128)(2,1)}), bf16[8,128,672]{1,2,0:T(8,128)(2,1)}, u32[]{:S(2)}, u32[]{:S(2)}) async-start(bf16[8,128,672]{1,2,0:T(8,128)(2,1)} %fusion.63), calls=%async_computation | async-start | bytes 2752512 | tf_op jit(solution)/shard_map/all_to_all | solution.py:108
  78.3 1.8 fusion.77
  80.9 2.3 reshape.123
  83.2 3.5 %all-to-all-done = bf16[8,128,672]{1,2,0:T(8,128)(2,1)} async-done(((bf16[8,128,672]{1,2,0:T(8,128)(2,1)}), bf16[8,128,672]{1,2,0:T(8,128)(2,1)}, u32[]{:S(2)}, u32[]{:S(2)}) %all-to-all-start) | async-done | bytes 1376288 | tf_op jit(solution)/shard_map/all_to_all | solution.py:108
  86.7 5.0 %convolution_convert_fusion.1 = bf16[8,128,1024]{2,1,0:T(8,128)(2,1)} fusion(bf16[8,128,672]{1,2,0:T(8,128)(2,1)} %all-to-all-done, bf16[672,1024,1]{1,0,2:T(8,128)(2,1)} %reshape.123), kind=kOutput, calls=%fused_computation.75 | convolution fusion | flops 1410334720 | bytes 4849664 | tf_op jit(solution)/shard_map/btk,kh->bth/dot_general | solution.py:109
  91.7 5.4 %all-to-all-start.2 = ((bf16[8,128,1024]{2,1,0:T(8,128)(2,1)}), bf16[8,128,1024]{2,1,0:T(8,128)(2,1)}, u32[]{:S(2)}, u32[]{:S(2)}) async-start(bf16[8,128,1024]{2,1,0:T(8,128)(2,1)} %convolution_convert_fusion.1), calls=%async_computation.2 | async-start | bytes 4194304 | tf_op jit(solution)/shard_map/all_to_all | solution.py:113
  97.1 7.3 %while.28 = (s32[]{:T(128)}, bf16[4,128,2,128]{1,3,2,0:T(8,128)(2,1)S(1)}, f32[4,2,128]{2,1,0:T(2,128)S(1)}, bf16[4,1152,128]{1,2,0:T(8,128)(2,1)S(1)}, bf16[4,1...) while((s32[]{:T(128)}, ...), condition=%wide.region_4.5_spmd.clone, body=%wide.region_1.0_spmd.clone.sunk | while | flops 153829120 | bytes 4571369 | solution.py:88
  105.2 13.5 %all-to-all-done.2 = bf16[8,128,1024]{2,1,0:T(8,128)(2,1)} async-done(((bf16[8,128,1024]{2,1,0:T(8,128)(2,1)}), bf16[8,128,1024]{2,1,0:T(8,128)(2,1)}, u32[]{:S(2)}, u32[]{:S(2)}) %all-to-all-start.2) | async-done | bytes 2097184 | tf_op jit(solution)/shard_map/all_to_all | solution.py:113
  118.7 2.0 reduce_sum.39
  120.9 19.9 %while.29 = (s32[]{:T(128)}, bf16[4,128,2,128]{1,3,2,0:T(8,128)(2,1)}, f32[4,1152,128]{2,1,0:T(8,128)}, f32[4,1152,128]{2,1,0:T(8,128)}, bf16[4,1152,128]{2,1,0:...) while((s32[]{:T(128)}, ...), condition=%wide.region_7.8_spmd.clone, body=%wide.region_6.7_spmd.clone.sunk | while | flops 380469248 | bytes 10175813 | solution.py:124
  140.8 2.1 bitcast_dynamic-update-slice_fusion.1
  144.0 9.1 %collective-permute-start.9 = (bf16[128,1024]{1,0:T(8,128)(2,1)S(1)}, bf16[128,1024]{1,0:T(8,128)(2,1)S(1)}, u32[]{:S(2)}, u32[]{:S(2)}) collective-permute-start(bf16[128,1024]{1,0:T(8,128)(2,1)S(1)} %get-tuple-element.268), channel_id=1, source_target_pairs={{2,0},{4,2},{6,4},{8,6},{10,8},{12,10},{14,12},{16,14},{18,16},{20... | collective-permute-start | bytes 786440 | tf_op jit(solution)/shard_map/ppermute | solution.py:19
  155.4 33.3 %collective-permute-start.10 = (bf16[4,128,1024]{2,1,0:T(8,128)(2,1)}, bf16[4,128,1024]{2,1,0:T(8,128)(2,1)}, u32[]{:S(2)}, u32[]{:S(2)}) collective-permute-start(bf16[4,128,1024]{2,1,0:T(8,128)(2,1)} %pad_maximum_fusion), channel_id=1, source_target_pairs={{8,0},{10,2},{12,4},{14,6},{16,8},{18,10},{20,12},{22,14},{24,16},... | collective-permute-start | bytes 3145736 | tf_op jit(solution)/shard_map/ppermute | solution.py:19
  188.7 18.0 %all-gather.2.cloned.1.call-done = bf16[1024,1024]{0,1:T(8,128)(2,1)} async-done(((bf16[128,1024]{0,1:T(8,128)(2,1)}), bf16[1024,1024]{0,1:T(8,128)(2,1)}) %all-gather.2.cloned.1.call-update) | async-done | bytes 2097168 | tf_op jit(solution)/shard_map/all_gather | solution.py:119
  206.8 1.9 copy.56
  209.3 4.4 %fusion.60 = bf16[8,1024,84]{1,2,0:T(8,128)(2,1)} fusion(bf16[1024,8,84]{0,2,1:T(8,128)(2,1)S(1)} %reshape.108, bf16[1024,1024]{0,1:T(8,128)(2,1)} %all-gather.2.cloned.1.call-done), kind=kOutput, calls=%fused_computation.76 | convolution fusion | flops 1410662400 | bytes 4849664 | tf_op jit(solution)/shard_map/th,tqk->qhk/dot_general | solution.py:151
  213.7 10.0 %all-to-all-start.3 = ((bf16[8,1024,84]{1,2,0:T(8,128)(2,1)}), bf16[8,1024,84]{1,2,0:T(8,128)(2,1)S(1)}, u32[]{:S(2)}, u32[]{:S(2)}) async-start(bf16[8,1024,84]{1,2,0:T(8,128)(2,1)} %fusion.60), calls=%async_computation.3 | async-start | bytes 2883584 | tf_op jit(solution)/shard_map/all_to_all | solution.py:157
  225.3 1.9 collective-permute-start.11
  227.3 29.0 %collective-permute-done.11 = bf16[2,128,1024]{2,1,0:T(8,128)(2,1)S(1)} collective-permute-done((bf16[2,128,1024]{2,1,0:T(8,128)(2,1)S(1)}, bf16[2,128,1024]{2,1,0:T(8,128)(2,1)S(1)}, u32[]{:S(2)}, u32[]{:S(2)}) %collective-permute-start.11) | collective-permute-done | bytes 524320 | tf_op jit(solution)/shard_map/ppermute | solution.py:19
  257.5 2.9 %collective-permute-start.12 = (bf16[1,128,1024]{2,1,0:T(8,128)(2,1)S(1)}, bf16[1,128,1024]{2,1,0:T(8,128)(2,1)S(1)}, u32[]{:S(2)}, u32[]{:S(2)}) collective-permute-start(bf16[1,128,1024]{2,1,0:T(8,128)(2,1)S(1)} %fusion.75), channel_id=1, source_target_pairs={{2,0},{4,2},{6,4},{8,6},{10,8},{12,10},{14,12},{16,14},{18,16},{20... | collective-permute-start | bytes 786440 | tf_op jit(solution)/shard_map/ppermute | solution.py:19
  262.2 3.0 %collective-permute-done.12 = bf16[1,128,1024]{2,1,0:T(8,128)(2,1)S(1)} collective-permute-done((bf16[1,128,1024]{2,1,0:T(8,128)(2,1)S(1)}, bf16[1,128,1024]{2,1,0:T(8,128)(2,1)S(1)}, u32[]{:S(2)}, u32[]{:S(2)}) %collective-permute-start.12) | collective-permute-done | bytes 262176 | tf_op jit(solution)/shard_map/ppermute | solution.py:19
  (148 shorter events, 57.9 us)
Async XLA Ops:
  7.2 8.4 %copy-start.11 = (bf16[128,512]{1,0:T(8,128)(2,1)S(1)}, bf16[128,512]{1,0:T(8,128)(2,1)}, u32[]{:S(2)}) copy-start(bf16[128,512]{1,0:T(8,128)(2,1)} %param.10) | copy-start | bytes 393220
  7.2 8.5 %copy-start.12 = (bf16[128,512]{1,0:T(8,128)(2,1)S(1)}, bf16[128,512]{1,0:T(8,128)(2,1)}, u32[]{:S(2)}) copy-start(bf16[128,512]{1,0:T(8,128)(2,1)} %param.11) | copy-start | bytes 393220
  9.4 22.9 %copy-start.7 = (bf16[128,1024]{1,0:T(8,128)(2,1)S(1)}, bf16[128,1024]{1,0:T(8,128)(2,1)}, u32[]{:S(2)}) copy-start(bf16[128,1024]{1,0:T(8,128)(2,1)} %param.9) | copy-start | bytes 786436
  9.4 49.8 %all-to-all-start.1 = ((bf16[8,84,1024]{2,1,0:T(8,128)(2,1)}), bf16[8,84,1024]{2,1,0:T(8,128)(2,1)S(1)}, u32[]{:S(2)}, u32[]{:S(2)}) async-start(bf16[8,84,1024]{2,1,0:T(8,128)(2,1)} %broadcast_in_dim.63), calls=%async_computation.1 | async-start | bytes 2883584 | tf_op jit(solution)/shard_map/all_to_all | solution.py:104
  15.8 17.5 %collective-permute-start = (bf16[128,1024]{0,1:T(8,128)(2,1)S(1)}, bf16[128,1024]{0,1:T(8,128)(2,1)}, u32[]{:S(2)}, u32[]{:S(2)}) collective-permute-start(bf16[128,1024]{0,1:T(8,128)(2,1)S(1)} %pad_maximum_fusion.2), channel_id=1, source_target_pairs={{0,16},{2,18},{4,20},{6,22},{8,24},{10,26},{12,28},{14,30},{16,32}... | collective-permute-start | bytes 786440 | tf_op jit(solution)/shard_map/ppermute | solution.py:19
  18.8 20.6 %collective-permute-start.1 = (bf16[128,1024]{0,1:T(8,128)(2,1)S(1)}, bf16[128,1024]{0,1:T(8,128)(2,1)}, u32[]{:S(2)}, u32[]{:S(2)}) collective-permute-start(bf16[128,1024]{0,1:T(8,128)(2,1)S(1)} %pad_maximum_fusion.2), channel_id=1, source_target_pairs={{0,14},{2,16},{4,18},{6,20},{8,22},{10,24},{12,26},{14,28},{16,30}... | collective-permute-start | bytes 786440 | tf_op jit(solution)/shard_map/ppermute | solution.py:19
  22.2 23.3 %collective-permute-start.2 = (bf16[128,1024]{0,1:T(8,128)(2,1)S(1)}, bf16[128,1024]{0,1:T(8,128)(2,1)}, u32[]{:S(2)}, u32[]{:S(2)}) collective-permute-start(bf16[128,1024]{0,1:T(8,128)(2,1)S(1)} %pad_maximum_fusion.2), channel_id=1, source_target_pairs={{0,12},{2,14},{4,16},{6,18},{8,20},{10,22},{12,24},{14,26},{16,28}... | collective-permute-start | bytes 786440 | tf_op jit(solution)/shard_map/ppermute | solution.py:19
  27.1 42.0 %collective-permute-start.3 = (bf16[128,1024]{0,1:T(8,128)(2,1)S(1)}, bf16[128,1024]{0,1:T(8,128)(2,1)}, u32[]{:S(2)}, u32[]{:S(2)}) collective-permute-start(bf16[128,1024]{0,1:T(8,128)(2,1)S(1)} %pad_maximum_fusion.2), channel_id=1, source_target_pairs={{0,10},{2,12},{4,14},{6,16},{8,18},{10,20},{12,22},{14,24},{16,26}... | collective-permute-start | bytes 786440 | tf_op jit(solution)/shard_map/ppermute | solution.py:19
  30.3 19.5 %collective-permute-start.8 = (bf16[128,2688]{1,0:T(8,128)(2,1)}, bf16[128,2688]{1,0:T(8,128)(2,1)}, u32[]{:S(2)}, u32[]{:S(2)}) collective-permute-start(bf16[128,2688]{1,0:T(8,128)(2,1)} %param.12), channel_id=1, source_target_pairs={{0,1},{1,0},{2,3},{3,2},{4,5},{5,4},{6,7},{7,6},{8,9},{9,8},{10,11... | collective-permute-start | bytes 2064392 | tf_op jit(solution)/shard_map/ppermute | solution.py:94
  33.4 37.4 %collective-permute-start.4 = (bf16[128,1024]{0,1:T(8,128)(2,1)S(1)}, bf16[128,1024]{0,1:T(8,128)(2,1)}, u32[]{:S(2)}, u32[]{:S(2)}) collective-permute-start(bf16[128,1024]{0,1:T(8,128)(2,1)S(1)} %pad_maximum_fusion.2), channel_id=1, source_target_pairs={{0,8},{2,10},{4,12},{6,14},{8,16},{10,18},{12,20},{14,22},{16,24},... | collective-permute-start | bytes 786440 | tf_op jit(solution)/shard_map/ppermute | solution.py:19
  39.4 33.1 %collective-permute-start.5 = (bf16[128,1024]{0,1:T(8,128)(2,1)S(1)}, bf16[128,1024]{0,1:T(8,128)(2,1)}, u32[]{:S(2)}, u32[]{:S(2)}) collective-permute-start(bf16[128,1024]{0,1:T(8,128)(2,1)S(1)} %pad_maximum_fusion.2), channel_id=1, source_target_pairs={{0,6},{2,8},{4,10},{6,12},{8,14},{10,16},{12,18},{14,20},{16,22},{... | collective-permute-start | bytes 786440 | tf_op jit(solution)/shard_map/ppermute | solution.py:19
  45.6 28.6 %collective-permute-start.6 = (bf16[128,1024]{0,1:T(8,128)(2,1)S(1)}, bf16[128,1024]{0,1:T(8,128)(2,1)}, u32[]{:S(2)}, u32[]{:S(2)}) collective-permute-start(bf16[128,1024]{0,1:T(8,128)(2,1)S(1)} %pad_maximum_fusion.2), channel_id=1, source_target_pairs={{0,4},{2,6},{4,8},{6,10},{8,12},{10,14},{12,16},{14,18},{16,20},{1... | collective-permute-start | bytes 786440 | tf_op jit(solution)/shard_map/ppermute | solution.py:19
  49.8 26.1 %collective-permute-start.7 = (bf16[128,1024]{0,1:T(8,128)(2,1)S(1)}, bf16[128,1024]{0,1:T(8,128)(2,1)}, u32[]{:S(2)}, u32[]{:S(2)}) collective-permute-start(bf16[128,1024]{0,1:T(8,128)(2,1)S(1)} %pad_maximum_fusion.2), channel_id=1, source_target_pairs={{0,2},{2,4},{4,6},{6,8},{8,10},{10,12},{12,14},{14,16},{16,18},{18... | collective-permute-start | bytes 786440 | tf_op jit(solution)/shard_map/ppermute | solution.py:19
  59.2 15.0 %copy-start.1 = (bf16[8,84,1024]{2,1,0:T(8,128)(2,1)}, bf16[8,84,1024]{2,1,0:T(8,128)(2,1)S(1)}, u32[]{:S(2)}) copy-start(bf16[8,84,1024]{2,1,0:T(8,128)(2,1)S(1)} %all-to-all-done.1) | copy-start | bytes 4128772
  59.2 27.5 %all-to-all-start = ((bf16[8,128,672]{1,2,0:T(8,128)(2,1)}), bf16[8,128,672]{1,2,0:T(8,128)(2,1)}, u32[]{:S(2)}, u32[]{:S(2)}) async-start(bf16[8,128,672]{1,2,0:T(8,128)(2,1)} %fusion.63), calls=%async_computation | async-start | bytes 2752512 | tf_op jit(solution)/shard_map/all_to_all | solution.py:108
  91.7 5.4 %copy-start.2 = (bf16[4,128,2,128]{3,1,2,0:T(8,128)(2,1)S(1)}, bf16[4,128,2,128]{3,1,2,0:T(8,128)(2,1)}, u32[]{:S(2)}) copy-start(bf16[4,128,2,128]{3,1,2,0:T(8,128)(2,1)} %copy.50) | copy-start | bytes 786436
  91.7 5.4 %copy-start.4 = (bf16[4,128,2,128]{1,3,2,0:T(8,128)(2,1)S(1)}, bf16[4,128,2,128]{1,3,2,0:T(8,128)(2,1)}, u32[]{:S(2)}) copy-start(bf16[4,128,2,128]{1,3,2,0:T(8,128)(2,1)} %custom-call.2) | copy-start | bytes 786436
  91.7 5.4 %copy-start.13 = (f32[4,2,128]{2,1,0:T(2,128)S(1)}, f32[4,2,128]{2,1,0:T(2,128)}, u32[]{:S(2)}) copy-start(f32[4,2,128]{2,1,0:T(2,128)} %custom-call.3) | copy-start | bytes 12292
  91.7 27.0 %all-to-all-start.2 = ((bf16[8,128,1024]{2,1,0:T(8,128)(2,1)}), bf16[8,128,1024]{2,1,0:T(8,128)(2,1)}, u32[]{:S(2)}, u32[]{:S(2)}) async-start(bf16[8,128,1024]{2,1,0:T(8,128)(2,1)} %convolution_convert_fusion.1), calls=%async_computation.2 | async-start | bytes 4194304 | tf_op jit(solution)/shard_map/all_to_all | solution.py:113
  97.0 109.7 %all-gather.2.cloned.1.call-start = ((), (), s32[]{:S(2)}) async-start(), calls=%async_computation.4 | async-start | bytes 2359296 | tf_op jit(solution)/shard_map/all_gather | solution.py:119
  105.2 15.7 %copy-start.6 = (bf16[4,128,2,128]{1,3,2,0:T(8,128)(2,1)S(1)}, bf16[4,128,2,128]{1,3,2,0:T(8,128)(2,1)}, u32[]{:S(2)}) copy-start(bf16[4,128,2,128]{1,3,2,0:T(8,128)(2,1)} %copy-done.5) | copy-start | bytes 786436
  122.2 2.6 copy-start.8
  127.2 2.7 copy-start.8
  132.1 2.7 copy-start.8
  137.1 2.7 copy-start.8
  143.5 10.7 %copy-start = (f32[1152,1024]{1,0:T(8,128)}, f32[1152,1024]{1,0:T(8,128)S(1)}, u32[]{:S(2)}) copy-start(f32[1152,1024]{1,0:T(8,128)S(1)} %bitcast_dynamic-update-slice_fusion) | copy-start | bytes 14155780
  144.0 10.3 %collective-permute-start.9 = (bf16[128,1024]{1,0:T(8,128)(2,1)S(1)}, bf16[128,1024]{1,0:T(8,128)(2,1)S(1)}, u32[]{:S(2)}, u32[]{:S(2)}) collective-permute-start(bf16[128,1024]{1,0:T(8,128)(2,1)S(1)} %get-tuple-element.268), channel_id=1, source_target_pairs={{2,0},{4,2},{6,4},{8,6},{10,8},{12,10},{14,12},{16,14},{18,16},{20... | collective-permute-start | bytes 786440 | tf_op jit(solution)/shard_map/ppermute | solution.py:19
  155.4 68.3 %collective-permute-start.10 = (bf16[4,128,1024]{2,1,0:T(8,128)(2,1)}, bf16[4,128,1024]{2,1,0:T(8,128)(2,1)}, u32[]{:S(2)}, u32[]{:S(2)}) collective-permute-start(bf16[4,128,1024]{2,1,0:T(8,128)(2,1)} %pad_maximum_fusion), channel_id=1, source_target_pairs={{8,0},{10,2},{12,4},{14,6},{16,8},{18,10},{20,12},{22,14},{24,16},... | collective-permute-start | bytes 3145736 | tf_op jit(solution)/shard_map/ppermute | solution.py:19
  213.7 47.5 %all-to-all-start.3 = ((bf16[8,1024,84]{1,2,0:T(8,128)(2,1)}), bf16[8,1024,84]{1,2,0:T(8,128)(2,1)S(1)}, u32[]{:S(2)}, u32[]{:S(2)}) async-start(bf16[8,1024,84]{1,2,0:T(8,128)(2,1)} %fusion.60), calls=%async_computation.3 | async-start | bytes 2883584 | tf_op jit(solution)/shard_map/all_to_all | solution.py:157
  223.7 36.7 %copy-start.10 = (bf16[4,128,2,128]{1,3,2,0:T(8,128)(2,1)S(1)}, bf16[4,128,2,128]{1,3,2,0:T(8,128)(2,1)}, u32[]{:S(2)}) copy-start(bf16[4,128,2,128]{1,3,2,0:T(8,128)(2,1)} %get-tuple-element.105) | copy-start | bytes 786436
  225.3 31.0 %collective-permute-start.11 = (bf16[2,128,1024]{2,1,0:T(8,128)(2,1)S(1)}, bf16[2,128,1024]{2,1,0:T(8,128)(2,1)S(1)}, u32[]{:S(2)}, u32[]{:S(2)}) collective-permute-start(bf16[2,128,1024]{2,1,0:T(8,128)(2,1)S(1)} %pad_maximum_fusion.1), channel_id=1, source_target_pairs={{4,0},{6,2},{8,4},{10,6},{12,8},{14,10},{16,12},{18,14},{20,16},{2... | collective-permute-start | bytes 1572872 | tf_op jit(solution)/shard_map/ppermute | solution.py:19
  257.5 7.7 %collective-permute-start.12 = (bf16[1,128,1024]{2,1,0:T(8,128)(2,1)S(1)}, bf16[1,128,1024]{2,1,0:T(8,128)(2,1)S(1)}, u32[]{:S(2)}, u32[]{:S(2)}) collective-permute-start(bf16[1,128,1024]{2,1,0:T(8,128)(2,1)S(1)} %fusion.75), channel_id=1, source_target_pairs={{2,0},{4,2},{6,4},{8,6},{10,8},{12,10},{14,12},{16,14},{18,16},{20... | collective-permute-start | bytes 786440 | tf_op jit(solution)/shard_map/ppermute | solution.py:19
  (6 other events, 5.9 us)
Sparse Core Ops, SparseCore 0:
  105.3 101.4 all-gather.1

commit v4 on v2

--- a/solution.py
+++ b/solution.py
@@ -115,13 +115,8 @@
         ),
         0,
     )
-    by_position = cotangent.reshape(tokens_dev, group_count, group_size, block).transpose(2, 0, 1, 3)
-    by_position, grad_sum = lax.optimization_barrier((by_position, grad_sum))
     attention_gradient = grad_sum.astype(jnp.bfloat16)
-    wg_columns = lax.all_to_all(by_position, "cp", 0, 0, tiled=True).reshape(
-        group_size * tokens_dev, group_count, block
-    )
-    group_probs = lax.all_gather(attention_probs, "cp", axis=0, tiled=True)
+    group_probs = lax.all_gather(attention_probs, "cg", axis=0, tiled=True)
     grad_rows = attention_gradient.reshape(tokens_dev, kv_local, group_width, HEAD_SIZE)
     row_deltas = jnp.sum(grad_rows.astype(jnp.float32) * attn_rows.astype(jnp.float32), axis=-1)
     head_gradients = grad_rows.transpose(1, 0, 2, 3)
@@ -144,12 +139,14 @@
     for offset in range(1, reach_count + 1):
         arrived = from_behind(sent[offset - 1], ("cg", "cp"), -offset)
         pair_total = pair_total + arrived.astype(jnp.float32)
-    group_probs, wg_columns, sent = lax.optimization_barrier((group_probs, wg_columns, sent))
+    group_probs, group_columns, sent = lax.optimization_barrier((group_probs, group_columns, sent))
     weight_term = jnp.einsum(
-        "th,tak->ahk", group_probs, wg_columns, preferred_element_type=jnp.float32
+        "th,tqk->qhk",
+        group_probs,
+        group_columns.reshape(group_count * tokens_dev, group_size, block),
+        preferred_element_type=jnp.float32,
     ) * (tokens_dev * n_ctx) ** (-0.5)
-    weight_parts = lax.all_to_all(weight_term.astype(jnp.bfloat16), "cg", 0, 0, tiled=True)
-    weight_grad = jnp.sum(weight_parts.astype(jnp.float32), 0)
+    weight_grad = lax.psum_scatter(weight_term, "cp", scatter_dimension=0, tiled=True)[0]
     key_total = pair_total[:, :kv_width]
     value_total = pair_total[:, kv_width:]
     query_grad = query_parts.transpose(1, 0, 2, 3).reshape(tokens_dev, -1).astype(jnp.bfloat16)

time: 291 us -> 266 us (0.914)
  starting transfers between devices: 104 us -> 84.7 us
  other arithmetic: 19.8 us -> 13.7 us
    all_gather x1, waiting for transfers between devices: 0.02 us -> 28.3 us  [device_body(): group_probs = lax.all_gather(attention_probs, 'cg', axis=0, tiled=True)]
    all_to_all x2 -> x0, starting transfers between devices: 28.3 us -> none  [the longest x1 22.3 us: device_body(): lax.all_to_all(by_position, 'cp', 0, 0, tiled=True)]
    ppermute x16, waiting for transfers between devices: 59.3 us -> 39.2 us  [from_behind(): return lax.ppermute(block, axis, route)]
    all_to_all x2 -> x0, waiting for transfers between devices: 13.4 us -> none  [the longest x1 13.4 us: device_body(): lax.all_to_all(by_position, 'cp', 0, 0, tiled=True)]
    ppermute x16, starting transfers between devices: 45.5 us -> 53.3 us  [from_behind(): return lax.ppermute(block, axis, route)]
    all_to_all x1, waiting for transfers between devices: 6.49 us -> 13 us  [device_body(): lax.all_to_all(partial_grads.astype(jnp.bfloat16), 'cg', 0, 0, tiled=True)]
    transpose x1 -> x0, other arithmetic: 3.3 us -> none  [device_body(): cotangent.reshape(tokens_dev, group_count, group_size, block)]
    unnamed x43 -> x51, local copies, waits for them, and re-layouts: 20.6 us -> 23 us
  transfers between devices with their start and end apart: 23 -> 22, of which waited for: 14 -> 11; matrix products, arithmetic and copies ran while one was open for 25% -> 22% of each run, Pallas kernels for 0% -> 0%
where the time goes in v4:
time: 266 us; the launch traced here: 261 us
  starting transfers between devices  84.7 us (32%)
  waiting for transfers between devices  81.8 us (31%)
  local copies, waits for them, and re-layouts  39.6 us (15%)
  matrix products  26.2 us (10%)
  between operations  14.5 us (5%)
  other arithmetic  13.7 us (5%)
    ppermute x16, starting transfers between devices, from_behind(): return lax.ppermute(block, axis, route)  53.3 us
    ppermute x16, waiting for transfers between devices, from_behind(): return lax.ppermute(block, axis, route)  39.2 us
    all_gather x1, waiting for transfers between devices, device_body(): group_probs = lax.all_gather(attention_probs, 'cg', axis=0, tiled=True)  28.3 us
    unnamed x51, local copies, waits for them, and re-layouts  23 us
    all_to_all x1, starting transfers between devices, device_body(): lax.all_to_all(partial_grads.astype(jnp.bfloat16), 'cg', 0, 0, tiled=True)  13.3 us
    all_to_all x1, waiting for transfers between devices, device_body(): lax.all_to_all(partial_grads.astype(jnp.bfloat16), 'cg', 0, 0, tiled=True)  13 us
    all_to_all x1, starting transfers between devices, device_body(): group_columns = lax.all_to_all(by_group, 'cg', 0, 0, tiled=True)  9.79 us
    and x8, other arithmetic, band_mask(): return earlier & within & (key_pos[None, :] >= 0)  6.89 us
  transfers between devices with their start and end apart: 22, of which 11 were waited for; matrix products, arithmetic and copies ran while one was open for 22% of the time, Pallas kernels for 0%

profile of v4, /device:TPU:8, one launch (start us, length us, event | category | flops | bytes accessed | tf_op | source)
XLA Modules:
  0.0 261.0 jit_solution(7394607238576105939)
XLA Ops:
  7.2 2.2 broadcast_in_dim.63
  9.4 5.4 %all-to-all-start.1 = ((bf16[8,84,1024]{2,1,0:T(8,128)(2,1)}), bf16[8,84,1024]{2,1,0:T(8,128)(2,1)S(1)}, u32[]{:S(2)}, u32[]{:S(2)}) async-start(bf16[8,84,1024]{2,1,0:T(8,128)(2,1)} %broadcast_in_dim.63), calls=%async_computation.1 | async-start | bytes 2883584 | tf_op jit(solution)/shard_map/all_to_all | solution.py:104
  15.2 3.3 %collective-permute-start = (bf16[128,1024]{0,1:T(8,128)(2,1)S(1)}, bf16[128,1024]{0,1:T(8,128)(2,1)}, u32[]{:S(2)}, u32[]{:S(2)}) collective-permute-start(bf16[128,1024]{0,1:T(8,128)(2,1)S(1)} %pad_maximum_fusion), channel_id=1, source_target_pairs={{0,16},{2,18},{4,20},{6,22},{8,24},{10,26},{12,28},{14,30},{16,32}... | collective-permute-start | bytes 786440 | tf_op jit(solution)/shard_map/ppermute | solution.py:19
  18.5 4.6 %collective-permute-start.1 = (bf16[128,1024]{0,1:T(8,128)(2,1)S(1)}, bf16[128,1024]{0,1:T(8,128)(2,1)}, u32[]{:S(2)}, u32[]{:S(2)}) collective-permute-start(bf16[128,1024]{0,1:T(8,128)(2,1)S(1)} %pad_maximum_fusion), channel_id=1, source_target_pairs={{0,14},{2,16},{4,18},{6,20},{8,22},{10,24},{12,26},{14,28},{16,30}... | collective-permute-start | bytes 786440 | tf_op jit(solution)/shard_map/ppermute | solution.py:19
  23.1 3.8 %collective-permute-start.2 = (bf16[128,1024]{0,1:T(8,128)(2,1)S(1)}, bf16[128,1024]{0,1:T(8,128)(2,1)}, u32[]{:S(2)}, u32[]{:S(2)}) collective-permute-start(bf16[128,1024]{0,1:T(8,128)(2,1)S(1)} %pad_maximum_fusion), channel_id=1, source_target_pairs={{0,12},{2,14},{4,16},{6,18},{8,20},{10,22},{12,24},{14,26},{16,28}... | collective-permute-start | bytes 786440 | tf_op jit(solution)/shard_map/ppermute | solution.py:19
  26.8 3.3 %collective-permute-start.3 = (bf16[128,1024]{0,1:T(8,128)(2,1)S(1)}, bf16[128,1024]{0,1:T(8,128)(2,1)}, u32[]{:S(2)}, u32[]{:S(2)}) collective-permute-start(bf16[128,1024]{0,1:T(8,128)(2,1)S(1)} %pad_maximum_fusion), channel_id=1, source_target_pairs={{0,10},{2,12},{4,14},{6,16},{8,18},{10,20},{12,22},{14,24},{16,26}... | collective-permute-start | bytes 786440 | tf_op jit(solution)/shard_map/ppermute | solution.py:19
  30.1 2.7 %collective-permute-start.8 = (bf16[128,2688]{1,0:T(8,128)(2,1)}, bf16[128,2688]{1,0:T(8,128)(2,1)}, u32[]{:S(2)}, u32[]{:S(2)}) collective-permute-start(bf16[128,2688]{1,0:T(8,128)(2,1)} %param.12), channel_id=1, source_target_pairs={{0,1},{1,0},{2,3},{3,2},{4,5},{5,4},{6,7},{7,6},{8,9},{9,8},{10,11... | collective-permute-start | bytes 2064392 | tf_op jit(solution)/shard_map/ppermute | solution.py:94
  35.4 4.6 %collective-permute-start.4 = (bf16[128,1024]{0,1:T(8,128)(2,1)S(1)}, bf16[128,1024]{0,1:T(8,128)(2,1)}, u32[]{:S(2)}, u32[]{:S(2)}) collective-permute-start(bf16[128,1024]{0,1:T(8,128)(2,1)S(1)} %pad_maximum_fusion), channel_id=1, source_target_pairs={{0,8},{2,10},{4,12},{6,14},{8,16},{10,18},{12,20},{14,22},{16,24},... | collective-permute-start | bytes 786440 | tf_op jit(solution)/shard_map/ppermute | solution.py:19
  45.3 3.2 %collective-permute-start.6 = (bf16[128,1024]{0,1:T(8,128)(2,1)S(1)}, bf16[128,1024]{0,1:T(8,128)(2,1)}, u32[]{:S(2)}, u32[]{:S(2)}) collective-permute-start(bf16[128,1024]{0,1:T(8,128)(2,1)S(1)} %pad_maximum_fusion), channel_id=1, source_target_pairs={{0,4},{2,6},{4,8},{6,10},{8,12},{10,14},{12,16},{14,18},{16,20},{1... | collective-permute-start | bytes 786440 | tf_op jit(solution)/shard_map/ppermute | solution.py:19
  50.2 3.5 %collective-permute-start.7 = (bf16[128,1024]{0,1:T(8,128)(2,1)S(1)}, bf16[128,1024]{0,1:T(8,128)(2,1)}, u32[]{:S(2)}, u32[]{:S(2)}) collective-permute-start(bf16[128,1024]{0,1:T(8,128)(2,1)S(1)} %pad_maximum_fusion), channel_id=1, source_target_pairs={{0,2},{2,4},{4,6},{6,8},{8,10},{10,12},{12,14},{14,16},{16,18},{18... | collective-permute-start | bytes 786440 | tf_op jit(solution)/shard_map/ppermute | solution.py:19
  56.5 9.8 %all-to-all-start = ((bf16[8,128,672]{1,2,0:T(8,128)(2,1)}), bf16[8,128,672]{1,2,0:T(8,128)(2,1)}, u32[]{:S(2)}, u32[]{:S(2)}) async-start(bf16[8,128,672]{1,2,0:T(8,128)(2,1)} %fusion.60), calls=%async_computation | async-start | bytes 2752512 | tf_op jit(solution)/shard_map/all_to_all | solution.py:108
  72.2 6.0 %collective-permute-done.6 = bf16[128,1024]{0,1:T(8,128)(2,1)} collective-permute-done((bf16[128,1024]{0,1:T(8,128)(2,1)S(1)}, bf16[128,1024]{0,1:T(8,128)(2,1)}, u32[]{:S(2)}, u32[]{:S(2)}) %collective-permute-start.6) | collective-permute-done | bytes 262176 | tf_op jit(solution)/shard_map/ppermute | solution.py:19
  85.2 2.3 reshape.101
  87.5 5.0 %convolution_convert_fusion.1 = bf16[8,128,1024]{2,1,0:T(8,128)(2,1)} fusion(bf16[8,128,672]{1,2,0:T(8,128)(2,1)} %all-to-all-done, bf16[672,1024,1]{1,0,2:T(8,128)(2,1)} %reshape.101), kind=kOutput, calls=%fused_computation.74 | convolution fusion | flops 1410334720 | bytes 4849664 | tf_op jit(solution)/shard_map/btk,kh->bth/dot_general | solution.py:109
  92.5 13.3 %all-to-all-start.2 = ((bf16[8,128,1024]{2,1,0:T(8,128)(2,1)}), bf16[8,128,1024]{2,1,0:T(8,128)(2,1)}, u32[]{:S(2)}, u32[]{:S(2)}) async-start(bf16[8,128,1024]{2,1,0:T(8,128)(2,1)} %convolution_convert_fusion.1), calls=%async_computation.2 | async-start | bytes 4194304 | tf_op jit(solution)/shard_map/all_to_all | solution.py:113
  105.8 7.3 %while.28 = (s32[]{:T(128)}, bf16[4,128,2,128]{1,3,2,0:T(8,128)(2,1)S(1)}, f32[4,2,128]{2,1,0:T(2,128)S(1)}, bf16[4,1152,128]{1,2,0:T(8,128)(2,1)S(1)}, bf16[4,1...) while((s32[]{:T(128)}, ...), condition=%wide.region_4.5_spmd.clone, body=%wide.region_1.0_spmd.clone.sunk | while | flops 153829120 | bytes 4571369 | solution.py:88
  114.1 13.0 %all-to-all-done.2 = bf16[8,128,1024]{2,1,0:T(8,128)(2,1)} async-done(((bf16[8,128,1024]{2,1,0:T(8,128)(2,1)}), bf16[8,128,1024]{2,1,0:T(8,128)(2,1)}, u32[]{:S(2)}, u32[]{:S(2)}) %all-to-all-start.2) | async-done | bytes 2097184 | tf_op jit(solution)/shard_map/all_to_all | solution.py:113
  127.1 2.0 reduce_sum.30
  129.3 20.0 %while.29 = (s32[]{:T(128)}, bf16[4,128,2,128]{1,3,2,0:T(8,128)(2,1)}, f32[4,1152,128]{2,1,0:T(8,128)}, f32[4,1152,128]{2,1,0:T(8,128)}, bf16[4,1152,128]{2,1,0:...) while((s32[]{:T(128)}, ...), condition=%wide.region_7.8_spmd.clone, body=%wide.region_6.7_spmd.clone.sunk | while | flops 380469248 | bytes 10175813 | solution.py:124
  149.3 2.2 bitcast_dynamic-update-slice_fusion.1
  155.4 28.3 %all-gather.2.cloned.1.call-done = bf16[1024,1024]{0,1:T(8,128)(2,1)} async-done(((bf16[128,1024]{0,1:T(8,128)(2,1)}), bf16[1024,1024]{0,1:T(8,128)(2,1)}) %all-gather.2.cloned.1.call-update) | async-done | bytes 2097168 | tf_op jit(solution)/shard_map/all_gather | solution.py:119
  186.4 4.9 %multiply_bitcast_fusion = f32[8,1024,84]{1,2,0:T(8,128)} fusion(bf16[1024,8,84]{0,2,1:T(8,128)(2,1)S(1)} %reshape.93, bf16[1024,1024]{0,1:T(8,128)(2,1)} %all-gather.2.cloned.1.call-done), kind=kOutput, calls=%fused_computation.69 | convolution fusion | flops 1409974272 | bytes 6225920 | tf_op jit(solution)/shard_map/th,tqk->qhk/dot_general | solution.py:143
  192.2 11.8 %collective-permute-start.10 = (bf16[128,1024]{1,0:T(8,128)(2,1)S(1)}, bf16[128,1024]{1,0:T(8,128)(2,1)S(1)}, u32[]{:S(2)}, u32[]{:S(2)}) collective-permute-start(bf16[128,1024]{1,0:T(8,128)(2,1)S(1)} %copy-done.12), channel_id=1, source_target_pairs={{4,0},{6,2},{8,4},{10,6},{12,8},{14,10},{16,12},{18,14},{20,16},{2... | collective-permute-start | bytes 786440 | tf_op jit(solution)/shard_map/ppermute | solution.py:19
  204.0 1.9 collective-permute-start.11
  206.0 1.9 collective-permute-start.12
  207.9 1.9 collective-permute-start.13
  209.8 1.9 collective-permute-start.14
  211.8 1.9 collective-permute-start.15
  213.7 3.3 %collective-permute-done.11 = bf16[128,1024]{1,0:T(8,128)(2,1)S(1)} collective-permute-done((bf16[128,1024]{1,0:T(8,128)(2,1)S(1)}, bf16[128,1024]{1,0:T(8,128)(2,1)S(1)}, u32[]{:S(2)}, u32[]{:S(2)}) %collective-permute-start.11) | collective-permute-done | bytes 262176 | tf_op jit(solution)/shard_map/ppermute | solution.py:19
  218.9 13.5 %collective-permute-done.12 = bf16[128,1024]{1,0:T(8,128)(2,1)S(1)} collective-permute-done((bf16[128,1024]{1,0:T(8,128)(2,1)S(1)}, bf16[128,1024]{1,0:T(8,128)(2,1)S(1)}, u32[]{:S(2)}, u32[]{:S(2)}) %collective-permute-start.12) | collective-permute-done | bytes 262176 | tf_op jit(solution)/shard_map/ppermute | solution.py:19
  236.8 4.7 %collective-permute-done.15 = bf16[128,1024]{1,0:T(8,128)(2,1)S(1)} collective-permute-done((bf16[128,1024]{1,0:T(8,128)(2,1)S(1)}, bf16[128,1024]{1,0:T(8,128)(2,1)S(1)}, u32[]{:S(2)}, u32[]{:S(2)}) %collective-permute-start.15) | collective-permute-done | bytes 262176 | tf_op jit(solution)/shard_map/ppermute | solution.py:19
  241.5 9.1 %collective-permute-done.16 = bf16[128,1024]{1,0:T(8,128)(2,1)S(1)} collective-permute-done((bf16[128,1024]{1,0:T(8,128)(2,1)S(1)}, bf16[128,1024]{1,0:T(8,128)(2,1)S(1)}, u32[]{:S(2)}, u32[]{:S(2)}) %collective-permute-start.16) | collective-permute-done | bytes 262176 | tf_op jit(solution)/shard_map/ppermute | solution.py:19
  (163 shorter events, 71.0 us)
Async XLA Ops:
  9.4 24.9 %copy-start.13 = (bf16[128,1024]{1,0:T(8,128)(2,1)S(1)}, bf16[128,1024]{1,0:T(8,128)(2,1)}, u32[]{:S(2)}) copy-start(bf16[128,1024]{1,0:T(8,128)(2,1)} %param.9) | copy-start | bytes 786436
  9.4 47.0 %all-to-all-start.1 = ((bf16[8,84,1024]{2,1,0:T(8,128)(2,1)}), bf16[8,84,1024]{2,1,0:T(8,128)(2,1)S(1)}, u32[]{:S(2)}, u32[]{:S(2)}) async-start(bf16[8,84,1024]{2,1,0:T(8,128)(2,1)} %broadcast_in_dim.63), calls=%async_computation.1 | async-start | bytes 2883584 | tf_op jit(solution)/shard_map/all_to_all | solution.py:104
  15.2 20.2 %collective-permute-start = (bf16[128,1024]{0,1:T(8,128)(2,1)S(1)}, bf16[128,1024]{0,1:T(8,128)(2,1)}, u32[]{:S(2)}, u32[]{:S(2)}) collective-permute-start(bf16[128,1024]{0,1:T(8,128)(2,1)S(1)} %pad_maximum_fusion), channel_id=1, source_target_pairs={{0,16},{2,18},{4,20},{6,22},{8,24},{10,26},{12,28},{14,30},{16,32}... | collective-permute-start | bytes 786440 | tf_op jit(solution)/shard_map/ppermute | solution.py:19
  18.5 23.2 %collective-permute-start.1 = (bf16[128,1024]{0,1:T(8,128)(2,1)S(1)}, bf16[128,1024]{0,1:T(8,128)(2,1)}, u32[]{:S(2)}, u32[]{:S(2)}) collective-permute-start(bf16[128,1024]{0,1:T(8,128)(2,1)S(1)} %pad_maximum_fusion), channel_id=1, source_target_pairs={{0,14},{2,16},{4,18},{6,20},{8,22},{10,24},{12,26},{14,28},{16,30}... | collective-permute-start | bytes 786440 | tf_op jit(solution)/shard_map/ppermute | solution.py:19
  23.1 22.3 %collective-permute-start.2 = (bf16[128,1024]{0,1:T(8,128)(2,1)S(1)}, bf16[128,1024]{0,1:T(8,128)(2,1)}, u32[]{:S(2)}, u32[]{:S(2)}) collective-permute-start(bf16[128,1024]{0,1:T(8,128)(2,1)S(1)} %pad_maximum_fusion), channel_id=1, source_target_pairs={{0,12},{2,14},{4,16},{6,18},{8,20},{10,22},{12,24},{14,26},{16,28}... | collective-permute-start | bytes 786440 | tf_op jit(solution)/shard_map/ppermute | solution.py:19
  26.8 39.4 %collective-permute-start.3 = (bf16[128,1024]{0,1:T(8,128)(2,1)S(1)}, bf16[128,1024]{0,1:T(8,128)(2,1)}, u32[]{:S(2)}, u32[]{:S(2)}) collective-permute-start(bf16[128,1024]{0,1:T(8,128)(2,1)S(1)} %pad_maximum_fusion), channel_id=1, source_target_pairs={{0,10},{2,12},{4,14},{6,16},{8,18},{10,20},{12,22},{14,24},{16,26}... | collective-permute-start | bytes 786440 | tf_op jit(solution)/shard_map/ppermute | solution.py:19
  30.1 20.1 %collective-permute-start.8 = (bf16[128,2688]{1,0:T(8,128)(2,1)}, bf16[128,2688]{1,0:T(8,128)(2,1)}, u32[]{:S(2)}, u32[]{:S(2)}) collective-permute-start(bf16[128,2688]{1,0:T(8,128)(2,1)} %param.12), channel_id=1, source_target_pairs={{0,1},{1,0},{2,3},{3,2},{4,5},{5,4},{6,7},{7,6},{8,9},{9,8},{10,11... | collective-permute-start | bytes 2064392 | tf_op jit(solution)/shard_map/ppermute | solution.py:94
  35.4 32.6 %collective-permute-start.4 = (bf16[128,1024]{0,1:T(8,128)(2,1)S(1)}, bf16[128,1024]{0,1:T(8,128)(2,1)}, u32[]{:S(2)}, u32[]{:S(2)}) collective-permute-start(bf16[128,1024]{0,1:T(8,128)(2,1)S(1)} %pad_maximum_fusion), channel_id=1, source_target_pairs={{0,8},{2,10},{4,12},{6,14},{8,16},{10,18},{12,20},{14,22},{16,24},... | collective-permute-start | bytes 786440 | tf_op jit(solution)/shard_map/ppermute | solution.py:19
  41.7 28.8 %collective-permute-start.5 = (bf16[128,1024]{0,1:T(8,128)(2,1)S(1)}, bf16[128,1024]{0,1:T(8,128)(2,1)}, u32[]{:S(2)}, u32[]{:S(2)}) collective-permute-start(bf16[128,1024]{0,1:T(8,128)(2,1)S(1)} %pad_maximum_fusion), channel_id=1, source_target_pairs={{0,6},{2,8},{4,10},{6,12},{8,14},{10,16},{12,18},{14,20},{16,22},{... | collective-permute-start | bytes 786440 | tf_op jit(solution)/shard_map/ppermute | solution.py:19
  45.3 32.9 %collective-permute-start.6 = (bf16[128,1024]{0,1:T(8,128)(2,1)S(1)}, bf16[128,1024]{0,1:T(8,128)(2,1)}, u32[]{:S(2)}, u32[]{:S(2)}) collective-permute-start(bf16[128,1024]{0,1:T(8,128)(2,1)S(1)} %pad_maximum_fusion), channel_id=1, source_target_pairs={{0,4},{2,6},{4,8},{6,10},{8,12},{10,14},{12,16},{14,18},{16,20},{1... | collective-permute-start | bytes 786440 | tf_op jit(solution)/shard_map/ppermute | solution.py:19
  50.2 29.9 %collective-permute-start.7 = (bf16[128,1024]{0,1:T(8,128)(2,1)S(1)}, bf16[128,1024]{0,1:T(8,128)(2,1)}, u32[]{:S(2)}, u32[]{:S(2)}) collective-permute-start(bf16[128,1024]{0,1:T(8,128)(2,1)S(1)} %pad_maximum_fusion), channel_id=1, source_target_pairs={{0,2},{2,4},{4,6},{6,8},{8,10},{10,12},{12,14},{14,16},{16,18},{18... | collective-permute-start | bytes 786440 | tf_op jit(solution)/shard_map/ppermute | solution.py:19
  56.5 15.8 %copy-start.1 = (bf16[8,84,1024]{2,1,0:T(8,128)(2,1)}, bf16[8,84,1024]{2,1,0:T(8,128)(2,1)S(1)}, u32[]{:S(2)}) copy-start(bf16[8,84,1024]{2,1,0:T(8,128)(2,1)S(1)} %all-to-all-done.1) | copy-start | bytes 4128772
  56.5 31.0 %all-to-all-start = ((bf16[8,128,672]{1,2,0:T(8,128)(2,1)}), bf16[8,128,672]{1,2,0:T(8,128)(2,1)}, u32[]{:S(2)}, u32[]{:S(2)}) async-start(bf16[8,128,672]{1,2,0:T(8,128)(2,1)} %fusion.60), calls=%async_computation | async-start | bytes 2752512 | tf_op jit(solution)/shard_map/all_to_all | solution.py:108
  92.5 13.3 %copy-start.4 = (bf16[4,128,2,128]{1,3,2,0:T(8,128)(2,1)S(1)}, bf16[4,128,2,128]{1,3,2,0:T(8,128)(2,1)}, u32[]{:S(2)}) copy-start(bf16[4,128,2,128]{1,3,2,0:T(8,128)(2,1)} %custom-call.2) | copy-start | bytes 786436
  92.5 13.3 %copy-start.19 = (f32[4,2,128]{2,1,0:T(2,128)S(1)}, f32[4,2,128]{2,1,0:T(2,128)}, u32[]{:S(2)}) copy-start(f32[4,2,128]{2,1,0:T(2,128)} %custom-call.3) | copy-start | bytes 12292
  92.5 34.6 %all-to-all-start.2 = ((bf16[8,128,1024]{2,1,0:T(8,128)(2,1)}), bf16[8,128,1024]{2,1,0:T(8,128)(2,1)}, u32[]{:S(2)}, u32[]{:S(2)}) async-start(bf16[8,128,1024]{2,1,0:T(8,128)(2,1)} %convolution_convert_fusion.1), calls=%async_computation.2 | async-start | bytes 4194304 | tf_op jit(solution)/shard_map/all_to_all | solution.py:113
  105.7 78.0 %all-gather.2.cloned.1.call-start = ((), (), s32[]{:S(2)}) async-start(), calls=%async_computation.4 | async-start | bytes 2359296 | tf_op jit(solution)/shard_map/all_gather | solution.py:119
  113.8 15.4 %copy-start.6 = (bf16[4,128,2,128]{1,3,2,0:T(8,128)(2,1)S(1)}, bf16[4,128,2,128]{1,3,2,0:T(8,128)(2,1)}, u32[]{:S(2)}) copy-start(bf16[4,128,2,128]{1,3,2,0:T(8,128)(2,1)} %copy-done.5) | copy-start | bytes 786436
  113.9 140.3 %reduce-scatter.2.cloned.1.call-start = ((), (), s32[]{:S(2)}) async-start(), calls=%async_computation.5 | async-start | bytes 3244032 | tf_op jit(solution)/shard_map/reduce_scatter | solution.py:149
  191.3 14.7 %copy-start.10 = (bf16[128,1024]{1,0:T(8,128)(2,1)S(1)}, bf16[128,1024]{1,0:T(8,128)(2,1)}, u32[]{:S(2)}) copy-start(bf16[128,1024]{1,0:T(8,128)(2,1)} %get-tuple-element.270) | copy-start | bytes 786436
  191.3 16.6 %copy-start.9 = (bf16[128,1024]{1,0:T(8,128)(2,1)S(1)}, bf16[128,1024]{1,0:T(8,128)(2,1)}, u32[]{:S(2)}) copy-start(bf16[128,1024]{1,0:T(8,128)(2,1)} %get-tuple-element.269) | copy-start | bytes 786436
  191.3 18.6 %copy-start.8 = (bf16[128,1024]{1,0:T(8,128)(2,1)S(1)}, bf16[128,1024]{1,0:T(8,128)(2,1)}, u32[]{:S(2)}) copy-start(bf16[128,1024]{1,0:T(8,128)(2,1)} %get-tuple-element.268) | copy-start | bytes 786436
  191.3 20.5 %copy-start.7 = (bf16[128,1024]{1,0:T(8,128)(2,1)S(1)}, bf16[128,1024]{1,0:T(8,128)(2,1)}, u32[]{:S(2)}) copy-start(bf16[128,1024]{1,0:T(8,128)(2,1)} %get-tuple-element.267) | copy-start | bytes 786436
  191.3 43.0 %copy-start.16 = (bf16[4,128,2,128]{1,3,2,0:T(8,128)(2,1)S(1)}, bf16[4,128,2,128]{1,3,2,0:T(8,128)(2,1)}, u32[]{:S(2)}) copy-start(bf16[4,128,2,128]{1,3,2,0:T(8,128)(2,1)} %get-tuple-element.105) | copy-start | bytes 786436
  192.2 19.6 %collective-permute-start.10 = (bf16[128,1024]{1,0:T(8,128)(2,1)S(1)}, bf16[128,1024]{1,0:T(8,128)(2,1)S(1)}, u32[]{:S(2)}, u32[]{:S(2)}) collective-permute-start(bf16[128,1024]{1,0:T(8,128)(2,1)S(1)} %copy-done.12), channel_id=1, source_target_pairs={{4,0},{6,2},{8,4},{10,6},{12,8},{14,10},{16,12},{18,14},{20,16},{2... | collective-permute-start | bytes 786440 | tf_op jit(solution)/shard_map/ppermute | solution.py:19
  204.0 13.0 %collective-permute-start.11 = (bf16[128,1024]{1,0:T(8,128)(2,1)S(1)}, bf16[128,1024]{1,0:T(8,128)(2,1)S(1)}, u32[]{:S(2)}, u32[]{:S(2)}) collective-permute-start(bf16[128,1024]{1,0:T(8,128)(2,1)S(1)} %copy-done.11), channel_id=1, source_target_pairs={{6,0},{8,2},{10,4},{12,6},{14,8},{16,10},{18,12},{20,14},{22,16},{... | collective-permute-start | bytes 786440 | tf_op jit(solution)/shard_map/ppermute | solution.py:19
  206.0 26.4 %collective-permute-start.12 = (bf16[128,1024]{1,0:T(8,128)(2,1)S(1)}, bf16[128,1024]{1,0:T(8,128)(2,1)S(1)}, u32[]{:S(2)}, u32[]{:S(2)}) collective-permute-start(bf16[128,1024]{1,0:T(8,128)(2,1)S(1)} %copy-done.10), channel_id=1, source_target_pairs={{8,0},{10,2},{12,4},{14,6},{16,8},{18,10},{20,12},{22,14},{24,16},... | collective-permute-start | bytes 786440 | tf_op jit(solution)/shard_map/ppermute | solution.py:19
  207.9 28.9 %collective-permute-start.13 = (bf16[128,1024]{1,0:T(8,128)(2,1)S(1)}, bf16[128,1024]{1,0:T(8,128)(2,1)}, u32[]{:S(2)}, u32[]{:S(2)}) collective-permute-start(bf16[128,1024]{1,0:T(8,128)(2,1)S(1)} %copy-done.9), channel_id=1, source_target_pairs={{10,0},{12,2},{14,4},{16,6},{18,8},{20,10},{22,12},{24,14},{26,16}... | collective-permute-start | bytes 786440 | tf_op jit(solution)/shard_map/ppermute | solution.py:19
  209.8 27.0 %collective-permute-start.14 = (bf16[128,1024]{1,0:T(8,128)(2,1)S(1)}, bf16[128,1024]{1,0:T(8,128)(2,1)}, u32[]{:S(2)}, u32[]{:S(2)}) collective-permute-start(bf16[128,1024]{1,0:T(8,128)(2,1)S(1)} %copy-done.8), channel_id=1, source_target_pairs={{12,0},{14,2},{16,4},{18,6},{20,8},{22,10},{24,12},{26,14},{28,16}... | collective-permute-start | bytes 786440 | tf_op jit(solution)/shard_map/ppermute | solution.py:19
  211.8 29.8 %collective-permute-start.15 = (bf16[128,1024]{1,0:T(8,128)(2,1)S(1)}, bf16[128,1024]{1,0:T(8,128)(2,1)S(1)}, u32[]{:S(2)}, u32[]{:S(2)}) collective-permute-start(bf16[128,1024]{1,0:T(8,128)(2,1)S(1)} %copy-done.7), channel_id=1, source_target_pairs={{14,0},{16,2},{18,4},{20,6},{22,8},{24,10},{26,12},{28,14},{30,16}... | collective-permute-start | bytes 786440 | tf_op jit(solution)/shard_map/ppermute | solution.py:19
  217.0 33.6 %collective-permute-start.16 = (bf16[128,1024]{1,0:T(8,128)(2,1)S(1)}, bf16[128,1024]{1,0:T(8,128)(2,1)S(1)}, u32[]{:S(2)}, u32[]{:S(2)}) collective-permute-start(bf16[128,1024]{1,0:T(8,128)(2,1)S(1)} %get-tuple-element.266), channel_id=1, source_target_pairs={{16,0},{18,2},{20,4},{22,6},{24,8},{26,10},{28,12},{30,14},{32,16}... | collective-permute-start | bytes 786440 | tf_op jit(solution)/shard_map/ppermute | solution.py:19
  232.4 18.2 %collective-permute-start.9 = (bf16[128,1024]{1,0:T(8,128)(2,1)S(1)}, bf16[128,1024]{1,0:T(8,128)(2,1)S(1)}, u32[]{:S(2)}, u32[]{:S(2)}) collective-permute-start(bf16[128,1024]{1,0:T(8,128)(2,1)S(1)} %get-tuple-element.265), channel_id=1, source_target_pairs={{2,0},{4,2},{6,4},{8,6},{10,8},{12,10},{14,12},{16,14},{18,16},{20... | collective-permute-start | bytes 786440 | tf_op jit(solution)/shard_map/ppermute | solution.py:19
  (16 other events, 61.4 us)
Sparse Core Ops, SparseCore 0:
  114.0 69.7 all-gather.1
  191.4 62.6 reduce-scatter.1

commit v5 on v4

--- a/solution.py
+++ b/solution.py
@@ -136,7 +136,7 @@
         for offset in range(1, reach_count + 1)
     ]
     sent = [block.astype(jnp.bfloat16) for block in sent]
-    for offset in range(1, reach_count + 1):
+    for offset in range(reach_count, 0, -1):
         arrived = from_behind(sent[offset - 1], ("cg", "cp"), -offset)
         pair_total = pair_total + arrived.astype(jnp.float32)
     group_probs, group_columns, sent = lax.optimization_barrier((group_probs, group_columns, sent))
@@ -146,7 +146,8 @@
         group_columns.reshape(group_count * tokens_dev, group_size, block),
         preferred_element_type=jnp.float32,
     ) * (tokens_dev * n_ctx) ** (-0.5)
-    weight_grad = lax.psum_scatter(weight_term, "cp", scatter_dimension=0, tiled=True)[0]
+    weight_parts = lax.all_to_all(weight_term.astype(jnp.bfloat16), "cp", 0, 0, tiled=True)
+    weight_grad = jnp.sum(weight_parts.astype(jnp.float32), 0)
     key_total = pair_total[:, :kv_width]
     value_total = pair_total[:, kv_width:]
     query_grad = query_parts.transpose(1, 0, 2, 3).reshape(tokens_dev, -1).astype(jnp.bfloat16)

time: 266 us -> 264 us (level)
  waiting for transfers between devices: 81.8 us -> 70.6 us
  starting transfers between devices: 84.7 us -> 95.2 us
    ppermute x16, waiting for transfers between devices: 39.2 us -> 29 us  [from_behind(): return lax.ppermute(block, axis, route)]
    all_to_all x0 -> x1, starting transfers between devices: none -> 9.85 us  [device_body(): lax.all_to_all(weight_term.astype(jnp.bfloat16), 'cp', 0, 0, tiled=True)]
    unnamed x51 -> x53, local copies, waits for them, and re-layouts: 23 us -> 22.1 us
  transfers between devices with their start and end apart: 22 -> 22, of which waited for: 11 -> 9; matrix products, arithmetic and copies ran while one was open for 22% -> 23% of each run, Pallas kernels for 0% -> 0%
where the time goes in v5:
time: 264 us; the launch traced here: 261 us
  starting transfers between devices  95.2 us (36%)
  waiting for transfers between devices  70.6 us (27%)
  local copies, waits for them, and re-layouts  39.6 us (15%)
  matrix products  25.7 us (10%)
  other arithmetic  15 us (6%)
  between operations  14.5 us (5%)
    ppermute x16, starting transfers between devices, from_behind(): return lax.ppermute(block, axis, route)  54.1 us
    ppermute x16, waiting for transfers between devices, from_behind(): return lax.ppermute(block, axis, route)  29 us
    all_gather x1, waiting for transfers between devices, device_body(): group_probs = lax.all_gather(attention_probs, 'cg', axis=0, tiled=True)  28.4 us
    unnamed x53, local copies, waits for them, and re-layouts  22.1 us
    all_to_all x1, starting transfers between devices, device_body(): lax.all_to_all(partial_grads.astype(jnp.bfloat16), 'cg', 0, 0, tiled=True)  13.3 us
    all_to_all x1, waiting for transfers between devices, device_body(): lax.all_to_all(partial_grads.astype(jnp.bfloat16), 'cg', 0, 0, tiled=True)  13.2 us
    all_to_all x1, starting transfers between devices, device_body(): lax.all_to_all(weight_term.astype(jnp.bfloat16), 'cp', 0, 0, tiled=True)  9.85 us
    all_to_all x1, starting transfers between devices, device_body(): group_columns = lax.all_to_all(by_group, 'cg', 0, 0, tiled=True)  9.79 us
  transfers between devices with their start and end apart: 22, of which 9 were waited for; matrix products, arithmetic and copies ran while one was open for 23% of the time, Pallas kernels for 0%

profile of v5, /device:TPU:8, one launch (start us, length us, event | category | flops | bytes accessed | tf_op | source)
XLA Modules:
  0.0 261.0 jit_solution(9234096265029561537)
XLA Ops:
  7.2 2.2 broadcast_in_dim.63
  9.4 5.4 %all-to-all-start.1 = ((bf16[8,84,1024]{2,1,0:T(8,128)(2,1)}), bf16[8,84,1024]{2,1,0:T(8,128)(2,1)S(1)}, u32[]{:S(2)}, u32[]{:S(2)}) async-start(bf16[8,84,1024]{2,1,0:T(8,128)(2,1)} %broadcast_in_dim.63), calls=%async_computation.1 | async-start | bytes 2883584 | tf_op jit(solution)/shard_map/all_to_all | solution.py:104
  15.1 3.3 %collective-permute-start = (bf16[128,1024]{0,1:T(8,128)(2,1)S(1)}, bf16[128,1024]{0,1:T(8,128)(2,1)}, u32[]{:S(2)}, u32[]{:S(2)}) collective-permute-start(bf16[128,1024]{0,1:T(8,128)(2,1)S(1)} %pad_maximum_fusion), channel_id=1, source_target_pairs={{0,16},{2,18},{4,20},{6,22},{8,24},{10,26},{12,28},{14,30},{16,32}... | collective-permute-start | bytes 786440 | tf_op jit(solution)/shard_map/ppermute | solution.py:19
  18.4 4.6 %collective-permute-start.1 = (bf16[128,1024]{0,1:T(8,128)(2,1)S(1)}, bf16[128,1024]{0,1:T(8,128)(2,1)}, u32[]{:S(2)}, u32[]{:S(2)}) collective-permute-start(bf16[128,1024]{0,1:T(8,128)(2,1)S(1)} %pad_maximum_fusion), channel_id=1, source_target_pairs={{0,14},{2,16},{4,18},{6,20},{8,22},{10,24},{12,26},{14,28},{16,30}... | collective-permute-start | bytes 786440 | tf_op jit(solution)/shard_map/ppermute | solution.py:19
  23.0 3.8 %collective-permute-start.2 = (bf16[128,1024]{0,1:T(8,128)(2,1)S(1)}, bf16[128,1024]{0,1:T(8,128)(2,1)}, u32[]{:S(2)}, u32[]{:S(2)}) collective-permute-start(bf16[128,1024]{0,1:T(8,128)(2,1)S(1)} %pad_maximum_fusion), channel_id=1, source_target_pairs={{0,12},{2,14},{4,16},{6,18},{8,20},{10,22},{12,24},{14,26},{16,28}... | collective-permute-start | bytes 786440 | tf_op jit(solution)/shard_map/ppermute | solution.py:19
  26.8 3.3 %collective-permute-start.3 = (bf16[128,1024]{0,1:T(8,128)(2,1)S(1)}, bf16[128,1024]{0,1:T(8,128)(2,1)}, u32[]{:S(2)}, u32[]{:S(2)}) collective-permute-start(bf16[128,1024]{0,1:T(8,128)(2,1)S(1)} %pad_maximum_fusion), channel_id=1, source_target_pairs={{0,10},{2,12},{4,14},{6,16},{8,18},{10,20},{12,22},{14,24},{16,26}... | collective-permute-start | bytes 786440 | tf_op jit(solution)/shard_map/ppermute | solution.py:19
  30.1 2.7 %collective-permute-start.8 = (bf16[128,2688]{1,0:T(8,128)(2,1)}, bf16[128,2688]{1,0:T(8,128)(2,1)}, u32[]{:S(2)}, u32[]{:S(2)}) collective-permute-start(bf16[128,2688]{1,0:T(8,128)(2,1)} %param.12), channel_id=1, source_target_pairs={{0,1},{1,0},{2,3},{3,2},{4,5},{5,4},{6,7},{7,6},{8,9},{9,8},{10,11... | collective-permute-start | bytes 2064392 | tf_op jit(solution)/shard_map/ppermute | solution.py:94
  35.3 4.6 %collective-permute-start.4 = (bf16[128,1024]{0,1:T(8,128)(2,1)S(1)}, bf16[128,1024]{0,1:T(8,128)(2,1)}, u32[]{:S(2)}, u32[]{:S(2)}) collective-permute-start(bf16[128,1024]{0,1:T(8,128)(2,1)S(1)} %pad_maximum_fusion), channel_id=1, source_target_pairs={{0,8},{2,10},{4,12},{6,14},{8,16},{10,18},{12,20},{14,22},{16,24},... | collective-permute-start | bytes 786440 | tf_op jit(solution)/shard_map/ppermute | solution.py:19
  45.3 3.2 %collective-permute-start.6 = (bf16[128,1024]{0,1:T(8,128)(2,1)S(1)}, bf16[128,1024]{0,1:T(8,128)(2,1)}, u32[]{:S(2)}, u32[]{:S(2)}) collective-permute-start(bf16[128,1024]{0,1:T(8,128)(2,1)S(1)} %pad_maximum_fusion), channel_id=1, source_target_pairs={{0,4},{2,6},{4,8},{6,10},{8,12},{10,14},{12,16},{14,18},{16,20},{1... | collective-permute-start | bytes 786440 | tf_op jit(solution)/shard_map/ppermute | solution.py:19
  50.2 3.5 %collective-permute-start.7 = (bf16[128,1024]{0,1:T(8,128)(2,1)S(1)}, bf16[128,1024]{0,1:T(8,128)(2,1)}, u32[]{:S(2)}, u32[]{:S(2)}) collective-permute-start(bf16[128,1024]{0,1:T(8,128)(2,1)S(1)} %pad_maximum_fusion), channel_id=1, source_target_pairs={{0,2},{2,4},{4,6},{6,8},{8,10},{10,12},{12,14},{14,16},{16,18},{18... | collective-permute-start | bytes 786440 | tf_op jit(solution)/shard_map/ppermute | solution.py:19
  56.4 9.8 %all-to-all-start = ((bf16[8,128,672]{1,2,0:T(8,128)(2,1)}), bf16[8,128,672]{1,2,0:T(8,128)(2,1)}, u32[]{:S(2)}, u32[]{:S(2)}) async-start(bf16[8,128,672]{1,2,0:T(8,128)(2,1)} %fusion.63), calls=%async_computation | async-start | bytes 2752512 | tf_op jit(solution)/shard_map/all_to_all | solution.py:108
  72.2 6.0 %collective-permute-done.6 = bf16[128,1024]{0,1:T(8,128)(2,1)} collective-permute-done((bf16[128,1024]{0,1:T(8,128)(2,1)S(1)}, bf16[128,1024]{0,1:T(8,128)(2,1)}, u32[]{:S(2)}, u32[]{:S(2)}) %collective-permute-start.6) | collective-permute-done | bytes 262176 | tf_op jit(solution)/shard_map/ppermute | solution.py:19
  85.1 2.3 reshape.101
  87.4 5.0 %convolution_convert_fusion.1 = bf16[8,128,1024]{2,1,0:T(8,128)(2,1)} fusion(bf16[8,128,672]{1,2,0:T(8,128)(2,1)} %all-to-all-done, bf16[672,1024,1]{1,0,2:T(8,128)(2,1)} %reshape.101), kind=kOutput, calls=%fused_computation.75 | convolution fusion | flops 1410334720 | bytes 4849664 | tf_op jit(solution)/shard_map/btk,kh->bth/dot_general | solution.py:109
  92.4 13.3 %all-to-all-start.2 = ((bf16[8,128,1024]{2,1,0:T(8,128)(2,1)}), bf16[8,128,1024]{2,1,0:T(8,128)(2,1)}, u32[]{:S(2)}, u32[]{:S(2)}) async-start(bf16[8,128,1024]{2,1,0:T(8,128)(2,1)} %convolution_convert_fusion.1), calls=%async_computation.2 | async-start | bytes 4194304 | tf_op jit(solution)/shard_map/all_to_all | solution.py:113
  105.7 7.3 %while.28 = (s32[]{:T(128)}, bf16[4,128,2,128]{1,3,2,0:T(8,128)(2,1)S(1)}, f32[4,2,128]{2,1,0:T(2,128)S(1)}, bf16[4,1152,128]{1,2,0:T(8,128)(2,1)S(1)}, bf16[4,1...) while((s32[]{:T(128)}, ...), condition=%wide.region_4.5_spmd.clone, body=%wide.region_1.0_spmd.clone.sunk | while | flops 153829120 | bytes 4571369 | solution.py:88
  113.8 13.2 %all-to-all-done.2 = bf16[8,128,1024]{2,1,0:T(8,128)(2,1)} async-done(((bf16[8,128,1024]{2,1,0:T(8,128)(2,1)}), bf16[8,128,1024]{2,1,0:T(8,128)(2,1)}, u32[]{:S(2)}, u32[]{:S(2)}) %all-to-all-start.2) | async-done | bytes 2097184 | tf_op jit(solution)/shard_map/all_to_all | solution.py:113
  129.2 19.9 %while.29 = (s32[]{:T(128)}, bf16[4,128,2,128]{1,3,2,0:T(8,128)(2,1)}, f32[4,1152,128]{2,1,0:T(8,128)}, f32[4,1152,128]{2,1,0:T(8,128)}, bf16[4,1152,128]{2,1,0:...) while((s32[]{:T(128)}, ...), condition=%wide.region_7.8_spmd.clone, body=%wide.region_6.7_spmd.clone.sunk | while | flops 380469248 | bytes 10175813 | solution.py:124
  149.2 2.2 bitcast_dynamic-update-slice_fusion.1
  155.3 28.4 %all-gather.2.cloned.1.call-done = bf16[1024,1024]{0,1:T(8,128)(2,1)} async-done(((bf16[128,1024]{0,1:T(8,128)(2,1)}), bf16[1024,1024]{0,1:T(8,128)(2,1)}) %all-gather.2.cloned.1.call-update) | async-done | bytes 2097168 | tf_op jit(solution)/shard_map/all_gather | solution.py:119
  186.3 4.4 %fusion.60 = bf16[8,1024,84]{1,2,0:T(8,128)(2,1)} fusion(bf16[1024,8,84]{0,2,1:T(8,128)(2,1)S(1)} %reshape.93, bf16[1024,1024]{0,1:T(8,128)(2,1)} %all-gather.2.cloned.1.call-done), kind=kOutput, calls=%fused_computation.76 | convolution fusion | flops 1410662400 | bytes 4849664 | tf_op jit(solution)/shard_map/th,tqk->qhk/dot_general | solution.py:143
  190.8 9.9 %all-to-all-start.3 = ((bf16[8,1024,84]{1,2,0:T(8,128)(2,1)}), bf16[8,1024,84]{1,2,0:T(8,128)(2,1)S(1)}, u32[]{:S(2)}, u32[]{:S(2)}) async-start(bf16[8,1024,84]{1,2,0:T(8,128)(2,1)} %fusion.60), calls=%async_computation.3 | async-start | bytes 2883584 | tf_op jit(solution)/shard_map/all_to_all | solution.py:149
  200.6 4.3 %collective-permute-start.10 = (bf16[128,1024]{1,0:T(8,128)(2,1)}, bf16[128,1024]{1,0:T(8,128)(2,1)S(1)}, u32[]{:S(2)}, u32[]{:S(2)}) collective-permute-start(bf16[128,1024]{1,0:T(8,128)(2,1)} %get-tuple-element.272), channel_id=1, source_target_pairs={{14,0},{16,2},{18,4},{20,6},{22,8},{24,10},{26,12},{28,14},{30,16}... | collective-permute-start | bytes 786440 | tf_op jit(solution)/shard_map/ppermute | solution.py:19
  204.9 2.6 %collective-permute-start.11 = (bf16[128,1024]{1,0:T(8,128)(2,1)S(1)}, bf16[128,1024]{1,0:T(8,128)(2,1)S(1)}, u32[]{:S(2)}, u32[]{:S(2)}) collective-permute-start(bf16[128,1024]{1,0:T(8,128)(2,1)S(1)} %copy-done.11), channel_id=1, source_target_pairs={{12,0},{14,2},{16,4},{18,6},{20,8},{22,10},{24,12},{26,14},{28,16}... | collective-permute-start | bytes 786440 | tf_op jit(solution)/shard_map/ppermute | solution.py:19
  209.5 2.2 collective-permute-start.13
  211.7 2.3 collective-permute-start.14
  214.0 5.9 %collective-permute-done.10 = bf16[128,1024]{1,0:T(8,128)(2,1)S(1)} collective-permute-done((bf16[128,1024]{1,0:T(8,128)(2,1)}, bf16[128,1024]{1,0:T(8,128)(2,1)S(1)}, u32[]{:S(2)}, u32[]{:S(2)}) %collective-permute-start.10) | collective-permute-done | bytes 262176 | tf_op jit(solution)/shard_map/ppermute | solution.py:19
  221.8 6.7 %collective-permute-start.16 = (bf16[128,1024]{1,0:T(8,128)(2,1)S(1)}, bf16[128,1024]{1,0:T(8,128)(2,1)S(1)}, u32[]{:S(2)}, u32[]{:S(2)}) collective-permute-start(bf16[128,1024]{1,0:T(8,128)(2,1)S(1)} %get-tuple-element.266), channel_id=1, source_target_pairs={{2,0},{4,2},{6,4},{8,6},{10,8},{12,10},{14,12},{16,14},{18,16},{20... | collective-permute-start | bytes 786440 | tf_op jit(solution)/shard_map/ppermute | solution.py:19
  228.6 8.5 %collective-permute-done.12 = bf16[128,1024]{1,0:T(8,128)(2,1)S(1)} collective-permute-done((bf16[128,1024]{1,0:T(8,128)(2,1)S(1)}, bf16[128,1024]{1,0:T(8,128)(2,1)S(1)}, u32[]{:S(2)}, u32[]{:S(2)}) %collective-permute-start.12) | collective-permute-done | bytes 262176 | tf_op jit(solution)/shard_map/ppermute | solution.py:19
  237.0 4.2 %collective-permute-start.9 = (bf16[128,1024]{1,0:T(8,128)(2,1)S(1)}, bf16[128,1024]{1,0:T(8,128)(2,1)S(1)}, u32[]{:S(2)}, u32[]{:S(2)}) collective-permute-start(bf16[128,1024]{1,0:T(8,128)(2,1)S(1)} %get-tuple-element.265), channel_id=1, source_target_pairs={{16,0},{18,2},{20,4},{22,6},{24,8},{26,10},{28,12},{30,14},{32,16}... | collective-permute-start | bytes 786440 | tf_op jit(solution)/shard_map/ppermute | solution.py:19
  243.0 2.8 %collective-permute-done.16 = bf16[128,1024]{1,0:T(8,128)(2,1)S(1)} collective-permute-done((bf16[128,1024]{1,0:T(8,128)(2,1)S(1)}, bf16[128,1024]{1,0:T(8,128)(2,1)S(1)}, u32[]{:S(2)}, u32[]{:S(2)}) %collective-permute-start.16) | collective-permute-done | bytes 262176 | tf_op jit(solution)/shard_map/ppermute | solution.py:19
  245.9 4.7 %collective-permute-done.9 = bf16[128,1024]{1,0:T(8,128)(2,1)S(1)} collective-permute-done((bf16[128,1024]{1,0:T(8,128)(2,1)S(1)}, bf16[128,1024]{1,0:T(8,128)(2,1)S(1)}, u32[]{:S(2)}, u32[]{:S(2)}) %collective-permute-start.9) | collective-permute-done | bytes 262176 | tf_op jit(solution)/shard_map/ppermute | solution.py:19
  (165 shorter events, 71.1 us)
Async XLA Ops:
  9.4 47.0 %all-to-all-start.1 = ((bf16[8,84,1024]{2,1,0:T(8,128)(2,1)}), bf16[8,84,1024]{2,1,0:T(8,128)(2,1)S(1)}, u32[]{:S(2)}, u32[]{:S(2)}) async-start(bf16[8,84,1024]{2,1,0:T(8,128)(2,1)} %broadcast_in_dim.63), calls=%async_computation.1 | async-start | bytes 2883584 | tf_op jit(solution)/shard_map/all_to_all | solution.py:104
  14.8 19.5 %copy-start.12 = (bf16[128,1024]{1,0:T(8,128)(2,1)S(1)}, bf16[128,1024]{1,0:T(8,128)(2,1)}, u32[]{:S(2)}) copy-start(bf16[128,1024]{1,0:T(8,128)(2,1)} %param.9) | copy-start | bytes 786436
  15.1 20.2 %collective-permute-start = (bf16[128,1024]{0,1:T(8,128)(2,1)S(1)}, bf16[128,1024]{0,1:T(8,128)(2,1)}, u32[]{:S(2)}, u32[]{:S(2)}) collective-permute-start(bf16[128,1024]{0,1:T(8,128)(2,1)S(1)} %pad_maximum_fusion), channel_id=1, source_target_pairs={{0,16},{2,18},{4,20},{6,22},{8,24},{10,26},{12,28},{14,30},{16,32}... | collective-permute-start | bytes 786440 | tf_op jit(solution)/shard_map/ppermute | solution.py:19
  18.4 23.2 %collective-permute-start.1 = (bf16[128,1024]{0,1:T(8,128)(2,1)S(1)}, bf16[128,1024]{0,1:T(8,128)(2,1)}, u32[]{:S(2)}, u32[]{:S(2)}) collective-permute-start(bf16[128,1024]{0,1:T(8,128)(2,1)S(1)} %pad_maximum_fusion), channel_id=1, source_target_pairs={{0,14},{2,16},{4,18},{6,20},{8,22},{10,24},{12,26},{14,28},{16,30}... | collective-permute-start | bytes 786440 | tf_op jit(solution)/shard_map/ppermute | solution.py:19
  23.0 22.3 %collective-permute-start.2 = (bf16[128,1024]{0,1:T(8,128)(2,1)S(1)}, bf16[128,1024]{0,1:T(8,128)(2,1)}, u32[]{:S(2)}, u32[]{:S(2)}) collective-permute-start(bf16[128,1024]{0,1:T(8,128)(2,1)S(1)} %pad_maximum_fusion), channel_id=1, source_target_pairs={{0,12},{2,14},{4,16},{6,18},{8,20},{10,22},{12,24},{14,26},{16,28}... | collective-permute-start | bytes 786440 | tf_op jit(solution)/shard_map/ppermute | solution.py:19
  26.8 39.4 %collective-permute-start.3 = (bf16[128,1024]{0,1:T(8,128)(2,1)S(1)}, bf16[128,1024]{0,1:T(8,128)(2,1)}, u32[]{:S(2)}, u32[]{:S(2)}) collective-permute-start(bf16[128,1024]{0,1:T(8,128)(2,1)S(1)} %pad_maximum_fusion), channel_id=1, source_target_pairs={{0,10},{2,12},{4,14},{6,16},{8,18},{10,20},{12,22},{14,24},{16,26}... | collective-permute-start | bytes 786440 | tf_op jit(solution)/shard_map/ppermute | solution.py:19
  30.1 20.1 %collective-permute-start.8 = (bf16[128,2688]{1,0:T(8,128)(2,1)}, bf16[128,2688]{1,0:T(8,128)(2,1)}, u32[]{:S(2)}, u32[]{:S(2)}) collective-permute-start(bf16[128,2688]{1,0:T(8,128)(2,1)} %param.12), channel_id=1, source_target_pairs={{0,1},{1,0},{2,3},{3,2},{4,5},{5,4},{6,7},{7,6},{8,9},{9,8},{10,11... | collective-permute-start | bytes 2064392 | tf_op jit(solution)/shard_map/ppermute | solution.py:94
  35.3 32.6 %collective-permute-start.4 = (bf16[128,1024]{0,1:T(8,128)(2,1)S(1)}, bf16[128,1024]{0,1:T(8,128)(2,1)}, u32[]{:S(2)}, u32[]{:S(2)}) collective-permute-start(bf16[128,1024]{0,1:T(8,128)(2,1)S(1)} %pad_maximum_fusion), channel_id=1, source_target_pairs={{0,8},{2,10},{4,12},{6,14},{8,16},{10,18},{12,20},{14,22},{16,24},... | collective-permute-start | bytes 786440 | tf_op jit(solution)/shard_map/ppermute | solution.py:19
  41.6 28.8 %collective-permute-start.5 = (bf16[128,1024]{0,1:T(8,128)(2,1)S(1)}, bf16[128,1024]{0,1:T(8,128)(2,1)}, u32[]{:S(2)}, u32[]{:S(2)}) collective-permute-start(bf16[128,1024]{0,1:T(8,128)(2,1)S(1)} %pad_maximum_fusion), channel_id=1, source_target_pairs={{0,6},{2,8},{4,10},{6,12},{8,14},{10,16},{12,18},{14,20},{16,22},{... | collective-permute-start | bytes 786440 | tf_op jit(solution)/shard_map/ppermute | solution.py:19
  45.3 32.9 %collective-permute-start.6 = (bf16[128,1024]{0,1:T(8,128)(2,1)S(1)}, bf16[128,1024]{0,1:T(8,128)(2,1)}, u32[]{:S(2)}, u32[]{:S(2)}) collective-permute-start(bf16[128,1024]{0,1:T(8,128)(2,1)S(1)} %pad_maximum_fusion), channel_id=1, source_target_pairs={{0,4},{2,6},{4,8},{6,10},{8,12},{10,14},{12,16},{14,18},{16,20},{1... | collective-permute-start | bytes 786440 | tf_op jit(solution)/shard_map/ppermute | solution.py:19
  50.2 29.9 %collective-permute-start.7 = (bf16[128,1024]{0,1:T(8,128)(2,1)S(1)}, bf16[128,1024]{0,1:T(8,128)(2,1)}, u32[]{:S(2)}, u32[]{:S(2)}) collective-permute-start(bf16[128,1024]{0,1:T(8,128)(2,1)S(1)} %pad_maximum_fusion), channel_id=1, source_target_pairs={{0,2},{2,4},{4,6},{6,8},{8,10},{10,12},{12,14},{14,16},{16,18},{18... | collective-permute-start | bytes 786440 | tf_op jit(solution)/shard_map/ppermute | solution.py:19
  56.4 31.0 %all-to-all-start = ((bf16[8,128,672]{1,2,0:T(8,128)(2,1)}), bf16[8,128,672]{1,2,0:T(8,128)(2,1)}, u32[]{:S(2)}, u32[]{:S(2)}) async-start(bf16[8,128,672]{1,2,0:T(8,128)(2,1)} %fusion.63), calls=%async_computation | async-start | bytes 2752512 | tf_op jit(solution)/shard_map/all_to_all | solution.py:108
  92.4 13.3 %copy-start.20 = (f32[4,2,128]{2,1,0:T(2,128)S(1)}, f32[4,2,128]{2,1,0:T(2,128)}, u32[]{:S(2)}) copy-start(f32[4,2,128]{2,1,0:T(2,128)} %custom-call.3) | copy-start | bytes 12292
  92.4 34.6 %all-to-all-start.2 = ((bf16[8,128,1024]{2,1,0:T(8,128)(2,1)}), bf16[8,128,1024]{2,1,0:T(8,128)(2,1)}, u32[]{:S(2)}, u32[]{:S(2)}) async-start(bf16[8,128,1024]{2,1,0:T(8,128)(2,1)} %convolution_convert_fusion.1), calls=%async_computation.2 | async-start | bytes 4194304 | tf_op jit(solution)/shard_map/all_to_all | solution.py:113
  105.7 78.0 %all-gather.2.cloned.1.call-start = ((), (), s32[]{:S(2)}) async-start(), calls=%async_computation.4 | async-start | bytes 2359296 | tf_op jit(solution)/shard_map/all_gather | solution.py:119
  113.8 15.4 %copy-start.6 = (bf16[4,128,2,128]{1,3,2,0:T(8,128)(2,1)S(1)}, bf16[4,128,2,128]{1,3,2,0:T(8,128)(2,1)}, u32[]{:S(2)}) copy-start(bf16[4,128,2,128]{1,3,2,0:T(8,128)(2,1)} %copy-done.5) | copy-start | bytes 786436
  190.7 14.2 %copy-start.11 = (bf16[128,1024]{1,0:T(8,128)(2,1)S(1)}, bf16[128,1024]{1,0:T(8,128)(2,1)}, u32[]{:S(2)}) copy-start(bf16[128,1024]{1,0:T(8,128)(2,1)} %get-tuple-element.271) | copy-start | bytes 786436
  190.7 16.8 %copy-start.10 = (bf16[128,1024]{1,0:T(8,128)(2,1)S(1)}, bf16[128,1024]{1,0:T(8,128)(2,1)}, u32[]{:S(2)}) copy-start(bf16[128,1024]{1,0:T(8,128)(2,1)} %get-tuple-element.270) | copy-start | bytes 786436
  190.7 18.8 %copy-start.9 = (bf16[128,1024]{1,0:T(8,128)(2,1)S(1)}, bf16[128,1024]{1,0:T(8,128)(2,1)}, u32[]{:S(2)}) copy-start(bf16[128,1024]{1,0:T(8,128)(2,1)} %get-tuple-element.269) | copy-start | bytes 786436
  190.7 20.9 %copy-start.8 = (bf16[128,1024]{1,0:T(8,128)(2,1)S(1)}, bf16[128,1024]{1,0:T(8,128)(2,1)}, u32[]{:S(2)}) copy-start(bf16[128,1024]{1,0:T(8,128)(2,1)} %get-tuple-element.268) | copy-start | bytes 786436
  190.7 29.1 %copy-start.7 = (bf16[128,1024]{1,0:T(8,128)(2,1)S(1)}, bf16[128,1024]{1,0:T(8,128)(2,1)}, u32[]{:S(2)}) copy-start(bf16[128,1024]{1,0:T(8,128)(2,1)} %get-tuple-element.267) | copy-start | bytes 786436
  190.8 62.4 %all-to-all-start.3 = ((bf16[8,1024,84]{1,2,0:T(8,128)(2,1)}), bf16[8,1024,84]{1,2,0:T(8,128)(2,1)S(1)}, u32[]{:S(2)}, u32[]{:S(2)}) async-start(bf16[8,1024,84]{1,2,0:T(8,128)(2,1)} %fusion.60), calls=%async_computation.3 | async-start | bytes 2883584 | tf_op jit(solution)/shard_map/all_to_all | solution.py:149
  200.6 19.3 %collective-permute-start.10 = (bf16[128,1024]{1,0:T(8,128)(2,1)}, bf16[128,1024]{1,0:T(8,128)(2,1)S(1)}, u32[]{:S(2)}, u32[]{:S(2)}) collective-permute-start(bf16[128,1024]{1,0:T(8,128)(2,1)} %get-tuple-element.272), channel_id=1, source_target_pairs={{14,0},{16,2},{18,4},{20,6},{22,8},{24,10},{26,12},{28,14},{30,16}... | collective-permute-start | bytes 786440 | tf_op jit(solution)/shard_map/ppermute | solution.py:19
  204.9 16.9 %collective-permute-start.11 = (bf16[128,1024]{1,0:T(8,128)(2,1)S(1)}, bf16[128,1024]{1,0:T(8,128)(2,1)S(1)}, u32[]{:S(2)}, u32[]{:S(2)}) collective-permute-start(bf16[128,1024]{1,0:T(8,128)(2,1)S(1)} %copy-done.11), channel_id=1, source_target_pairs={{12,0},{14,2},{16,4},{18,6},{20,8},{22,10},{24,12},{26,14},{28,16}... | collective-permute-start | bytes 786440 | tf_op jit(solution)/shard_map/ppermute | solution.py:19
  207.6 29.5 %collective-permute-start.12 = (bf16[128,1024]{1,0:T(8,128)(2,1)S(1)}, bf16[128,1024]{1,0:T(8,128)(2,1)S(1)}, u32[]{:S(2)}, u32[]{:S(2)}) collective-permute-start(bf16[128,1024]{1,0:T(8,128)(2,1)S(1)} %copy-done.10), channel_id=1, source_target_pairs={{10,0},{12,2},{14,4},{16,6},{18,8},{20,10},{22,12},{24,14},{26,16}... | collective-permute-start | bytes 786440 | tf_op jit(solution)/shard_map/ppermute | solution.py:19
  209.5 33.5 %collective-permute-start.13 = (bf16[128,1024]{1,0:T(8,128)(2,1)S(1)}, bf16[128,1024]{1,0:T(8,128)(2,1)}, u32[]{:S(2)}, u32[]{:S(2)}) collective-permute-start(bf16[128,1024]{1,0:T(8,128)(2,1)S(1)} %copy-done.9), channel_id=1, source_target_pairs={{8,0},{10,2},{12,4},{14,6},{16,8},{18,10},{20,12},{22,14},{24,16},... | collective-permute-start | bytes 786440 | tf_op jit(solution)/shard_map/ppermute | solution.py:19
  211.7 31.4 %collective-permute-start.14 = (bf16[128,1024]{1,0:T(8,128)(2,1)S(1)}, bf16[128,1024]{1,0:T(8,128)(2,1)}, u32[]{:S(2)}, u32[]{:S(2)}) collective-permute-start(bf16[128,1024]{1,0:T(8,128)(2,1)S(1)} %copy-done.8), channel_id=1, source_target_pairs={{6,0},{8,2},{10,4},{12,6},{14,8},{16,10},{18,12},{20,14},{22,16},{... | collective-permute-start | bytes 786440 | tf_op jit(solution)/shard_map/ppermute | solution.py:19
  219.9 21.3 %copy-start.15 = (bf16[128,1024]{1,0:T(8,128)(2,1)}, bf16[128,1024]{1,0:T(8,128)(2,1)S(1)}, u32[]{:S(2)}) copy-start(bf16[128,1024]{1,0:T(8,128)(2,1)S(1)} %collective-permute-done.10) | copy-start | bytes 786436
  219.9 23.1 %collective-permute-start.15 = (bf16[128,1024]{1,0:T(8,128)(2,1)S(1)}, bf16[128,1024]{1,0:T(8,128)(2,1)}, u32[]{:S(2)}, u32[]{:S(2)}) collective-permute-start(bf16[128,1024]{1,0:T(8,128)(2,1)S(1)} %copy-done.7), channel_id=1, source_target_pairs={{4,0},{6,2},{8,4},{10,6},{12,8},{14,10},{16,12},{18,14},{20,16},{2... | collective-permute-start | bytes 786440 | tf_op jit(solution)/shard_map/ppermute | solution.py:19
  221.8 19.4 %copy-start.16 = (bf16[128,1024]{1,0:T(8,128)(2,1)}, bf16[128,1024]{1,0:T(8,128)(2,1)S(1)}, u32[]{:S(2)}) copy-start(bf16[128,1024]{1,0:T(8,128)(2,1)S(1)} %collective-permute-done.11) | copy-start | bytes 786436
  221.8 24.0 %collective-permute-start.16 = (bf16[128,1024]{1,0:T(8,128)(2,1)S(1)}, bf16[128,1024]{1,0:T(8,128)(2,1)S(1)}, u32[]{:S(2)}, u32[]{:S(2)}) collective-permute-start(bf16[128,1024]{1,0:T(8,128)(2,1)S(1)} %get-tuple-element.266), channel_id=1, source_target_pairs={{2,0},{4,2},{6,4},{8,6},{10,8},{12,10},{14,12},{16,14},{18,16},{20... | collective-permute-start | bytes 786440 | tf_op jit(solution)/shard_map/ppermute | solution.py:19
  237.0 13.5 %collective-permute-start.9 = (bf16[128,1024]{1,0:T(8,128)(2,1)S(1)}, bf16[128,1024]{1,0:T(8,128)(2,1)S(1)}, u32[]{:S(2)}, u32[]{:S(2)}) collective-permute-start(bf16[128,1024]{1,0:T(8,128)(2,1)S(1)} %get-tuple-element.265), channel_id=1, source_target_pairs={{16,0},{18,2},{20,4},{22,6},{24,8},{26,10},{28,12},{30,14},{32,16}... | collective-permute-start | bytes 786440 | tf_op jit(solution)/shard_map/ppermute | solution.py:19
  (17 other events, 70.7 us)
Sparse Core Ops, SparseCore 0:
  113.9 69.7 all-gather.1
